TPU v7x, 128 devices: a whole 4x4x4 slice. The times are simulated.
128 devices in a mesh: tm: 8 (over z_lo, y), space: 16 (over z_hi, x, core).
Axes of the slice: x: 4, y: 4, z: 4 (z_hi: 2, z_lo: 2; z = z_hi * 2 + z_lo), core: 2. Of those that a mesh axis runs over, the one named last changes fastest.
Arguments:
- spectrum: float32 [2, 512, 128, 1024], P(None, 'tm', 'space'), may hold values from -6 to 6
- diffusivity: float32 [128, 1024], P('space'), may hold values from 0.5 to 2
Outputs:
- solution: float32 [2, 512, 128, 1024], P(None, 'tm', 'space')
All inputs are finite; a program needn't handle non-finite values.
Results may differ from a plain program's by a relative error of at most 0.00016.
Values sent between devices are 32-bit elements; how exact they have to be, the bound alone decides.
No kernel may reach another device: no remote copies, remote signals or barrier semaphores. Data moves between devices by JAX's collectives and lax.ppermute only.
A program may use at most 128 MiB of HBM per device.

v0:
```python
import math

import jax
import jax.numpy as jnp
import numpy as np
from jax import lax
from jax.sharding import PartitionSpec as P

alpha_wrap = 0.25
step_rate = 0.5
flow_speed = 2.0
sweep_weights = [
    1.0 / (1.0 + 0.7 * math.cos(math.pi * (2 * order + 1) / 6.0)) for order in range(3)
]


def extended_2(block, sides, width):
    for axis, dim in sides:
        count = lax.axis_size(axis)
        forward = [(i, i + 1) for i in range(count - 1)]
        backward = [(target, source) for source, target in forward]
        low = lax.ppermute(
            lax.slice_in_dim(block, block.shape[dim] - width, None, axis=dim), axis, forward
        )
        high = lax.ppermute(lax.slice_in_dim(block, 0, width, axis=dim), axis, backward)
        block = jnp.concatenate([low, block, high], axis=dim)
    return block


def in_blocks(x, dim, peers):
    dims = x.shape
    tiles = x.reshape(*dims[:dim], peers, dims[dim] // peers, *dims[dim + 1 :])
    return jnp.moveaxis(tiles, dim, 0)


def cut_rows(length, count):
    hop = length // count
    if hop >= 8:
        hop -= hop % 8
    return [hop * k for k in range(1, count)]


def joined_along(tiles, dim):
    dims = list(tiles.shape[1:])
    dims[dim] *= tiles.shape[0]
    return jnp.moveaxis(tiles, 0, dim).reshape(dims)


def exchange_in_pieces(x, axis, pieces, split_dim, concat_dim):
    tiles = in_blocks(x, split_dim, lax.axis_size(axis))
    cut = max(range(1, max(2, tiles.ndim - 1)), key=lambda d: tiles.shape[d])
    finished = []
    for piece in jnp.split(tiles, cut_rows(tiles.shape[cut], pieces), axis=cut):
        if piece.size:
            finished.append(lax.all_to_all(piece, axis, split_axis=0, concat_axis=0, tiled=True))
    return joined_along(jnp.concatenate(finished, axis=cut), concat_dim)


def reverse_bits(number, bit_count):
    result = number * 0
    for bit_place in range(bit_count):
        result = result + (number >> bit_place & 1) * (1 << bit_count - 1 - bit_place)
    return result


def shift_parts(freq_ids, total_steps):
    phase_angle = freq_ids.astype(jnp.float32) * (2.0 * math.pi / total_steps)
    root_scale = alpha_wrap ** (1.0 / total_steps)
    return (
        step_rate * (1.0 - root_scale * jnp.cos(phase_angle)),
        step_rate * root_scale * jnp.sin(phase_angle),
    )


def divide_diag(residual, diag_real, diag_imag, magnitude):
    real_part = (residual[0] * diag_real + residual[1] * diag_imag) / magnitude
    imag_part = (residual[1] * diag_real - residual[0] * diag_imag) / magnitude
    return jnp.stack([real_part, imag_part])


def apply_operator(current, diffusion, diag_real, diag_imag):
    padded = jnp.pad(current, ((0, 0), (0, 0), (0, 0), (1, 1)))
    center = padded[:, :, 1:-1, 1:-1]
    from_north = padded[:, :, :-2, 1:-1]
    from_south = padded[:, :, 2:, 1:-1]
    from_west = padded[:, :, 1:-1, :-2]
    from_east = padded[:, :, 1:-1, 2:]
    beside_all = from_north + from_south + from_west + from_east
    real_part = (
        diag_real * center[0]
        - diag_imag * center[1]
        - diffusion * beside_all[0]
        - flow_speed * from_north[0]
    )
    imag_part = (
        diag_real * center[1]
        + diag_imag * center[0]
        - diffusion * beside_all[1]
        - flow_speed * from_north[1]
    )
    return jnp.stack([real_part, imag_part])


def complex_scale(values, cos_part, sin_part):
    return jnp.stack(
        [cos_part * values[0] - sin_part * values[1], sin_part * values[0] + cos_part * values[1]]
    )


def on_device(spectrum, diffusivity):
    local_count = spectrum.shape[1]
    row_count = spectrum.shape[2]
    col_count = spectrum.shape[3]
    tm_count = lax.axis_size("tm")
    bit_count = tm_count.bit_length() - 1
    total_steps = local_count * tm_count
    tm_place = lax.axis_index("tm")
    residue = reverse_bits(tm_place, bit_count)
    index_f = jnp.arange(local_count, dtype=jnp.int32)
    freq_ids = index_f * tm_count + residue
    lam_real, lam_imag = shift_parts(freq_ids, total_steps)
    diag_real = lam_real[:, None, None] + 4.0 * diffusivity + flow_speed
    diag_imag = lam_imag[:, None, None] + jnp.zeros_like(diag_real)
    magnitude = diag_real * diag_real + diag_imag * diag_imag
    current = sweep_weights[0] * divide_diag(spectrum, diag_real, diag_imag, magnitude)
    for order in (1, 2):
        extended = extended_2(current, (("space", 2),), 1)
        applied = apply_operator(extended, diffusivity, diag_real, diag_imag)
        current = current + sweep_weights[order] * divide_diag(
            spectrum - applied, diag_real, diag_imag, magnitude
        )
    grid_angle = (index_f[:, None] * index_f[None, :] % local_count).astype(jnp.float32) * (
        2.0 * math.pi / local_count
    )
    cosine = jnp.cos(grid_angle)
    sine = jnp.sin(grid_angle)
    dft_table = jnp.concatenate(
        [jnp.concatenate([cosine, -sine], 1), jnp.concatenate([sine, cosine], 1)], 0
    )
    flat_field = current.reshape(2 * local_count, row_count * col_count)
    spectral = jnp.dot(dft_table, flat_field, precision=lax.Precision.HIGHEST).reshape(
        2, local_count, row_count, col_count
    )
    twist_angle = (residue * index_f % total_steps).astype(jnp.float32) * (
        2.0 * math.pi / total_steps
    )
    twisted = complex_scale(
        spectral, jnp.cos(twist_angle)[:, None, None], jnp.sin(twist_angle)[:, None, None]
    )
    outgoing = twisted.reshape(2, 1, local_count, row_count, col_count)
    arrived = exchange_in_pieces(outgoing, "tm", 2, 4, 1)
    source_residue = np.array([reverse_bits(source, bit_count) for source in range(tm_count)])
    target_place = np.arange(tm_count)
    class_index = target_place[:, None] * source_residue[None, :] % tm_count
    class_angle = jnp.asarray(class_index, dtype=jnp.int32).astype(jnp.float32) * (
        2.0 * math.pi / tm_count
    )
    class_cos = jnp.cos(class_angle)
    class_sin = jnp.sin(class_angle)
    arrived_real = arrived[0].reshape(tm_count, -1)
    arrived_imag = arrived[1].reshape(tm_count, -1)
    high = lax.Precision.HIGHEST
    combined_real = jnp.dot(class_cos, arrived_real, precision=high) - jnp.dot(
        class_sin, arrived_imag, precision=high
    )
    combined_imag = jnp.dot(class_sin, arrived_real, precision=high) + jnp.dot(
        class_cos, arrived_imag, precision=high
    )
    combined = jnp.stack([combined_real, combined_imag]).reshape(arrived.shape)
    returned = lax.all_to_all(combined, "tm", split_axis=1, concat_axis=4, tiled=True)
    temporal = returned.reshape(2, local_count, row_count, col_count)
    step_ids = (tm_place * local_count + index_f).astype(jnp.float32)
    factor = jnp.exp(step_ids * (-math.log(alpha_wrap) / total_steps)) / math.sqrt(total_steps)
    return temporal * factor[None, :, None, None]


def solution(mesh):
    in_specs = (P(None, "tm", "space", None), P("space", None))
    out_specs = P(None, "tm", "space", None)
    return jax.shard_map(
        on_device, mesh=mesh, in_specs=in_specs, out_specs=out_specs, check_vma=False
    )
```

profile of v0, /device:TPU:31, one launch (start us, length us, event | category | flops | bytes accessed | tf_op | source)
XLA Modules:
  0.0 231.5 jit_solution(12765973861173869705)
XLA Ops:
  0.9 4.6 %copy.14 = f32[2,64,8,1024]{3,1,2,0:T(8,128)S(1)} copy(f32[2,64,8,1024]{3,2,1,0:T(8,128)} %param.3) | data formatting | bytes 8388608 | tf_op args[0]
  7.5 6.0 %collective-permute-start = (f32[2,64,1,1024]{3,1,2,0:T(8,128)S(1)}, f32[2,64,1,1024]{3,1,2,0:T(8,128)S(1)}, u32[]{:S(2)}, u32[]{:S(2)}) collective-permute-start(f32[2,64,1,1024]{3,1,2,0:T(8,128)S(1)} %get-tuple-element.26), channel_id=1, source_target_pairs={{0,1},{1,2},{2,3},{3,4},{4,5},{5,6},{6,7},{7,8},{8,9},{9,10},{10,1... | collective-permute-start | bytes 1572872 | tf_op jit(solution)/shard_map/ppermute | solution.py:22
  15.9 3.7 %collective-permute-done = f32[2,64,1,1024]{3,1,2,0:T(8,128)S(1)} collective-permute-done((f32[2,64,1,1024]{3,1,2,0:T(8,128)S(1)}, f32[2,64,1,1024]{3,1,2,0:T(8,128)S(1)}, u32[]{:S(2)}, u32[]{:S(2)}) %collective-permute-start) | collective-permute-done | bytes 524320 | tf_op jit(solution)/shard_map/ppermute | solution.py:22
  19.6 8.0 %collective-permute-done.1 = f32[2,64,1,1024]{3,1,2,0:T(8,128)S(1)} collective-permute-done((f32[2,64,1,1024]{3,1,2,0:T(8,128)S(1)}, f32[2,64,1,1024]{3,1,2,0:T(8,128)S(1)}, u32[]{:S(2)}, u32[]{:S(2)}) %collective-permute-start.1) | collective-permute-done | bytes 524320 | tf_op jit(solution)/shard_map/ppermute | solution.py:25
  27.6 2.4 %select_maximum_fusion.2 = f32[2,64,10,1026]{3,1,2,0:T(8,128)S(1)} fusion(f32[2,64,1,1024]{3,1,2,0:T(8,128)S(1)} %collective-permute-done.1, f32[2,64,8,1024]{3,1,2,0:T(8,128)S(1)} %maximum_multiply_fusion, f32[2,64,1,1024]{3,1,2,0:T(8,128)S(1)} %collective-permute-done), kind=kLoop, calls=%fused_computation.10 | loop fusion | flops 10506240 | bytes 10496000 | tf_op jit(solution)/shard_map/concatenate | solution.py:26
  33.9 2.7 %maximum_subtract_fusion = f32[2,64,8,1024]{3,1,2,0:T(8,128)S(1)} fusion(f32[1,64,8,1024]{3,1,2,0:T(8,128)S(1)} %get-tuple-element.8, f32[1,64,8,1024]{3,1,2,0:T(8,128)S(1)} %get-tuple-element.7, f32[2,64,8,1024]{3,2,1,0:T(8,128)S(1)} %copy-done), kind=kLoop, calls=%fused_computation.28 | loop fusion | flops 2097152 | bytes 12582912 | tf_op jit(solution)/shard_map/sub | solution.py:130
  41.2 2.6 %collective-permute-start.3 = (f32[2,64,1,1024]{3,1,2,0:T(8,128)S(1)}, f32[2,64,1,1024]{3,1,2,0:T(8,128)S(1)}, u32[]{:S(2)}, u32[]{:S(2)}) collective-permute-start(f32[2,64,1,1024]{3,1,2,0:T(8,128)S(1)} %get-tuple-element.23), channel_id=1, source_target_pairs={{1,0},{2,1},{3,2},{4,3},{5,4},{6,5},{7,6},{8,7},{9,8},{10,9},{11,1... | collective-permute-start | bytes 1572872 | tf_op jit(solution)/shard_map/ppermute | solution.py:25
  44.1 3.2 %collective-permute-done.2 = f32[2,64,1,1024]{3,1,2,0:T(8,128)S(1)} collective-permute-done((f32[2,64,1,1024]{3,1,2,0:T(8,128)S(1)}, f32[2,64,1,1024]{3,1,2,0:T(8,128)S(1)}, u32[]{:S(2)}, u32[]{:S(2)}) %collective-permute-start.2) | collective-permute-done | bytes 524320 | tf_op jit(solution)/shard_map/ppermute | solution.py:22
  47.3 8.0 %collective-permute-done.3 = f32[2,64,1,1024]{3,1,2,0:T(8,128)S(1)} collective-permute-done((f32[2,64,1,1024]{3,1,2,0:T(8,128)S(1)}, f32[2,64,1,1024]{3,1,2,0:T(8,128)S(1)}, u32[]{:S(2)}, u32[]{:S(2)}) %collective-permute-start.3) | collective-permute-done | bytes 524320 | tf_op jit(solution)/shard_map/ppermute | solution.py:25
  55.3 2.4 %select_maximum_fusion = f32[2,64,10,1026]{3,1,2,0:T(8,128)S(1)} fusion(f32[2,64,1,1024]{3,1,2,0:T(8,128)S(1)} %collective-permute-done.3, f32[2,64,8,1024]{3,1,2,0:T(8,128)S(1)} %maximum_add_fusion, f32[2,64,1,1024]{3,1,2,0:T(8,128)S(1)} %collective-permute-done.2), kind=kLoop, calls=%fused_computation.8 | loop fusion | flops 10506240 | bytes 10496000 | tf_op jit(solution)/shard_map/concatenate | solution.py:26
  61.6 2.7 %maximum_subtract_fusion.1 = f32[2,64,8,1024]{3,1,2,0:T(8,128)S(1)} fusion(f32[1,64,8,1024]{3,1,2,0:T(8,128)S(1)} %get-tuple-element.6, f32[1,64,8,1024]{3,1,2,0:T(8,128)S(1)} %get-tuple-element.5, f32[2,64,8,1024]{3,2,1,0:T(8,128)S(1)} %copy-done), kind=kLoop, calls=%fused_computation.30 | loop fusion | flops 2097152 | bytes 12582912 | tf_op jit(solution)/shard_map/sub | solution.py:130
  69.4 3.6 %copy.26 = f32[16,8,8,1024]{3,1,2,0:T(8,128)S(1)} copy(f32[16,8,8,1024]{3,2,1,0:T(8,128)S(1)} %bitcast.48) | data formatting | bytes 8388608
  73.0 3.8 %fusion.35 = f32[128,8192]{1,0:T(8,128)S(1)} fusion(f32[128,8192]{1,0:T(8,128)S(1)} %bitcast.47, f32[64,64]{1,0:T(8,128)S(1)} %get-tuple-element.32, f32[64,64]{1,0:T(8,128)S(1)} %get-tuple-element.31, f32[64,64]{1,0:T(8,128)S(1)} %fusion.51), kind=kOutput, calls=%fused_computation.81 | convolution fusion | flops 1610661888 | bytes 8437760 | tf_op jit(solution)/shard_map/dot_general | solution.py:141
  80.0 25.7 %all_to_all.25 = f32[8,2,1,32,8,128]{5,4,3,2,1,0:T(8,128)S(1)} all-to-all(f32[8,2,1,32,8,128]{5,4,3,2,1,0:T(8,128)S(1)} %get-tuple-element.19), channel_id=1, replica_groups=mesh['tm'=8,'space'=16] {'tm'}, dimensions={0} | all-to-all | bytes 4194304 | tf_op jit(solution)/shard_map/all_to_all | solution.py:55
  105.7 26.9 %all_to_all.26 = f32[8,2,1,32,8,128]{5,4,3,2,1,0:T(8,128)S(1)} all-to-all(f32[8,2,1,32,8,128]{5,4,3,2,1,0:T(8,128)S(1)} %get-tuple-element.20), channel_id=1, replica_groups=mesh['tm'=8,'space'=16] {'tm'}, dimensions={0} | all-to-all | bytes 4194304 | tf_op jit(solution)/shard_map/all_to_all | solution.py:55
  133.7 2.9 %fusion.20 = f32[8,65536]{1,0:T(8,128)S(1)} fusion(f32[8,8]{1,0:T(8,128)S(1)} %copy-done.2, f32[1,8,512,128]{3,2,1,0:T(8,128)S(1)} %get-tuple-element.18), kind=kOutput, calls=%fused_computation.46 | convolution fusion | flops 50331648 | bytes 4194560 | tf_op jit(solution)/shard_map/dot_general | solution.py:163
  136.6 2.9 %fusion.18 = f32[8,65536]{1,0:T(8,128)S(1)} fusion(f32[8,8]{1,0:T(8,128)S(1)} %copy-done.3, f32[1,8,512,128]{3,2,1,0:T(8,128)S(1)} %get-tuple-element.18), kind=kOutput, calls=%fused_computation.44 | convolution fusion | flops 50331648 | bytes 4194560 | tf_op jit(solution)/shard_map/dot_general | solution.py:166
  139.5 2.9 %convolution_subtract_fusion = f32[8,65536]{1,0:T(8,128)S(1)} fusion(f32[8,65536]{1,0:T(8,128)S(1)} %fusion.20, f32[8,8]{1,0:T(8,128)S(1)} %copy-done.3, f32[1,8,512,128]{3,2,1,0:T(8,128)S(1)} %get-tuple-element.17), kind=kOutput, calls=%fused_computation.1 | convolution fusion | flops 50855936 | bytes 6291712 | tf_op jit(solution)/shard_map/dot_general | solution.py:163
  142.8 3.1 %convolution_add_fusion = f32[8,65536]{1,0:T(8,128)S(1)} fusion(f32[8,65536]{1,0:T(8,128)S(1)} %fusion.18, f32[8,8]{1,0:T(8,128)S(1)} %copy-done.2, f32[1,8,512,128]{3,2,1,0:T(8,128)S(1)} %get-tuple-element.17), kind=kOutput, calls=%fused_computation | convolution fusion | flops 50855936 | bytes 6291712 | tf_op jit(solution)/shard_map/dot_general | solution.py:166
  148.7 6.0 %all-to-all-start.2 = ((f32[2,8,64,8,128]{4,3,2,0,1:T(8,128)}), f32[2,8,64,8,128]{4,3,2,0,1:T(8,128)}, u32[]{:S(2)}, u32[]{:S(2)}) async-start(f32[2,8,64,8,128]{4,3,2,0,1:T(8,128)} %pad_maximum_fusion.2), calls=%async_computation.2 | async-start | bytes 8388608 | tf_op jit(solution)/shard_map/all_to_all | solution.py:170
  154.7 60.6 %all-to-all-done.2 = f32[2,8,64,8,128]{4,3,2,0,1:T(8,128)} async-done(((f32[2,8,64,8,128]{4,3,2,0,1:T(8,128)}), f32[2,8,64,8,128]{4,3,2,0,1:T(8,128)}, u32[]{:S(2)}, u32[]{:S(2)}) %all-to-all-start.2) | async-done | bytes 4194336 | tf_op jit(solution)/shard_map/all_to_all | solution.py:170
  215.3 6.6 %copy.25 = f32[2,1,64,8,8,128]{5,4,3,2,0,1:T(8,128)} copy(f32[2,1,64,8,8,128]{5,3,2,0,4,1:T(8,128)} %bitcast.5) | data formatting | bytes 8388608 | tf_op jit(solution)/shard_map/all_to_all | solution.py:170
  221.9 4.9 %reshape.139 = f32[2,64,8,1024]{3,2,1,0:T(8,128)} reshape(f32[2,1,64,8,8,128]{5,4,3,2,0,1:T(8,128)} %copy.25) | data formatting | bytes 8388608 | tf_op jit(solution)/shard_map/reshape | solution.py:171
  226.8 4.5 %broadcast_multiply_fusion = f32[2,64,8,1024]{3,2,1,0:T(8,128)} fusion(f32[2,64,8,1024]{3,2,1,0:T(8,128)} %reshape.139, f32[64]{0:T(128)S(1)} %exponential_multiply_fusion), kind=kLoop, calls=%fused_computation.66 | loop fusion | flops 1048576 | bytes 8388864 | tf_op jit(solution)/shard_map/mul | solution.py:174
  (41 shorter events, 30.3 us)
Async XLA Ops:
  7.5 12.1 %collective-permute-start = (f32[2,64,1,1024]{3,1,2,0:T(8,128)S(1)}, f32[2,64,1,1024]{3,1,2,0:T(8,128)S(1)}, u32[]{:S(2)}, u32[]{:S(2)}) collective-permute-start(f32[2,64,1,1024]{3,1,2,0:T(8,128)S(1)} %get-tuple-element.26), channel_id=1, source_target_pairs={{0,1},{1,2},{2,3},{3,4},{4,5},{5,6},{6,7},{7,8},{8,9},{9,10},{10,1... | collective-permute-start | bytes 1572872 | tf_op jit(solution)/shard_map/ppermute | solution.py:22
  13.5 14.1 %collective-permute-start.1 = (f32[2,64,1,1024]{3,1,2,0:T(8,128)S(1)}, f32[2,64,1,1024]{3,1,2,0:T(8,128)S(1)}, u32[]{:S(2)}, u32[]{:S(2)}) collective-permute-start(f32[2,64,1,1024]{3,1,2,0:T(8,128)S(1)} %get-tuple-element.25), channel_id=1, source_target_pairs={{1,0},{2,1},{3,2},{4,3},{5,4},{6,5},{7,6},{8,7},{9,8},{10,9},{11,1... | collective-permute-start | bytes 1572872 | tf_op jit(solution)/shard_map/ppermute | solution.py:25
  30.1 1.6 copy-start.1
  31.7 2.2 copy-start
  39.3 8.0 %collective-permute-start.2 = (f32[2,64,1,1024]{3,1,2,0:T(8,128)S(1)}, f32[2,64,1,1024]{3,1,2,0:T(8,128)S(1)}, u32[]{:S(2)}, u32[]{:S(2)}) collective-permute-start(f32[2,64,1,1024]{3,1,2,0:T(8,128)S(1)} %get-tuple-element.24), channel_id=1, source_target_pairs={{0,1},{1,2},{2,3},{3,4},{4,5},{5,6},{6,7},{7,8},{8,9},{9,10},{10,1... | collective-permute-start | bytes 1572872 | tf_op jit(solution)/shard_map/ppermute | solution.py:22
  41.2 14.1 %collective-permute-start.3 = (f32[2,64,1,1024]{3,1,2,0:T(8,128)S(1)}, f32[2,64,1,1024]{3,1,2,0:T(8,128)S(1)}, u32[]{:S(2)}, u32[]{:S(2)}) collective-permute-start(f32[2,64,1,1024]{3,1,2,0:T(8,128)S(1)} %get-tuple-element.23), channel_id=1, source_target_pairs={{1,0},{2,1},{3,2},{4,3},{5,4},{6,5},{7,6},{8,7},{9,8},{10,9},{11,1... | collective-permute-start | bytes 1572872 | tf_op jit(solution)/shard_map/ppermute | solution.py:25
  133.0 0.7 copy-start.2
  133.7 2.9 %copy-start.3 = (f32[8,8]{1,0:T(8,128)S(1)}, f32[8,8]{1,0:T(8,128)}, u32[]{:S(2)}) copy-start(f32[8,8]{1,0:T(8,128)} %constant.85) | copy-start | bytes 772
  148.7 66.6 %all-to-all-start.2 = ((f32[2,8,64,8,128]{4,3,2,0,1:T(8,128)}), f32[2,8,64,8,128]{4,3,2,0,1:T(8,128)}, u32[]{:S(2)}, u32[]{:S(2)}) async-start(f32[2,8,64,8,128]{4,3,2,0,1:T(8,128)} %pad_maximum_fusion.2), calls=%async_computation.2 | async-start | bytes 8388608 | tf_op jit(solution)/shard_map/all_to_all | solution.py:170
where the time goes:
time: 236 us; the launch traced here: 231 us
  waiting for transfers between devices  83.4 us (35%)
  blocking collectives  52.6 us (22%)
  other arithmetic  34.6 us (15%)
  local copies, waits for them, and re-layouts  25.8 us (11%)
  starting transfers between devices  19 us (8%)
  matrix products  15.6 us (7%)
    all_to_all x1, waiting for transfers between devices, on_device(): lax.all_to_all(combined, 'tm', split_axis=1, concat_axis=4, tiled=True)  60.6 us
    all_to_all x2, blocking collectives, exchange_in_pieces(): lax.all_to_all(piece, axis, split_axis=0, concat_axis=0, tiled=True)  52.6 us
    ppermute x2, waiting for transfers between devices, extended_2(): lax.ppermute(lax.slice_in_dim(block, 0, width, axis=dim), axis, backward)  16 us
    unnamed x14, local copies, waits for them, and re-layouts  10 us
    ppermute x2, starting transfers between devices, extended_2(): lax.ppermute(lax.slice_in_dim(block, block.shape[dim] - width, None, axis...  7.9 us
    ppermute x2, waiting for transfers between devices, extended_2(): lax.ppermute(lax.slice_in_dim(block, block.shape[dim] - width, None, axis...  6.82 us
    all_to_all x1, local copies, waits for them, and re-layouts, on_device(): lax.all_to_all(combined, 'tm', split_axis=1, concat_axis=4, tiled=True)  6.63 us
    all_to_all x1, starting transfers between devices, on_device(): lax.all_to_all(combined, 'tm', split_axis=1, concat_axis=4, tiled=True)  6.03 us
  transfers between devices with their start and end apart: 5, of which 5 were waited for; matrix products, arithmetic and copies ran while one was open for 0% of the time, Pallas kernels for 0%

commit v1 on v0

v1 whole, which is shorter than its diff:
```python
import math

import jax
import jax.numpy as jnp
import numpy as np
from jax import lax
from jax.sharding import PartitionSpec as P

alpha_wrap = 0.25
step_rate = 0.5
flow_speed = 2.0
sweep_weights = [
    1.0 / (1.0 + 0.7 * math.cos(math.pi * (2 * order + 1) / 6.0)) for order in range(3)
]
Q_CHUNKS = 4
HALO = 2


def reverse_bits(number, bit_count):
    result = number * 0
    for bit_place in range(bit_count):
        result = result + (number >> bit_place & 1) * (1 << bit_count - 1 - bit_place)
    return result


def shift_parts(freq_ids, total_steps):
    phase_angle = freq_ids.astype(jnp.float32) * (2.0 * math.pi / total_steps)
    root_scale = alpha_wrap ** (1.0 / total_steps)
    return (
        step_rate * (1.0 - root_scale * jnp.cos(phase_angle)),
        step_rate * root_scale * jnp.sin(phase_angle),
    )


def halo_rows(block, axis, dim, width):
    count = lax.axis_size(axis)
    forward = [(i, i + 1) for i in range(count - 1)]
    backward = [(i + 1, i) for i in range(count - 1)]
    size = block.shape[dim]
    top = lax.ppermute(lax.slice_in_dim(block, size - width, size, axis=dim), axis, forward)
    bottom = lax.ppermute(lax.slice_in_dim(block, 0, width, axis=dim), axis, backward)
    return jnp.concatenate([top, block, bottom], axis=dim)


def divide_diag(re, im, diag_real, diag_imag, inv_mag):
    return (re * diag_real + im * diag_imag) * inv_mag, (im * diag_real - re * diag_imag) * inv_mag


def shift_cols(v, direction):
    zeros = jnp.zeros_like(v[..., :1])
    if direction > 0:
        return jnp.concatenate([zeros, v[..., :-1]], axis=-1)
    return jnp.concatenate([v[..., 1:], zeros], axis=-1)


def apply_operator(v_re, v_im, lo, hi, diffusion, diag_real, diag_imag):
    def parts(v):
        center = v[:, 1:-1]
        north = v[:, :-2]
        south = v[:, 2:]
        beside = north + south + shift_cols(center, 1) + shift_cols(center, -1)
        return center, north, beside

    c_re, n_re, b_re = parts(v_re)
    c_im, n_im, b_im = parts(v_im)
    d = diffusion[lo:hi]
    real_part = diag_real * c_re - diag_imag * c_im - d * b_re - flow_speed * n_re
    imag_part = diag_real * c_im + diag_imag * c_re - d * b_im - flow_speed * n_im
    return real_part, imag_part


def on_device(spectrum, diffusivity):
    local_count = spectrum.shape[1]
    row_count = spectrum.shape[2]
    col_count = spectrum.shape[3]
    tm_count = lax.axis_size("tm")
    space_count = lax.axis_size("space")
    bit_count = tm_count.bit_length() - 1
    total_steps = local_count * tm_count
    tm_place = lax.axis_index("tm")
    space_place = lax.axis_index("space")
    residue = reverse_bits(tm_place, bit_count)
    index_f = jnp.arange(local_count, dtype=jnp.int32)
    freq_ids = index_f * tm_count + residue
    lam_real, lam_imag = shift_parts(freq_ids, total_steps)

    rhs = halo_rows(spectrum, "space", 2, HALO)
    diff = halo_rows(diffusivity, "space", 0, HALO)
    ext_rows = row_count + 2 * HALO
    global_row = space_place * row_count - HALO + jnp.arange(ext_rows, dtype=jnp.int32)
    inside = ((global_row >= 0) & (global_row < space_count * row_count))[None, :, None]

    diag_real = lam_real[:, None, None] + 4.0 * diff + flow_speed
    diag_imag = jnp.broadcast_to(lam_imag[:, None, None], diag_real.shape)
    inv_mag = 1.0 / (diag_real * diag_real + diag_imag * diag_imag)

    r_re, r_im = rhs[0], rhs[1]
    c_re, c_im = divide_diag(r_re, r_im, diag_real, diag_imag, inv_mag)
    c_re = sweep_weights[0] * c_re
    c_im = sweep_weights[0] * c_im
    lo, hi = 0, ext_rows
    for order in (1, 2):
        lo, hi = lo + 1, hi - 1
        a_re, a_im = apply_operator(c_re, c_im, lo, hi, diff, diag_real[:, lo:hi], diag_imag[:, lo:hi])
        u_re, u_im = divide_diag(
            r_re[:, lo:hi] - a_re, r_im[:, lo:hi] - a_im,
            diag_real[:, lo:hi], diag_imag[:, lo:hi], inv_mag[:, lo:hi],
        )
        c_re = c_re[:, 1:-1] + sweep_weights[order] * u_re
        c_im = c_im[:, 1:-1] + sweep_weights[order] * u_im
        if order == 1:
            keep = inside[:, lo:hi]
            c_re = jnp.where(keep, c_re, 0.0)
            c_im = jnp.where(keep, c_im, 0.0)
    flat_field = jnp.concatenate([c_re, c_im], 0).reshape(2 * local_count, row_count * col_count)

    grid_angle = (index_f[:, None] * index_f[None, :] % local_count).astype(jnp.float32) * (
        2.0 * math.pi / local_count
    )
    cosine = jnp.cos(grid_angle)
    sine = jnp.sin(grid_angle)
    twist_angle = (residue * index_f % total_steps).astype(jnp.float32) * (
        2.0 * math.pi / total_steps
    )
    twist_cos = jnp.cos(twist_angle)
    twist_sin = jnp.sin(twist_angle)

    source_residue = np.array([reverse_bits(source, bit_count) for source in range(tm_count)])
    class_index = np.arange(tm_count)[:, None] * source_residue[None, :] % tm_count
    class_angle = class_index.astype(np.float64) * (2.0 * math.pi / tm_count)
    class_cos = jnp.asarray(np.cos(class_angle), jnp.float32)
    class_sin = jnp.asarray(np.sin(class_angle), jnp.float32)
    high = lax.Precision.HIGHEST
    step_rate_log = -math.log(alpha_wrap) / total_steps
    col_block = col_count // tm_count

    chunk = local_count // Q_CHUNKS
    pieces = []
    for c in range(Q_CHUNKS):
        qs = slice(c * chunk, (c + 1) * chunk)
        table = jnp.concatenate(
            [jnp.concatenate([cosine[qs], -sine[qs]], 1), jnp.concatenate([sine[qs], cosine[qs]], 1)], 0
        )
        spectral = jnp.dot(table, flat_field, precision=high).reshape(2, chunk, row_count, col_count)
        tc = twist_cos[qs][:, None, None]
        ts = twist_sin[qs][:, None, None]
        tw_re = tc * spectral[0] - ts * spectral[1]
        tw_im = ts * spectral[0] + tc * spectral[1]
        outgoing = jnp.stack([tw_re, tw_im]).reshape(2, chunk, row_count, tm_count, col_block)
        outgoing = jnp.moveaxis(outgoing, 3, 0)
        arrived = lax.all_to_all(outgoing, "tm", 0, 0, tiled=True)
        a_re = arrived[:, 0].reshape(tm_count, -1)
        a_im = arrived[:, 1].reshape(tm_count, -1)
        comb_re = jnp.dot(class_cos, a_re, precision=high) - jnp.dot(class_sin, a_im, precision=high)
        comb_im = jnp.dot(class_sin, a_re, precision=high) + jnp.dot(class_cos, a_im, precision=high)
        step_ids = (
            jnp.arange(tm_count, dtype=jnp.int32)[:, None] * local_count + c * chunk
            + jnp.arange(chunk, dtype=jnp.int32)[None, :]
        ).astype(jnp.float32)
        factor = (jnp.exp(step_ids * step_rate_log) / math.sqrt(total_steps))[:, :, None, None]
        comb_re = comb_re.reshape(tm_count, chunk, row_count, col_block) * factor
        comb_im = comb_im.reshape(tm_count, chunk, row_count, col_block) * factor
        combined = jnp.stack([comb_re, comb_im], 1)
        returned = lax.all_to_all(combined, "tm", 0, 0, tiled=True)
        pieces.append(jnp.moveaxis(returned, 0, 3).reshape(2, chunk, row_count, col_count))
    return jnp.concatenate(pieces, axis=1)


def solution(mesh):
    in_specs = (P(None, "tm", "space", None), P("space", None))
    out_specs = P(None, "tm", "space", None)
    return jax.shard_map(
        on_device, mesh=mesh, in_specs=in_specs, out_specs=out_specs, check_vma=False
    )
```

time: 236 us -> 285 us (1.21)
  the two profiles are of different devices: /device:TPU:31 before, /device:TPU:4 now
where the time goes in v1:
time: 285 us; the launch traced here: 280 us
  other arithmetic  80.1 us (28%)
  waiting for transfers between devices  80 us (28%)
  local copies, waits for them, and re-layouts  46.2 us (16%)
  starting transfers between devices  43.9 us (15%)
  matrix products  28.5 us (10%)
    all_to_all x4, waiting for transfers between devices, on_device(): returned = lax.all_to_all(combined, 'tm', 0, 0, tiled=True)  46.5 us
    all_to_all x4, waiting for transfers between devices, on_device(): arrived = lax.all_to_all(outgoing, 'tm', 0, 0, tiled=True)  32.9 us
    add x1, other arithmetic, on_device(): c_re = c_re[:, 1:-1] + sweep_weights[order] * u_re  20.2 us
    slice x4, local copies, waits for them, and re-layouts, shift_cols(): return jnp.concatenate([zeros, v[..., :-1]], axis=-1)  17.3 us
    all_to_all x4, starting transfers between devices, on_device(): arrived = lax.all_to_all(outgoing, 'tm', 0, 0, tiled=True)  16.9 us
    all_to_all x4, starting transfers between devices, on_device(): returned = lax.all_to_all(combined, 'tm', 0, 0, tiled=True)  15.8 us
    select_n x1, other arithmetic, on_device(): c_im = jnp.where(keep, c_im, 0.0)  14.9 us
    dot_general x4, matrix products, on_device(): jnp.dot(table, flat_field, precision=high)  10.9 us
  transfers between devices with their start and end apart: 12, of which 9 were waited for; matrix products, arithmetic and copies ran while one was open for 20% of the time, Pallas kernels for 0%

profile of v1, /device:TPU:4, one launch (start us, length us, event | category | flops | bytes accessed | tf_op | source)
XLA Modules:
  0.0 279.9 jit_solution(12800259886718756636)
XLA Ops:
  0.0 4.6 %fusion.122 = (f32[2,64,2,1024]{3,2,1,0:T(2,128)S(1)}, f32[2,64,2,1024]{3,2,1,0:T(2,128)S(1)}) fusion(f32[2,64,8,1024]{3,2,1,0:T(8,128)} %param.4), kind=kLoop, calls=%fused_computation.212 | loop fusion | bytes 4194304 | tf_op jit(solution)/shard_map/slice | solution.py:40
  7.2 3.6 %collective-permute-start.1 = (f32[2,64,2,1024]{3,1,2,0:T(8,128)S(1)}, f32[2,64,2,1024]{3,1,2,0:T(8,128)}, u32[]{:S(2)}, u32[]{:S(2)}) collective-permute-start(f32[2,64,2,1024]{3,1,2,0:T(8,128)S(1)} %copy.66), channel_id=1, source_target_pairs={{1,0},{2,1},{3,2},{4,3},{5,4},{6,5},{7,6},{8,7},{9,8},{10,9},{11,1... | collective-permute-start | bytes 3145736 | tf_op jit(solution)/shard_map/ppermute | solution.py:41
  28.6 4.2 %slice_bitcast_fusion = (f32[64,12,1024]{2,1,0:T(8,128)}, f32[64,12,1024]{2,1,0:T(8,128)}) fusion(f32[2,64,12,1024]{3,2,1,0:T(8,128)S(1)} %pad_maximum_fusion), kind=kLoop, calls=%fused_computation.23 | loop fusion | bytes 12582912 | tf_op jit(solution)/shard_map/squeeze | solution.py:97
  32.8 5.2 %multiply_multiply_fusion.1 = (f32[64,12,1024]{2,1,0:T(8,128)S(1)}, f32[64,12,1024]{2,1,0:T(8,128)S(1)}, f32[64,12,1024]{2,1,0:T(8,128)S(1)}, f32[64,12,1024]{2,1,0:T(8,128)}) fusion(f32[64]{0:T(128)S(1)} %copy-done.31, f32[12,1024]{1,0:T(8,128)S(1)} %get-tuple-element.52, f32[64]{0:T(128)S(1)} %copy-done.41, f32[64]{0:T(128)S(1)} %fusion.113, ...), kind=kLoop, calls=%fused_computation.30 | loop fusion | flops 11796480 | bytes 18924288 | tf_op jit(solution)/shard_map/mul | solution.py:99
  37.9 5.4 %fusion.121 = (f32[64,10,1023]{2,1,0:T(8,128)}, f32[64,10,1023]{2,1,0:T(8,128)}) fusion(f32[64,12,1024]{2,1,0:T(8,128)S(1)} %get-tuple-element.11), kind=kLoop, calls=%fused_computation.211 | loop fusion | bytes 10475520 | tf_op jit(solution)/shard_map/slice | solution.py:52
  43.4 5.4 %fusion.120 = (f32[64,10,1023]{2,1,0:T(8,128)}, f32[64,10,1023]{2,1,0:T(8,128)}) fusion(f32[64,12,1024]{2,1,0:T(8,128)S(1)} %get-tuple-element.12), kind=kLoop, calls=%fused_computation.210 | loop fusion | bytes 10475520 | tf_op jit(solution)/shard_map/slice | solution.py:52
  48.8 14.9 %add_select_fusion = (f32[64,10,1024]{2,1,0:T(8,128)S(1)}, f32[64,10,1024]{2,1,0:T(8,128)}, f32[64,10,1024]{2,1,0:T(8,128)}) fusion(f32[64,12,1024]{2,1,0:T(8,128)S(1)} %get-tuple-element.49, f32[64,12,1024]{2,1,0:T(8,128)S(1)} %get-tuple-element.12, f32[64,12,1024]{2,1,0:T(8,128)S(1)} %copy-done.3, f32[64]{0:T(128)} %get-tuple-element.83, ...), kind=kLoop, calls=%fused_computation.27 | loop fusion | flops 18350080 | bytes 44595464 | tf_op jit(solution)/shard_map/jit(_where)/select_n | solution.py:114
  63.7 7.3 %add_select_fusion.1 = f32[64,10,1024]{2,1,0:T(8,128)S(1)} fusion(f32[64,10,1024]{2,1,0:T(8,128)} %get-tuple-element.10, f32[64,10,1024]{2,1,0:T(8,128)} %get-tuple-element.9, f32[64,12,1024]{2,1,0:T(8,128)S(1)} %get-tuple-element.49, f32[64,12,1024]{2,1,0:T(8,128)S(1)} %get-tuple-element.11, f32[64,12,1024]{2,1,0:T(8,128)S(1)} %copy-done.3, ...), kind=kLoop, calls=%fused_computation.28 | loop fusion | flops 3932160 | bytes 15728906 | tf_op jit(solution)/shard_map/jit(_where)/select_n | solution.py:113
  77.5 20.2 %multiply_add_fusion.1 = (f32[64,8,1024]{2,1,0:T(8,128)}, f32[64,8,1024]{2,1,0:T(8,128)S(1)}, f32[64,8,1024]{2,1,0:T(8,128)}) fusion(f32[64,12,1024]{2,1,0:T(8,128)} %copy-done.2, f32[64,10,1024]{2,1,0:T(8,128)} %copy-done.5, f32[64,12,1024]{2,1,0:T(8,128)} %get-tuple-element.50, f32[64]{0:T(128)} %get-tuple-element.83, ...), kind=kLoop, calls=%fused_computation.48 | loop fusion | flops 14680064 | bytes 35676416 | tf_op jit(solution)/shard_map/add | solution.py:109
  97.7 7.5 %multiply_add_fusion = f32[64,8,1024]{2,1,0:T(8,128)S(1)} fusion(f32[64,8,1024]{2,1,0:T(8,128)} %get-tuple-element.7, f32[64,8,1024]{2,1,0:T(8,128)S(1)} %get-tuple-element.6, f32[64,12,1024]{2,1,0:T(8,128)} %copy-done.2, f32[64,10,1024]{2,1,0:T(8,128)} %copy-done.4, f32[64,12,1024]{2,1,0:T(8,128)} %get-tuple-element.50, f32[64]{0:T(128)S(1)} %copy-done.32), kind=kLoop, calls=%fused_computation.47 | loop fusion | flops 3145728 | bytes 12583168 | tf_op jit(solution)/shard_map/add | solution.py:110
  112.9 6.0 %all-to-all-start = ((f32[8,2,16,8,128]{4,3,2,1,0:T(8,128)}), f32[8,2,16,8,128]{4,3,2,1,0:T(8,128)S(1)}, u32[]{:S(2)}, u32[]{:S(2)}) async-start(f32[8,2,16,8,128]{4,3,2,1,0:T(8,128)} %maximum_bitcast_fusion), calls=%async_computation | async-start | bytes 2097152 | tf_op jit(solution)/shard_map/all_to_all | solution.py:151
  119.0 4.1 %fusion.78 = f32[32,8192]{1,0:T(8,128)S(1)} fusion(f32[128,8192]{1,0:T(8,128)} %bitcast.189, f32[16,64]{1,0:T(8,128)S(1)} %copy-done.23, f32[16,64]{1,0:T(8,128)S(1)} %copy-done.22, f32[16,64]{1,0:T(8,128)S(1)} %copy-done.21), kind=kOutput, calls=%fused_computation.152 | convolution fusion | flops 402665472 | bytes 5255168 | tf_op jit(solution)/shard_map/dot_general | solution.py:144
  131.5 4.2 %all-to-all-done = f32[8,2,16,8,128]{4,3,2,1,0:T(8,128)S(1)} async-done(((f32[8,2,16,8,128]{4,3,2,1,0:T(8,128)}), f32[8,2,16,8,128]{4,3,2,1,0:T(8,128)S(1)}, u32[]{:S(2)}, u32[]{:S(2)}) %all-to-all-start) | async-done | bytes 1048608 | tf_op jit(solution)/shard_map/all_to_all | solution.py:151
  146.1 9.4 %all-to-all-done.2 = f32[8,2,16,8,128]{4,3,2,1,0:T(8,128)S(1)} async-done(((f32[8,2,16,8,128]{4,3,2,1,0:T(8,128)}), f32[8,2,16,8,128]{4,3,2,1,0:T(8,128)S(1)}, u32[]{:S(2)}, u32[]{:S(2)}) %all-to-all-start.2) | async-done | bytes 1048608 | tf_op jit(solution)/shard_map/all_to_all | solution.py:151
  155.5 3.8 %all-to-all-start.4 = ((f32[8,2,16,8,128]{4,3,2,1,0:T(8,128)}), f32[8,2,16,8,128]{4,3,2,1,0:T(8,128)S(1)}, u32[]{:S(2)}, u32[]{:S(2)}) async-start(f32[8,2,16,8,128]{4,3,2,1,0:T(8,128)} %maximum_bitcast_fusion.2), calls=%async_computation.4 | async-start | bytes 2097152 | tf_op jit(solution)/shard_map/all_to_all | solution.py:151
  165.0 10.1 %all-to-all-done.4 = f32[8,2,16,8,128]{4,3,2,1,0:T(8,128)S(1)} async-done(((f32[8,2,16,8,128]{4,3,2,1,0:T(8,128)}), f32[8,2,16,8,128]{4,3,2,1,0:T(8,128)S(1)}, u32[]{:S(2)}, u32[]{:S(2)}) %all-to-all-start.4) | async-done | bytes 1048608 | tf_op jit(solution)/shard_map/all_to_all | solution.py:151
  186.3 9.2 %all-to-all-done.6 = f32[8,2,16,8,128]{4,3,2,1,0:T(8,128)S(1)} async-done(((f32[8,2,16,8,128]{4,3,2,1,0:T(8,128)}), f32[8,2,16,8,128]{4,3,2,1,0:T(8,128)S(1)}, u32[]{:S(2)}, u32[]{:S(2)}) %all-to-all-start.6) | async-done | bytes 1048608 | tf_op jit(solution)/shard_map/all_to_all | solution.py:151
  204.6 11.2 %all-to-all-done.1 = f32[8,2,16,8,128]{4,3,2,1,0:T(8,128)S(1)} async-done(((f32[8,2,16,8,128]{4,3,2,1,0:T(8,128)}), f32[8,2,16,8,128]{4,3,2,1,0:T(8,128)S(1)}, u32[]{:S(2)}, u32[]{:S(2)}) %all-to-all-start.1) | async-done | bytes 1048608 | tf_op jit(solution)/shard_map/all_to_all | solution.py:164
  215.8 4.5 %all-to-all-start.3 = ((f32[8,2,16,8,128]{4,3,2,1,0:T(8,128)}), f32[8,2,16,8,128]{4,3,2,1,0:T(8,128)}, u32[]{:S(2)}, u32[]{:S(2)}) async-start(f32[8,2,16,8,128]{4,3,2,1,0:T(8,128)} %pad_maximum_fusion.4), calls=%async_computation.3 | async-start | bytes 2097152 | tf_op jit(solution)/shard_map/all_to_all | solution.py:164
  224.6 11.6 %all-to-all-done.3 = f32[8,2,16,8,128]{4,3,2,1,0:T(8,128)} async-done(((f32[8,2,16,8,128]{4,3,2,1,0:T(8,128)}), f32[8,2,16,8,128]{4,3,2,1,0:T(8,128)}, u32[]{:S(2)}, u32[]{:S(2)}) %all-to-all-start.3) | async-done | bytes 1048608 | tf_op jit(solution)/shard_map/all_to_all | solution.py:164
  236.2 4.2 %all-to-all-start.5 = ((f32[8,2,16,8,128]{4,3,2,1,0:T(8,128)}), f32[8,2,16,8,128]{4,3,2,1,0:T(8,128)}, u32[]{:S(2)}, u32[]{:S(2)}) async-start(f32[8,2,16,8,128]{4,3,2,1,0:T(8,128)} %pad_maximum_fusion.5), calls=%async_computation.5 | async-start | bytes 2097152 | tf_op jit(solution)/shard_map/all_to_all | solution.py:164
  243.5 12.8 %all-to-all-done.5 = f32[8,2,16,8,128]{4,3,2,1,0:T(8,128)} async-done(((f32[8,2,16,8,128]{4,3,2,1,0:T(8,128)}), f32[8,2,16,8,128]{4,3,2,1,0:T(8,128)}, u32[]{:S(2)}, u32[]{:S(2)}) %all-to-all-start.5) | async-done | bytes 1048608 | tf_op jit(solution)/shard_map/all_to_all | solution.py:164
  264.8 11.0 %all-to-all-done.7 = f32[8,2,16,8,128]{4,3,2,1,0:T(8,128)S(1)} async-done(((f32[8,2,16,8,128]{4,3,2,1,0:T(8,128)}), f32[8,2,16,8,128]{4,3,2,1,0:T(8,128)S(1)}, u32[]{:S(2)}, u32[]{:S(2)}) %all-to-all-start.7) | async-done | bytes 1048608 | tf_op jit(solution)/shard_map/all_to_all | solution.py:164
  275.9 3.8 %pad_maximum_fusion.2 = f32[2,64,8,1024]{3,2,1,0:T(8,128)} fusion(f32[2,16,8,1024]{3,2,1,0:T(8,128)S(1)} %copy_bitcast_fusion, f32[2,16,8,1024]{3,2,1,0:T(8,128)} %copy_bitcast_fusion.1, f32[2,16,8,1024]{3,2,1,0:T(8,128)S(1)} %copy_bitcast_fusion.2, f32[2,16,8,1024]{3,2,1,0:T(8,128)S(1)} %copy-done.10), kind=kLoop, calls=%fused_computation.26 | loop fusion | flops 3145728 | bytes 8388608 | tf_op jit(solution)/shard_map/concatenate | solution.py:166
  (180 shorter events, 94.3 us)
Async XLA Ops:
  0.0 10.8 %copy-start.15 = (f32[8,1024]{1,0:T(8,128)S(1)}, f32[8,1024]{1,0:T(8,128)}, u32[]{:S(2)}) copy-start(f32[8,1024]{1,0:T(8,128)} %param.5) | copy-start | bytes 98308
  4.9 18.9 %collective-permute-start = (f32[2,64,2,1024]{3,1,2,0:T(8,128)S(1)}, f32[2,64,2,1024]{3,1,2,0:T(8,128)S(1)}, u32[]{:S(2)}, u32[]{:S(2)}) collective-permute-start(f32[2,64,2,1024]{3,1,2,0:T(8,128)S(1)} %copy.65), channel_id=1, source_target_pairs={{0,1},{1,2},{2,3},{3,4},{4,5},{5,6},{6,7},{7,8},{8,9},{9,10},{10,1... | collective-permute-start | bytes 3145736 | tf_op jit(solution)/shard_map/ppermute | solution.py:40
  7.2 17.5 %collective-permute-start.1 = (f32[2,64,2,1024]{3,1,2,0:T(8,128)S(1)}, f32[2,64,2,1024]{3,1,2,0:T(8,128)}, u32[]{:S(2)}, u32[]{:S(2)}) collective-permute-start(f32[2,64,2,1024]{3,1,2,0:T(8,128)S(1)} %copy.66), channel_id=1, source_target_pairs={{1,0},{2,1},{3,2},{4,3},{5,4},{6,5},{7,6},{8,7},{9,8},{10,9},{11,1... | collective-permute-start | bytes 3145736 | tf_op jit(solution)/shard_map/ppermute | solution.py:41
  10.9 11.8 %collective-permute-start.2 = (f32[2,1024]{1,0:T(2,128)S(1)}, f32[2,1024]{1,0:T(2,128)S(1)}, u32[]{:S(2)}, u32[]{:S(2)}) collective-permute-start(f32[2,1024]{1,0:T(2,128)S(1)} %get-tuple-element.65), channel_id=1, source_target_pairs={{0,1},{1,2},{2,3},{3,4},{4,5},{5,6},{6,7},{7,8},{8,9},{9,10},{10,1... | collective-permute-start | bytes 24584 | tf_op jit(solution)/shard_map/ppermute | solution.py:40
  12.8 10.4 %collective-permute-start.3 = (f32[2,1024]{1,0:T(2,128)S(1)}, f32[2,1024]{1,0:T(2,128)S(1)}, u32[]{:S(2)}, u32[]{:S(2)}) collective-permute-start(f32[2,1024]{1,0:T(2,128)S(1)} %get-tuple-element.66), channel_id=1, source_target_pairs={{1,0},{2,1},{3,2},{4,3},{5,4},{6,5},{7,6},{8,7},{9,8},{10,9},{11,1... | collective-permute-start | bytes 24584 | tf_op jit(solution)/shard_map/ppermute | solution.py:41
  17.3 9.5 %copy-start.6 = (f32[2,64,8,1024]{3,2,1,0:T(8,128)S(1)}, f32[2,64,8,1024]{3,2,1,0:T(8,128)}, u32[]{:S(2)}) copy-start(f32[2,64,8,1024]{3,2,1,0:T(8,128)} %param.4) | copy-start | bytes 12582916
  37.9 25.7 %copy-start.2 = (f32[64,12,1024]{2,1,0:T(8,128)}, f32[64,12,1024]{2,1,0:T(8,128)S(1)}, u32[]{:S(2)}) copy-start(f32[64,12,1024]{2,1,0:T(8,128)S(1)} %get-tuple-element.49) | copy-start | bytes 9437188
  63.7 10.7 %copy-start.4 = (f32[64,10,1024]{2,1,0:T(8,128)}, f32[64,10,1024]{2,1,0:T(8,128)S(1)}, u32[]{:S(2)}) copy-start(f32[64,10,1024]{2,1,0:T(8,128)S(1)} %get-tuple-element.8) | copy-start | bytes 7864324
  77.5 20.2 %copy-start.32 = (f32[64]{0:T(128)S(1)}, f32[64]{0:T(128)}, u32[]{:S(2)}) copy-start(f32[64]{0:T(128)} %get-tuple-element.83) | copy-start | bytes 772
  111.3 7.6 %copy-start.21 = (f32[16,64]{1,0:T(8,128)S(1)}, f32[16,64]{1,0:T(8,128)}, u32[]{:S(2)}) copy-start(f32[16,64]{1,0:T(8,128)} %get-tuple-element.54) | copy-start | bytes 12292
  111.3 7.6 %copy-start.22 = (f32[16,64]{1,0:T(8,128)S(1)}, f32[16,64]{1,0:T(8,128)}, u32[]{:S(2)}) copy-start(f32[16,64]{1,0:T(8,128)} %get-tuple-element.59) | copy-start | bytes 12292
  111.3 7.6 %copy-start.23 = (f32[16,64]{1,0:T(8,128)S(1)}, f32[16,64]{1,0:T(8,128)}, u32[]{:S(2)}) copy-start(f32[16,64]{1,0:T(8,128)} %get-tuple-element.87) | copy-start | bytes 12292
  112.9 22.9 %all-to-all-start = ((f32[8,2,16,8,128]{4,3,2,1,0:T(8,128)}), f32[8,2,16,8,128]{4,3,2,1,0:T(8,128)S(1)}, u32[]{:S(2)}, u32[]{:S(2)}) async-start(f32[8,2,16,8,128]{4,3,2,1,0:T(8,128)} %maximum_bitcast_fusion), calls=%async_computation | async-start | bytes 2097152 | tf_op jit(solution)/shard_map/all_to_all | solution.py:151
  131.5 11.2 %copy-start.13 = (f32[8,8]{1,0:T(8,128)S(1)}, f32[8,8]{1,0:T(8,128)}, u32[]{:S(2)}) copy-start(f32[8,8]{1,0:T(8,128)} %constant.100.clone) | copy-start | bytes 772
  135.7 19.8 %all-to-all-start.2 = ((f32[8,2,16,8,128]{4,3,2,1,0:T(8,128)}), f32[8,2,16,8,128]{4,3,2,1,0:T(8,128)S(1)}, u32[]{:S(2)}, u32[]{:S(2)}) async-start(f32[8,2,16,8,128]{4,3,2,1,0:T(8,128)} %maximum_bitcast_fusion.1), calls=%async_computation.2 | async-start | bytes 2097152 | tf_op jit(solution)/shard_map/all_to_all | solution.py:151
  155.5 19.6 %all-to-all-start.4 = ((f32[8,2,16,8,128]{4,3,2,1,0:T(8,128)}), f32[8,2,16,8,128]{4,3,2,1,0:T(8,128)S(1)}, u32[]{:S(2)}, u32[]{:S(2)}) async-start(f32[8,2,16,8,128]{4,3,2,1,0:T(8,128)} %maximum_bitcast_fusion.2), calls=%async_computation.4 | async-start | bytes 2097152 | tf_op jit(solution)/shard_map/all_to_all | solution.py:151
  176.1 19.4 %all-to-all-start.6 = ((f32[8,2,16,8,128]{4,3,2,1,0:T(8,128)}), f32[8,2,16,8,128]{4,3,2,1,0:T(8,128)S(1)}, u32[]{:S(2)}, u32[]{:S(2)}) async-start(f32[8,2,16,8,128]{4,3,2,1,0:T(8,128)} %maximum_bitcast_fusion.3), calls=%async_computation.6 | async-start | bytes 2097152 | tf_op jit(solution)/shard_map/all_to_all | solution.py:151
  196.4 19.4 %all-to-all-start.1 = ((f32[8,2,16,8,128]{4,3,2,1,0:T(8,128)}), f32[8,2,16,8,128]{4,3,2,1,0:T(8,128)S(1)}, u32[]{:S(2)}, u32[]{:S(2)}) async-start(f32[8,2,16,8,128]{4,3,2,1,0:T(8,128)} %pad_maximum_fusion.3), calls=%async_computation.1 | async-start | bytes 2097152 | tf_op jit(solution)/shard_map/all_to_all | solution.py:164
  200.9 19.4 %copy-start.28 = (f32[8,16]{1,0:T(8,128)S(1)}, f32[8,16]{1,0:T(8,128)}, u32[]{:S(2)}) copy-start(f32[8,16]{1,0:T(8,128)} %exponential_multiply_fusion.1) | copy-start | bytes 1540
  215.8 20.4 %all-to-all-start.3 = ((f32[8,2,16,8,128]{4,3,2,1,0:T(8,128)}), f32[8,2,16,8,128]{4,3,2,1,0:T(8,128)}, u32[]{:S(2)}, u32[]{:S(2)}) async-start(f32[8,2,16,8,128]{4,3,2,1,0:T(8,128)} %pad_maximum_fusion.4), calls=%async_computation.3 | async-start | bytes 2097152 | tf_op jit(solution)/shard_map/all_to_all | solution.py:164
  222.9 19.4 %copy-start.27 = (f32[8,16]{1,0:T(8,128)S(1)}, f32[8,16]{1,0:T(8,128)}, u32[]{:S(2)}) copy-start(f32[8,16]{1,0:T(8,128)} %exponential_multiply_fusion) | copy-start | bytes 1540
  236.2 20.2 %all-to-all-start.5 = ((f32[8,2,16,8,128]{4,3,2,1,0:T(8,128)}), f32[8,2,16,8,128]{4,3,2,1,0:T(8,128)}, u32[]{:S(2)}, u32[]{:S(2)}) async-start(f32[8,2,16,8,128]{4,3,2,1,0:T(8,128)} %pad_maximum_fusion.5), calls=%async_computation.5 | async-start | bytes 2097152 | tf_op jit(solution)/shard_map/all_to_all | solution.py:164
  256.4 19.4 %all-to-all-start.7 = ((f32[8,2,16,8,128]{4,3,2,1,0:T(8,128)}), f32[8,2,16,8,128]{4,3,2,1,0:T(8,128)S(1)}, u32[]{:S(2)}, u32[]{:S(2)}) async-start(f32[8,2,16,8,128]{4,3,2,1,0:T(8,128)} %pad_maximum_fusion.6), calls=%async_computation.7 | async-start | bytes 2097152 | tf_op jit(solution)/shard_map/all_to_all | solution.py:164
  261.0 14.8 %copy-start.10 = (f32[2,16,8,1024]{3,2,1,0:T(8,128)S(1)}, f32[2,16,8,1024]{3,2,1,0:T(8,128)}, u32[]{:S(2)}) copy-start(f32[2,16,8,1024]{3,2,1,0:T(8,128)} %copy_bitcast_fusion.3) | copy-start | bytes 3145732
  (30 other events, 102.0 us)

commit v2 on v1

v2 whole, which is shorter than its diff:
```python
import math

import jax
import jax.numpy as jnp
import numpy as np
from jax import lax
from jax.experimental import pallas as pl
from jax.experimental.pallas import tpu as pltpu
from jax.sharding import PartitionSpec as P

alpha_wrap = 0.25
step_rate = 0.5
flow_speed = 2.0
sweep_weights = [
    1.0 / (1.0 + 0.7 * math.cos(math.pi * (2 * order + 1) / 6.0)) for order in range(3)
]
Q_CHUNKS = 1
F_BLOCK = 4
HALO = 2


def reverse_bits(number, bit_count):
    result = number * 0
    for bit_place in range(bit_count):
        result = result + (number >> bit_place & 1) * (1 << bit_count - 1 - bit_place)
    return result


def shift_parts(freq_ids, total_steps):
    phase_angle = freq_ids.astype(jnp.float32) * (2.0 * math.pi / total_steps)
    root_scale = alpha_wrap ** (1.0 / total_steps)
    return (
        step_rate * (1.0 - root_scale * jnp.cos(phase_angle)),
        step_rate * root_scale * jnp.sin(phase_angle),
    )


def halo_pair(block, axis, dim, width):
    count = lax.axis_size(axis)
    forward = [(i, i + 1) for i in range(count - 1)]
    backward = [(i + 1, i) for i in range(count - 1)]
    size = block.shape[dim]
    top = lax.ppermute(lax.slice_in_dim(block, size - width, size, axis=dim), axis, forward)
    bottom = lax.ppermute(lax.slice_in_dim(block, 0, width, axis=dim), axis, backward)
    return top, bottom


def sweep_kernel(lam_ref, rhs_ref, top_ref, bot_ref, diff_ref, mask_ref, o_ref):
    block = rhs_ref.shape[1]
    cols = rhs_ref.shape[3]
    base = pl.program_id(0) * block
    diff = diff_ref[...]
    diag_base = 4.0 * diff + flow_speed
    keep = mask_ref[...]
    row8 = lax.broadcasted_iota(jnp.int32, (8, cols), 0)
    col = lax.broadcasted_iota(jnp.int32, (16, cols), 1)

    def frame(x, f):
        local = rhs_ref[x, f]
        bv = bot_ref[x, f]
        tv = top_ref[x, f]
        hi = jnp.where(row8 == 0, jnp.broadcast_to(bv[0:1], (8, cols)), 0.0)
        hi = jnp.where(row8 == 1, jnp.broadcast_to(bv[1:2], (8, cols)), hi)
        hi = jnp.where(row8 == 6, jnp.broadcast_to(tv[0:1], (8, cols)), hi)
        hi = jnp.where(row8 == 7, jnp.broadcast_to(tv[1:2], (8, cols)), hi)
        return jnp.concatenate([local, hi], axis=0)

    def around(v):
        north = pltpu.roll(v, 1, 0)
        south = pltpu.roll(v, 15, 0)
        west = jnp.where(col == 0, 0.0, pltpu.roll(v, 1, 1))
        east = jnp.where(col == cols - 1, 0.0, pltpu.roll(v, cols - 1, 1))
        return north, north + south + west + east

    def body(f, carry):
        lam_r = lam_ref[0, base + f]
        lam_i = lam_ref[1, base + f]
        dr = diag_base + lam_r
        inv_mag = 1.0 / (dr * dr + lam_i * lam_i)
        r_re = frame(0, f)
        r_im = frame(1, f)
        c_re = sweep_weights[0] * ((r_re * dr + r_im * lam_i) * inv_mag)
        c_im = sweep_weights[0] * ((r_im * dr - r_re * lam_i) * inv_mag)
        for order in (1, 2):
            n_re, b_re = around(c_re)
            n_im, b_im = around(c_im)
            a_re = dr * c_re - lam_i * c_im - diff * b_re - flow_speed * n_re
            a_im = dr * c_im + lam_i * c_re - diff * b_im - flow_speed * n_im
            s_re = r_re - a_re
            s_im = r_im - a_im
            c_re = c_re + sweep_weights[order] * ((s_re * dr + s_im * lam_i) * inv_mag)
            c_im = c_im + sweep_weights[order] * ((s_im * dr - s_re * lam_i) * inv_mag)
            if order == 1:
                c_re = c_re * keep
                c_im = c_im * keep
        o_ref[0, f] = c_re[0:8]
        o_ref[1, f] = c_im[0:8]
        return carry

    lax.fori_loop(0, block, body, 0)


def sweep_call(lam, spectrum, top, bottom, diff_frame, mask_frame):
    _, count, rows, cols = spectrum.shape
    block = F_BLOCK
    big = pl.BlockSpec((2, block, rows, cols), lambda g: (0, g, 0, 0))
    edge = pl.BlockSpec((2, block, HALO, cols), lambda g: (0, g, 0, 0))
    whole = pl.BlockSpec((16, cols), lambda g: (0, 0))
    return pl.pallas_call(
        sweep_kernel,
        out_shape=jax.ShapeDtypeStruct(spectrum.shape, jnp.float32),
        grid=(count // block,),
        in_specs=[pl.BlockSpec(memory_space=pltpu.SMEM), big, edge, edge, whole, whole],
        out_specs=big,
        compiler_params=pltpu.CompilerParams(dimension_semantics=("arbitrary",)),
        cost_estimate=pl.CostEstimate(
            flops=200 * spectrum.size, transcendentals=0, bytes_accessed=8 * spectrum.size
        ),
    )(lam, spectrum, top, bottom, diff_frame, mask_frame)


def frames(diffusivity, space_place, space_count):
    rows, cols = diffusivity.shape
    d_top, d_bot = halo_pair(diffusivity, "space", 0, HALO)
    gap = jnp.zeros((16 - rows - 2 * HALO, cols), jnp.float32)
    diff_frame = jnp.concatenate([diffusivity, d_bot, gap, d_top], axis=0)
    row = jnp.arange(16, dtype=jnp.int32)
    keep = (row < rows) | ((row == rows) & (space_place < space_count - 1)) | (
        (row == 15) & (space_place > 0)
    )
    mask_frame = jnp.broadcast_to(keep.astype(jnp.float32)[:, None], (16, cols))
    return diff_frame, mask_frame


def on_device(spectrum, diffusivity):
    local_count = spectrum.shape[1]
    row_count = spectrum.shape[2]
    col_count = spectrum.shape[3]
    tm_count = lax.axis_size("tm")
    space_count = lax.axis_size("space")
    bit_count = tm_count.bit_length() - 1
    total_steps = local_count * tm_count
    tm_place = lax.axis_index("tm")
    space_place = lax.axis_index("space")
    residue = reverse_bits(tm_place, bit_count)
    index_f = jnp.arange(local_count, dtype=jnp.int32)
    freq_ids = index_f * tm_count + residue
    lam = jnp.stack(shift_parts(freq_ids, total_steps))

    top, bottom = halo_pair(spectrum, "space", 2, HALO)
    diff_frame, mask_frame = frames(diffusivity, space_place, space_count)
    current = sweep_call(lam, spectrum, top, bottom, diff_frame, mask_frame)
    flat_field = current.reshape(2 * local_count, row_count * col_count)

    grid_angle = (index_f[:, None] * freq_ids[None, :] % total_steps).astype(jnp.float32) * (
        2.0 * math.pi / total_steps
    )
    cosine = jnp.cos(grid_angle)
    sine = jnp.sin(grid_angle)

    source_residue = np.array([reverse_bits(source, bit_count) for source in range(tm_count)])
    class_index = np.arange(tm_count)[:, None] * source_residue[None, :] % tm_count
    class_angle = class_index.astype(np.float64) * (2.0 * math.pi / tm_count)
    class_cos = jnp.asarray(np.cos(class_angle), jnp.float32)
    class_sin = jnp.asarray(np.sin(class_angle), jnp.float32)
    high = lax.Precision.HIGHEST
    step_rate_log = -math.log(alpha_wrap) / total_steps
    col_block = col_count // tm_count

    chunk = local_count // Q_CHUNKS
    pieces = []
    for c in range(Q_CHUNKS):
        qs = slice(c * chunk, (c + 1) * chunk)
        table = jnp.concatenate(
            [jnp.concatenate([cosine[qs], -sine[qs]], 1), jnp.concatenate([sine[qs], cosine[qs]], 1)], 0
        )
        spectral = jnp.dot(table, flat_field, precision=high)
        outgoing = spectral.reshape(2, chunk, row_count, tm_count, col_block)
        outgoing = jnp.moveaxis(outgoing, 3, 0)
        arrived = lax.all_to_all(outgoing, "tm", 0, 0, tiled=True)
        a_re = arrived[:, 0].reshape(tm_count, -1)
        a_im = arrived[:, 1].reshape(tm_count, -1)
        comb_re = jnp.dot(class_cos, a_re, precision=high) - jnp.dot(class_sin, a_im, precision=high)
        comb_im = jnp.dot(class_sin, a_re, precision=high) + jnp.dot(class_cos, a_im, precision=high)
        step_ids = (
            jnp.arange(tm_count, dtype=jnp.int32)[:, None] * local_count + c * chunk
            + jnp.arange(chunk, dtype=jnp.int32)[None, :]
        ).astype(jnp.float32)
        factor = (jnp.exp(step_ids * step_rate_log) / math.sqrt(total_steps))[:, :, None, None]
        comb_re = comb_re.reshape(tm_count, chunk, row_count, col_block) * factor
        comb_im = comb_im.reshape(tm_count, chunk, row_count, col_block) * factor
        combined = jnp.stack([comb_re, comb_im], 1)
        returned = lax.all_to_all(combined, "tm", 0, 0, tiled=True)
        pieces.append(jnp.moveaxis(returned, 0, 3).reshape(2, chunk, row_count, col_count))
    return jnp.concatenate(pieces, axis=1) if len(pieces) > 1 else pieces[0]


def solution(mesh):
    in_specs = (P(None, "tm", "space", None), P("space", None))
    out_specs = P(None, "tm", "space", None)
    return jax.shard_map(
        on_device, mesh=mesh, in_specs=in_specs, out_specs=out_specs, check_vma=False
    )
```

time: 285 us -> 218 us (0.76); the launches traced: 280 us -> 217 us
  other arithmetic: 80.1 us -> 2.86 us
  blocking collectives: 0 us -> 67.7 us
  starting transfers between devices: 43.9 us -> 15.7 us
  waiting for transfers between devices: 80 us -> 57.6 us
  Pallas kernels: 0 us -> 20.3 us
  matrix products: 28.5 us -> 13 us
  local copies, waits for them, and re-layouts: 46.2 us -> 39.8 us
    all_to_all x0 -> x1, blocking collectives: none -> 67.7 us  [on_device(): returned = lax.all_to_all(combined, 'tm', 0, 0, tiled=True)]
    all_to_all x4 -> x0, waiting for transfers between devices: 46.5 us -> none  [on_device(): returned = lax.all_to_all(combined, 'tm', 0, 0, tiled=True)]
    add x5 -> x1, other arithmetic: 27.8 us -> 0.01 us  [on_device(): freq_ids = index_f * tm_count + residue]
    select_n x2 -> x0, other arithmetic: 22.2 us -> none  [the longest x1 14.9 us: on_device(): c_im = jnp.where(keep, c_im, 0.0)]
    pallas_call x0 -> x1, Pallas kernels: none -> 20.3 us  [sweep_call(): pl.pallas_call(sweep_kernel, out_shape=jax.ShapeDtypeStruct(spectrum.shap...]
    all_to_all x4 -> x1, waiting for transfers between devices: 32.9 us -> 50.6 us  [on_device(): arrived = lax.all_to_all(outgoing, 'tm', 0, 0, tiled=True)]
    all_to_all x4 -> x0, starting transfers between devices: 15.8 us -> none  [on_device(): returned = lax.all_to_all(combined, 'tm', 0, 0, tiled=True)]
    all_to_all x4 -> x1, starting transfers between devices: 16.9 us -> 5.82 us  [on_device(): arrived = lax.all_to_all(outgoing, 'tm', 0, 0, tiled=True)]
  transfers between devices with their start and end apart: 12 -> 5, of which waited for: 9 -> 2; matrix products, arithmetic and copies ran while one was open for 20% -> 1% of each run, Pallas kernels for 0% -> 0%
where the time goes in v2:
time: 218 us; the launch traced here: 217 us
  blocking collectives  67.7 us (31%)
  waiting for transfers between devices  57.6 us (26%)
  local copies, waits for them, and re-layouts  39.8 us (18%)
  Pallas kernels  20.3 us (9%)
  starting transfers between devices  15.7 us (7%)
  matrix products  13 us (6%)
  other arithmetic  2.86 us (1%)
    all_to_all x1, blocking collectives, on_device(): returned = lax.all_to_all(combined, 'tm', 0, 0, tiled=True)  67.7 us
    all_to_all x1, waiting for transfers between devices, on_device(): arrived = lax.all_to_all(outgoing, 'tm', 0, 0, tiled=True)  50.6 us
    pallas_call x1, Pallas kernels, sweep_call(): pl.pallas_call(sweep_kernel, out_shape=jax.ShapeDtypeStruct(spectrum.shap...  20.3 us
    slice x2, local copies, waits for them, and re-layouts, on_device(): a_im = arrived[:, 1].reshape(tm_count, -1)  8.11 us
    unnamed x11, local copies, waits for them, and re-layouts  7.95 us
    ppermute x2, waiting for transfers between devices, halo_pair(): lax.ppermute(lax.slice_in_dim(block, 0, width, axis=dim), axis, backward)  6.99 us
    all_to_all x1, starting transfers between devices, on_device(): arrived = lax.all_to_all(outgoing, 'tm', 0, 0, tiled=True)  5.82 us
    ppermute x2, starting transfers between devices, halo_pair(): lax.ppermute(lax.slice_in_dim(block, 0, width, axis=dim), axis, backward)  5.56 us
  transfers between devices with their start and end apart: 5, of which 2 were waited for; matrix products, arithmetic and copies ran while one was open for 1% of the time, Pallas kernels for 0%

profile of v2, /device:TPU:4, one launch (start us, length us, event | category | flops | bytes accessed | tf_op | source)
XLA Modules:
  0.0 217.2 jit_solution(1357414585289583306)
XLA Ops:
  0.0 4.6 %fusion.10 = (f32[2,64,2,1024]{3,2,1,0:T(2,128)S(1)}, f32[2,64,2,1024]{3,2,1,0:T(2,128)S(1)}) fusion(f32[2,64,8,1024]{3,2,1,0:T(8,128)} %rhs_ref.1), kind=kLoop, calls=%fused_computation.30 | loop fusion | bytes 4194304 | tf_op jit(solution)/shard_map/slice | solution.py:44
  4.6 1.9 collective-permute-start
  6.5 3.6 %collective-permute-start.1 = (f32[2,64,2,1024]{3,2,1,0:T(2,128)S(1)}, f32[2,64,2,1024]{3,2,1,0:T(2,128)}, u32[]{:S(2)}, u32[]{:S(2)}) collective-permute-start(f32[2,64,2,1024]{3,2,1,0:T(2,128)S(1)} %get-tuple-element.7), channel_id=1, source_target_pairs={{1,0},{2,1},{3,2},{4,3},{5,4},{6,5},{7,6},{8,7},{9,8},{10,9},{11,1... | collective-permute-start | bytes 3145736 | tf_op jit(solution)/shard_map/ppermute | solution.py:44
  10.2 1.9 collective-permute-start.2
  12.2 2.4 %collective-permute-start.3 = (f32[2,1024]{1,0:T(2,128)S(1)}, f32[2,1024]{1,0:T(2,128)S(1)}, u32[]{:S(2)}, u32[]{:S(2)}) collective-permute-start(f32[2,1024]{1,0:T(2,128)S(1)} %get-tuple-element.10), channel_id=1, source_target_pairs={{0,1},{1,2},{2,3},{3,4},{4,5},{5,6},{6,7},{7,8},{8,9},{9,10},{10,1... | collective-permute-start | bytes 24584 | tf_op jit(solution)/shard_map/ppermute | solution.py:43
  15.6 7.0 %collective-permute-done.2 = f32[2,1024]{1,0:T(2,128)S(1)} collective-permute-done((f32[2,1024]{1,0:T(2,128)S(1)}, f32[2,1024]{1,0:T(2,128)S(1)}, u32[]{:S(2)}, u32[]{:S(2)}) %collective-permute-start.2) | collective-permute-done | bytes 8224 | tf_op jit(solution)/shard_map/ppermute | solution.py:44
  24.3 20.3 %shard_map.46 = f32[2,64,8,1024]{3,2,1,0:T(8,128)} custom-call(f32[2,64]{1,0:T(2,128)} %pad_maximum_fusion.2.lam_ref, f32[2,64,8,1024]{3,2,1,0:T(8,128)} %rhs_ref.1, f32[2,64,2,1024]{3,2,1,0:T(2,128)} %copy-done.1, f32[2,64,2,1024]{3,2,1,0:T(2,128)} %collective-permute-done.1.bot_ref, f32[16,1024]{1,0:T(8,128)} %pad_maximum_fusion.1.diff_ref, ...), custom_call_target="tpu_custom_call" | custom-call | flops 209715200 | bytes 8388608 | tf_op jit(solution)/shard_map/pallas_call | solution.py:109
  44.6 7.7 %copy.24 = f32[16,8,8,1024]{3,1,2,0:T(8,128)} copy(f32[16,8,8,1024]{3,2,1,0:T(8,128)} %bitcast.45) | data formatting | bytes 8388608
  52.3 5.6 %copy.15 = f32[8192,128]{1,0:T(8,128)} copy(f32[8192,128]{0,1:T(8,128)} %bitcast.47) | data formatting | bytes 8388608 | tf_op jit(solution)/shard_map/dot_general | solution.py:177
  57.9 5.4 %convolution_bitcast_fusion = f32[8,2,64,8,128]{4,2,0,3,1:T(8,128)S(1)} fusion(f32[2,64,128,1,1]{2,1,4,3,0:T(8,128)S(1)} %bitcast.50, f32[8,8,128,128,1]{3,2,1,0,4:T(8,128)} %bitcast.46), kind=kOutput, calls=%fused_computation.4 | convolution fusion | flops 1610612736 | bytes 8454144 | tf_op jit(solution)/shard_map/dot_general | solution.py:177
  63.3 2.3 %copy.16 = f32[8,2,64,8,128]{4,2,3,1,0:T(8,128)} copy(f32[8,2,64,8,128]{4,2,0,3,1:T(8,128)S(1)} %convolution_bitcast_fusion) | data formatting | bytes 8388608 | tf_op jit(solution)/shard_map/transpose | solution.py:179
  65.6 5.8 %all-to-all-start = ((f32[8,2,64,8,128]{4,2,3,1,0:T(8,128)}), f32[8,2,64,8,128]{4,2,3,1,0:T(8,128)}, u32[]{:S(2)}, u32[]{:S(2)}) async-start(f32[8,2,64,8,128]{4,2,3,1,0:T(8,128)} %copy.16), calls=%async_computation | async-start | bytes 8388608 | tf_op jit(solution)/shard_map/all_to_all | solution.py:180
  71.5 50.6 %all-to-all-done = f32[8,2,64,8,128]{4,2,3,1,0:T(8,128)} async-done(((f32[8,2,64,8,128]{4,2,3,1,0:T(8,128)}), f32[8,2,64,8,128]{4,2,3,1,0:T(8,128)}, u32[]{:S(2)}, u32[]{:S(2)}) %all-to-all-start) | async-done | bytes 4194336 | tf_op jit(solution)/shard_map/all_to_all | solution.py:180
  122.1 4.0 %fusion.9 = (f32[8,1,64,8,128]{4,2,3,1,0:T(8,128)}, f32[8,1,64,8,128]{4,2,3,1,0:T(8,128)S(1)}) fusion(f32[8,2,64,8,128]{4,2,3,1,0:T(8,128)} %all-to-all-done), kind=kLoop, calls=%fused_computation.29 | loop fusion | bytes 8388608 | tf_op jit(solution)/shard_map/slice | solution.py:182
  126.1 2.5 %copy.17 = f32[8,1,64,8,128]{4,3,2,0,1:T(8,128)} copy(f32[8,1,64,8,128]{4,2,3,1,0:T(8,128)S(1)} %get-tuple-element.6) | data formatting | bytes 4194304 | tf_op jit(solution)/shard_map/slice | solution.py:181
  128.7 2.0 reshape_squeeze.6
  130.6 4.1 %copy.18 = f32[8,1,64,8,128]{4,3,2,0,1:T(8,128)} copy(f32[8,1,64,8,128]{4,2,3,1,0:T(8,128)} %get-tuple-element.5) | data formatting | bytes 4194304 | tf_op jit(solution)/shard_map/slice | solution.py:182
  134.7 3.3 %reshape_squeeze.7 = f32[8,65536]{1,0:T(8,128)} reshape(f32[8,1,64,8,128]{4,3,2,0,1:T(8,128)} %copy.18) | data formatting | bytes 4194304 | tf_op jit(solution)/shard_map/reshape;squeeze | solution.py:182
  138.0 1.9 fusion.13
  139.9 1.9 fusion.12
  141.8 1.9 convolution_add_fusion
  143.7 1.9 convolution_subtract_fusion
  146.9 67.7 %all_to_all.10 = f32[8,2,64,8,128]{4,3,2,1,0:T(8,128)S(1)} all-to-all(f32[8,2,64,8,128]{4,3,2,1,0:T(8,128)S(1)} %pad_maximum_fusion), channel_id=1, replica_groups=mesh['tm'=8,'space'=16] {'tm'}, dimensions={0} | all-to-all | bytes 8388608 | tf_op jit(solution)/shard_map/all_to_all | solution.py:193
  214.6 2.6 %copy_bitcast_fusion = f32[2,64,8,1024]{3,2,1,0:T(8,128)} fusion(f32[8,2,64,8,128]{4,3,2,1,0:T(8,128)S(1)} %all_to_all.10), kind=kLoop, calls=%fused_computation.2 | loop fusion | bytes 8388608 | tf_op jit(solution)/shard_map/reshape | solution.py:194
  (28 shorter events, 4.0 us)
Async XLA Ops:
  0.0 10.2 %copy-start.2 = (f32[8,1024]{1,0:T(8,128)S(1)}, f32[8,1024]{1,0:T(8,128)}, u32[]{:S(2)}) copy-start(f32[8,1024]{1,0:T(8,128)} %param.5) | copy-start | bytes 98308
  4.6 18.7 %collective-permute-start = (f32[2,64,2,1024]{3,2,1,0:T(2,128)S(1)}, f32[2,64,2,1024]{3,2,1,0:T(2,128)S(1)}, u32[]{:S(2)}, u32[]{:S(2)}) collective-permute-start(f32[2,64,2,1024]{3,2,1,0:T(2,128)S(1)} %get-tuple-element.8), channel_id=1, source_target_pairs={{0,1},{1,2},{2,3},{3,4},{4,5},{5,6},{6,7},{7,8},{8,9},{9,10},{10,1... | collective-permute-start | bytes 3145736 | tf_op jit(solution)/shard_map/ppermute | solution.py:43
  6.5 16.7 %collective-permute-start.1 = (f32[2,64,2,1024]{3,2,1,0:T(2,128)S(1)}, f32[2,64,2,1024]{3,2,1,0:T(2,128)}, u32[]{:S(2)}, u32[]{:S(2)}) collective-permute-start(f32[2,64,2,1024]{3,2,1,0:T(2,128)S(1)} %get-tuple-element.7), channel_id=1, source_target_pairs={{1,0},{2,1},{3,2},{4,3},{5,4},{6,5},{7,6},{8,7},{9,8},{10,9},{11,1... | collective-permute-start | bytes 3145736 | tf_op jit(solution)/shard_map/ppermute | solution.py:44
  10.2 12.4 %collective-permute-start.2 = (f32[2,1024]{1,0:T(2,128)S(1)}, f32[2,1024]{1,0:T(2,128)S(1)}, u32[]{:S(2)}, u32[]{:S(2)}) collective-permute-start(f32[2,1024]{1,0:T(2,128)S(1)} %get-tuple-element.9), channel_id=1, source_target_pairs={{1,0},{2,1},{3,2},{4,3},{5,4},{6,5},{7,6},{8,7},{9,8},{10,9},{11,1... | collective-permute-start | bytes 24584 | tf_op jit(solution)/shard_map/ppermute | solution.py:44
  12.2 10.4 %collective-permute-start.3 = (f32[2,1024]{1,0:T(2,128)S(1)}, f32[2,1024]{1,0:T(2,128)S(1)}, u32[]{:S(2)}, u32[]{:S(2)}) collective-permute-start(f32[2,1024]{1,0:T(2,128)S(1)} %get-tuple-element.10), channel_id=1, source_target_pairs={{0,1},{1,2},{2,3},{3,4},{4,5},{5,6},{6,7},{7,8},{8,9},{9,10},{10,1... | collective-permute-start | bytes 24584 | tf_op jit(solution)/shard_map/ppermute | solution.py:43
  23.3 1.0 copy-start.1
  65.6 56.5 %all-to-all-start = ((f32[8,2,64,8,128]{4,2,3,1,0:T(8,128)}), f32[8,2,64,8,128]{4,2,3,1,0:T(8,128)}, u32[]{:S(2)}, u32[]{:S(2)}) async-start(f32[8,2,64,8,128]{4,2,3,1,0:T(8,128)} %copy.16), calls=%async_computation | async-start | bytes 8388608 | tf_op jit(solution)/shard_map/all_to_all | solution.py:180
  134.7 3.3 %copy-start.3 = (f32[8,8]{1,0:T(8,128)S(1)}, f32[8,8]{1,0:T(8,128)}, u32[]{:S(2)}) copy-start(f32[8,8]{1,0:T(8,128)} %constant.62.clone) | copy-start | bytes 772
  138.0 1.9 copy-start.4
  139.9 1.9 copy-start

commit v3 on v2

--- a/solution.py
+++ b/solution.py
@@ -1,3 +1,4 @@
+import functools
 import math
 
 import jax
@@ -14,7 +15,7 @@
 sweep_weights = [
     1.0 / (1.0 + 0.7 * math.cos(math.pi * (2 * order + 1) / 6.0)) for order in range(3)
 ]
-Q_CHUNKS = 1
+Q_BLOCK = 16
 F_BLOCK = 4
 HALO = 2
 
@@ -45,8 +46,9 @@
     return top, bottom
 
 
-def sweep_kernel(lam_ref, rhs_ref, top_ref, bot_ref, diff_ref, mask_ref, o_ref):
+def sweep_kernel(lam_ref, rhs_ref, top_ref, bot_ref, diff_ref, mask_ref, table_ref, o_ref, field):
     block = rhs_ref.shape[1]
+    count = lam_ref.shape[1]
     cols = rhs_ref.shape[3]
     base = pl.program_id(0) * block
     diff = diff_ref[...]
@@ -93,30 +95,103 @@
             if order == 1:
                 c_re = c_re * keep
                 c_im = c_im * keep
-        o_ref[0, f] = c_re[0:8]
-        o_ref[1, f] = c_im[0:8]
+        width = field.shape[2]
+        for blk in range(field.shape[0]):
+            lanes = slice(blk * width, (blk + 1) * width)
+            field[blk, pl.ds(pl.multiple_of((base + f) * 8, 8), 8), :] = c_re[0:8, lanes]
+            field[blk, pl.ds(pl.multiple_of((count + base + f) * 8, 8), 8), :] = c_im[0:8, lanes]
         return carry
 
     lax.fori_loop(0, block, body, 0)
 
-
-def sweep_call(lam, spectrum, top, bottom, diff_frame, mask_frame):
+    @pl.when(pl.program_id(0) == pl.num_programs(0) - 1)
+    def _():
+        table = table_ref[...]
+        for blk in range(o_ref.shape[0]):
+            for r in range(8):
+                plane = field[blk, pl.ds(r, 2 * count, stride=8), :]
+                o_ref[blk, pl.ds(r, 2 * count, stride=8), :] = jnp.dot(
+                    table, plane, precision=lax.Precision.HIGHEST, preferred_element_type=jnp.float32
+                )
+
+
+def sweep_call(lam, spectrum, top, bottom, diff_frame, mask_frame, table, blocks):
     _, count, rows, cols = spectrum.shape
     block = F_BLOCK
+    width = cols // blocks
     big = pl.BlockSpec((2, block, rows, cols), lambda g: (0, g, 0, 0))
     edge = pl.BlockSpec((2, block, HALO, cols), lambda g: (0, g, 0, 0))
     whole = pl.BlockSpec((16, cols), lambda g: (0, 0))
+    square = pl.BlockSpec((2 * count, 2 * count), lambda g: (0, 0))
+    out_rows = 2 * count * rows
     return pl.pallas_call(
         sweep_kernel,
-        out_shape=jax.ShapeDtypeStruct(spectrum.shape, jnp.float32),
+        out_shape=jax.ShapeDtypeStruct((blocks, out_rows, width), jnp.float32),
         grid=(count // block,),
-        in_specs=[pl.BlockSpec(memory_space=pltpu.SMEM), big, edge, edge, whole, whole],
-        out_specs=big,
+        in_specs=[pl.BlockSpec(memory_space=pltpu.SMEM), big, edge, edge, whole, whole, square],
+        out_specs=pl.BlockSpec((blocks, out_rows, width), lambda g: (0, 0, 0)),
+        scratch_shapes=[pltpu.VMEM((blocks, out_rows, width), jnp.float32)],
         compiler_params=pltpu.CompilerParams(dimension_semantics=("arbitrary",)),
         cost_estimate=pl.CostEstimate(
             flops=200 * spectrum.size, transcendentals=0, bytes_accessed=8 * spectrum.size
         ),
-    )(lam, spectrum, top, bottom, diff_frame, mask_frame)
+    )(lam, spectrum, top, bottom, diff_frame, mask_frame, table)
+
+
+def combine_kernel(weights, fac_ref, a_ref, o_ref):
+    block = a_ref.shape[2] // 8
+    base = pl.program_id(0) * block
+
+    def body(qi, carry):
+        rows = pl.ds(pl.multiple_of(qi * 8, 8), 8)
+        parts = [(a_ref[s, 0, rows, :], a_ref[s, 1, rows, :]) for s in range(a_ref.shape[0])]
+        for m, row in enumerate(weights):
+            acc_re = []
+            acc_im = []
+            for (c, s), (x_re, x_im) in zip(row, parts):
+                for coef, val, acc in ((c, x_re, acc_re), (-s, x_im, acc_re), (s, x_re, acc_im), (c, x_im, acc_im)):
+                    if coef == 1.0:
+                        acc.append(val)
+                    elif coef == -1.0:
+                        acc.append(-val)
+                    elif coef != 0.0:
+                        acc.append(coef * val)
+            scale = fac_ref[m, base + qi]
+            o_ref[m, 0, rows, :] = sum(acc_re[1:], acc_re[0]) * scale
+            o_ref[m, 1, rows, :] = sum(acc_im[1:], acc_im[0]) * scale
+        return carry
+
+    lax.fori_loop(0, block, body, 0)
+
+
+def combine_call(weights, factor, arrived, q_block):
+    blocks, _, rows, width = arrived.shape
+    spec = pl.BlockSpec((blocks, 2, q_block * 8, width), lambda g: (0, 0, g, 0))
+    return pl.pallas_call(
+        functools.partial(combine_kernel, weights),
+        out_shape=jax.ShapeDtypeStruct(arrived.shape, jnp.float32),
+        grid=(rows // (q_block * 8),),
+        in_specs=[pl.BlockSpec(memory_space=pltpu.SMEM), spec],
+        out_specs=spec,
+        compiler_params=pltpu.CompilerParams(dimension_semantics=("arbitrary",)),
+        cost_estimate=pl.CostEstimate(
+            flops=40 * arrived.size, transcendentals=0, bytes_accessed=8 * arrived.size
+        ),
+    )(factor, arrived)
+
+
+def class_weights(tm_count, bit_count):
+    rows = []
+    for m in range(tm_count):
+        row = []
+        for source in range(tm_count):
+            angle = 2.0 * math.pi * ((m * reverse_bits(source, bit_count)) % tm_count) / tm_count
+            c, s = math.cos(angle), math.sin(angle)
+            c = float(np.float32(0.0 if abs(c) < 1e-9 else c))
+            s = float(np.float32(0.0 if abs(s) < 1e-9 else s))
+            row.append((c, s))
+        rows.append(tuple(row))
+    return tuple(rows)
 
 
 def frames(diffusivity, space_place, space_count):
@@ -149,50 +224,28 @@
 
     top, bottom = halo_pair(spectrum, "space", 2, HALO)
     diff_frame, mask_frame = frames(diffusivity, space_place, space_count)
-    current = sweep_call(lam, spectrum, top, bottom, diff_frame, mask_frame)
-    flat_field = current.reshape(2 * local_count, row_count * col_count)
-
     grid_angle = (index_f[:, None] * freq_ids[None, :] % total_steps).astype(jnp.float32) * (
         2.0 * math.pi / total_steps
     )
     cosine = jnp.cos(grid_angle)
     sine = jnp.sin(grid_angle)
-
-    source_residue = np.array([reverse_bits(source, bit_count) for source in range(tm_count)])
-    class_index = np.arange(tm_count)[:, None] * source_residue[None, :] % tm_count
-    class_angle = class_index.astype(np.float64) * (2.0 * math.pi / tm_count)
-    class_cos = jnp.asarray(np.cos(class_angle), jnp.float32)
-    class_sin = jnp.asarray(np.sin(class_angle), jnp.float32)
-    high = lax.Precision.HIGHEST
-    step_rate_log = -math.log(alpha_wrap) / total_steps
+    table = jnp.concatenate(
+        [jnp.concatenate([cosine, -sine], 1), jnp.concatenate([sine, cosine], 1)], 0
+    )
+    outgoing = sweep_call(lam, spectrum, top, bottom, diff_frame, mask_frame, table, tm_count)
     col_block = col_count // tm_count
-
-    chunk = local_count // Q_CHUNKS
-    pieces = []
-    for c in range(Q_CHUNKS):
-        qs = slice(c * chunk, (c + 1) * chunk)
-        table = jnp.concatenate(
-            [jnp.concatenate([cosine[qs], -sine[qs]], 1), jnp.concatenate([sine[qs], cosine[qs]], 1)], 0
-        )
-        spectral = jnp.dot(table, flat_field, precision=high)
-        outgoing = spectral.reshape(2, chunk, row_count, tm_count, col_block)
-        outgoing = jnp.moveaxis(outgoing, 3, 0)
-        arrived = lax.all_to_all(outgoing, "tm", 0, 0, tiled=True)
-        a_re = arrived[:, 0].reshape(tm_count, -1)
-        a_im = arrived[:, 1].reshape(tm_count, -1)
-        comb_re = jnp.dot(class_cos, a_re, precision=high) - jnp.dot(class_sin, a_im, precision=high)
-        comb_im = jnp.dot(class_sin, a_re, precision=high) + jnp.dot(class_cos, a_im, precision=high)
-        step_ids = (
-            jnp.arange(tm_count, dtype=jnp.int32)[:, None] * local_count + c * chunk
-            + jnp.arange(chunk, dtype=jnp.int32)[None, :]
-        ).astype(jnp.float32)
-        factor = (jnp.exp(step_ids * step_rate_log) / math.sqrt(total_steps))[:, :, None, None]
-        comb_re = comb_re.reshape(tm_count, chunk, row_count, col_block) * factor
-        comb_im = comb_im.reshape(tm_count, chunk, row_count, col_block) * factor
-        combined = jnp.stack([comb_re, comb_im], 1)
-        returned = lax.all_to_all(combined, "tm", 0, 0, tiled=True)
-        pieces.append(jnp.moveaxis(returned, 0, 3).reshape(2, chunk, row_count, col_count))
-    return jnp.concatenate(pieces, axis=1) if len(pieces) > 1 else pieces[0]
+    outgoing = outgoing.reshape(tm_count, 2, local_count * row_count, col_block)
+    arrived = lax.all_to_all(outgoing, "tm", 0, 0, tiled=True)
+
+    step_ids = (
+        jnp.arange(tm_count, dtype=jnp.int32)[:, None] * local_count
+        + jnp.arange(local_count, dtype=jnp.int32)[None, :]
+    ).astype(jnp.float32)
+    factor = jnp.exp(step_ids * (-math.log(alpha_wrap) / total_steps)) / math.sqrt(total_steps)
+    combined = combine_call(class_weights(tm_count, bit_count), factor, arrived, Q_BLOCK)
+    returned = lax.all_to_all(combined, "tm", 0, 0, tiled=True)
+    returned = returned.reshape(tm_count, 2, local_count, row_count, col_block)
+    return jnp.moveaxis(returned, 0, 3).reshape(2, local_count, row_count, col_count)
 
 
 def solution(mesh):

time: 218 us -> 183 us (0.84)
  local copies, waits for them, and re-layouts: 39.8 us -> 8.29 us
  matrix products: 13 us -> 0 us
  Pallas kernels: 20.3 us -> 31.2 us
    dot_general x5 -> x0, matrix products: 13 us -> none  [the longest x1 5.44 us: on_device(): spectral = jnp.dot(table, flat_field, precision=high)]
    pallas_call x1 -> x2, Pallas kernels: 20.3 us -> 31.2 us  [the longest x1 25.5 us: sweep_call(): pl.pallas_call(sweep_kernel, out_shape=jax.ShapeDtypeStruct((blocks, out_...]
    slice x3 -> x0, local copies, waits for them, and re-layouts: 10.6 us -> none  [the longest x2 8.11 us: on_device(): a_im = arrived[:, 1].reshape(tm_count, -1)]
    unnamed x11 -> x4, local copies, waits for them, and re-layouts: 7.95 us -> 0.19 us
    dot_general x1 -> x0, local copies, waits for them, and re-layouts: 5.56 us -> none  [on_device(): spectral = jnp.dot(table, flat_field, precision=high)]
    another operation x2 -> x0, local copies, waits for them, and re-layouts: 5.26 us -> none  [the longest x1 3.3 us: on_device(): a_im = arrived[:, 1].reshape(tm_count, -1)]
    transpose x1 -> x0, local copies, waits for them, and re-layouts: 2.32 us -> none  [on_device(): outgoing = jnp.moveaxis(outgoing, 3, 0)]
  transfers between devices with their start and end apart: 5 -> 5, of which waited for: 2 -> 2; matrix products, arithmetic and copies ran while one was open for 1% -> 2% of each run, Pallas kernels for 0% -> 0%
where the time goes in v3:
time: 183 us
  blocking collectives  67.9 us (37%)
  waiting for transfers between devices  56.4 us (31%)
  Pallas kernels  31.2 us (17%)
  starting transfers between devices  15.7 us (9%)
  local copies, waits for them, and re-layouts  8.29 us (5%)
  other arithmetic  2.87 us (2%)
    all_to_all x1, blocking collectives, on_device(): returned = lax.all_to_all(combined, 'tm', 0, 0, tiled=True)  67.9 us
    all_to_all x1, waiting for transfers between devices, on_device(): arrived = lax.all_to_all(outgoing, 'tm', 0, 0, tiled=True)  50 us
    pallas_call x1, Pallas kernels, sweep_call(): pl.pallas_call(sweep_kernel, out_shape=jax.ShapeDtypeStruct((blocks, out_...  25.5 us
    ppermute x2, waiting for transfers between devices, halo_pair(): lax.ppermute(lax.slice_in_dim(block, 0, width, axis=dim), axis, backward)  6.41 us
    all_to_all x1, starting transfers between devices, on_device(): arrived = lax.all_to_all(outgoing, 'tm', 0, 0, tiled=True)  5.82 us
    pallas_call x1, Pallas kernels, combine_call(): pl.pallas_call(functools.partial(combine_kernel, weights), out_shape=jax....  5.78 us
    ppermute x2, starting transfers between devices, halo_pair(): lax.ppermute(lax.slice_in_dim(block, 0, width, axis=dim), axis, backward)  5.56 us
    slice x2, local copies, waits for them, and re-layouts, halo_pair(): lax.slice_in_dim(block, 0, width, axis=dim)  4.61 us
  transfers between devices with their start and end apart: 5, of which 2 were waited for; matrix products, arithmetic and copies ran while one was open for 2% of the time, Pallas kernels for 0%

profile of v3, /device:TPU:4, one launch (start us, length us, event | category | flops | bytes accessed | tf_op | source)
XLA Modules:
  0.0 182.6 jit_solution(5788743585342655710)
XLA Ops:
  0.0 4.6 %fusion.9 = (f32[2,64,2,1024]{3,2,1,0:T(2,128)S(1)}, f32[2,64,2,1024]{3,2,1,0:T(2,128)S(1)}) fusion(f32[2,64,8,1024]{3,2,1,0:T(8,128)} %rhs_ref.1), kind=kLoop, calls=%fused_computation.23 | loop fusion | bytes 4194304 | tf_op jit(solution)/shard_map/slice | solution.py:45
  4.6 1.9 %collective-permute-start = (f32[2,64,2,1024]{3,2,1,0:T(2,128)S(1)}, f32[2,64,2,1024]{3,2,1,0:T(2,128)S(1)}, u32[]{:S(2)}, u32[]{:S(2)}) collective-permute-start(f32[2,64,2,1024]{3,2,1,0:T(2,128)S(1)} %get-tuple-element.6), channel_id=1, source_target_pairs={{0,1},{1,2},{2,3},{3,4},{4,5},{5,6},{6,7},{7,8},{8,9},{9,10},{10,1... | collective-permute-start | bytes 3145736 | tf_op jit(solution)/shard_map/ppermute | solution.py:44
  6.5 3.6 %collective-permute-start.1 = (f32[2,64,2,1024]{3,2,1,0:T(2,128)S(1)}, f32[2,64,2,1024]{3,2,1,0:T(2,128)}, u32[]{:S(2)}, u32[]{:S(2)}) collective-permute-start(f32[2,64,2,1024]{3,2,1,0:T(2,128)S(1)} %get-tuple-element.5), channel_id=1, source_target_pairs={{1,0},{2,1},{3,2},{4,3},{5,4},{6,5},{7,6},{8,7},{9,8},{10,9},{11,1... | collective-permute-start | bytes 3145736 | tf_op jit(solution)/shard_map/ppermute | solution.py:45
  10.2 0.0 copy-done.1
  10.2 1.9 %collective-permute-start.2 = (f32[2,1024]{1,0:T(2,128)S(1)}, f32[2,1024]{1,0:T(2,128)S(1)}, u32[]{:S(2)}, u32[]{:S(2)}) collective-permute-start(f32[2,1024]{1,0:T(2,128)S(1)} %get-tuple-element.7), channel_id=1, source_target_pairs={{1,0},{2,1},{3,2},{4,3},{5,4},{6,5},{7,6},{8,7},{9,8},{10,9},{11,1... | collective-permute-start | bytes 24584 | tf_op jit(solution)/shard_map/ppermute | solution.py:45
  12.2 2.4 %collective-permute-start.3 = (f32[2,1024]{1,0:T(2,128)S(1)}, f32[2,1024]{1,0:T(2,128)S(1)}, u32[]{:S(2)}, u32[]{:S(2)}) collective-permute-start(f32[2,1024]{1,0:T(2,128)S(1)} %get-tuple-element.8), channel_id=1, source_target_pairs={{0,1},{1,2},{2,3},{3,4},{4,5},{5,6},{6,7},{7,8},{8,9},{9,10},{10,1... | collective-permute-start | bytes 24584 | tf_op jit(solution)/shard_map/ppermute | solution.py:44
  14.6 0.6 pad_maximum_fusion.1.lam_ref
  15.2 0.1 fusion.8
  15.4 0.7 maximum_maximum_fusion.table_ref
  16.1 0.1 pad.6.clone
  16.2 6.4 %collective-permute-done.2 = f32[2,1024]{1,0:T(2,128)S(1)} collective-permute-done((f32[2,1024]{1,0:T(2,128)S(1)}, f32[2,1024]{1,0:T(2,128)S(1)}, u32[]{:S(2)}, u32[]{:S(2)}) %collective-permute-start.2) | collective-permute-done | bytes 8224 | tf_op jit(solution)/shard_map/ppermute | solution.py:45
  22.6 0.0 collective-permute-done.3
  22.6 0.7 pad_maximum_fusion.diff_ref
  23.3 0.0 collective-permute-done.top_ref
  23.3 0.0 collective-permute-done.1.bot_ref
  23.3 0.8 broadcast_in_dim.5.mask_ref
  24.1 0.2 copy-done
  24.3 25.5 %shard_map.28 = f32[8,1024,128]{2,1,0:T(8,128)} custom-call(f32[2,64]{1,0:T(2,128)} %pad_maximum_fusion.1.lam_ref, f32[2,64,8,1024]{3,2,1,0:T(8,128)} %rhs_ref.1, f32[2,64,2,1024]{3,2,1,0:T(2,128)} %copy-done, f32[2,64,2,1024]{3,2,1,0:T(2,128)} %collective-permute-done.1.bot_ref, f32[16,1024]{1,0:T(8,128)} %pad_maximum_fusion.diff_ref, ...), custom_call_target="tpu_custom_call" | custom-call | flops 209715200 | bytes 8388608 | tf_op jit(solution)/shard_map/pallas_call | solution.py:127
  49.8 5.8 %all-to-all-start = ((f32[8,2,512,128]{3,2,1,0:T(8,128)}), f32[8,2,512,128]{3,2,1,0:T(8,128)}, u32[]{:S(2)}, u32[]{:S(2)}) async-start(f32[8,2,512,128]{3,2,1,0:T(8,128)} %bitcast.8), calls=%async_computation | async-start | bytes 8388608 | tf_op jit(solution)/shard_map/all_to_all | solution.py:238
  55.6 0.7 exponential_multiply_fusion.fac_ref
  56.2 50.0 %all-to-all-done.a_ref = f32[8,2,512,128]{3,2,1,0:T(8,128)} async-done(((f32[8,2,512,128]{3,2,1,0:T(8,128)}), f32[8,2,512,128]{3,2,1,0:T(8,128)}, u32[]{:S(2)}, u32[]{:S(2)}) %all-to-all-start) | async-done | bytes 4194336 | tf_op jit(solution)/shard_map/all_to_all | solution.py:238
  106.3 5.8 %shard_map.29 = f32[8,2,512,128]{3,2,1,0:T(8,128)} custom-call(f32[8,64]{1,0:T(8,128)} %exponential_multiply_fusion.fac_ref, f32[8,2,512,128]{3,2,1,0:T(8,128)} %all-to-all-done.a_ref), custom_call_target="tpu_custom_call" | custom-call | flops 41943040 | bytes 8388608 | tf_op jit(solution)/shard_map/pallas_call | solution.py:170
  112.1 67.9 %all_to_all.10 = f32[8,2,512,128]{3,2,1,0:T(8,128)S(1)} all-to-all(f32[8,2,512,128]{3,2,1,0:T(8,128)} %shard_map.29), channel_id=1, replica_groups=mesh['tm'=8,'space'=16] {'tm'}, dimensions={0} | all-to-all | bytes 8388608 | tf_op jit(solution)/shard_map/all_to_all | solution.py:246
  180.0 2.6 %copy_bitcast_fusion = f32[2,64,8,1024]{3,2,1,0:T(8,128)} fusion(f32[8,2,512,128]{3,2,1,0:T(8,128)S(1)} %all_to_all.10), kind=kLoop, calls=%fused_computation | loop fusion | bytes 8388608 | tf_op jit(solution)/shard_map/reshape | solution.py:248
  (8 shorter events, 0.1 us)
Async XLA Ops:
  0.0 10.2 %copy-start.1 = (f32[8,1024]{1,0:T(8,128)S(1)}, f32[8,1024]{1,0:T(8,128)}, u32[]{:S(2)}) copy-start(f32[8,1024]{1,0:T(8,128)} %param.3) | copy-start | bytes 98308
  4.6 18.7 %collective-permute-start = (f32[2,64,2,1024]{3,2,1,0:T(2,128)S(1)}, f32[2,64,2,1024]{3,2,1,0:T(2,128)S(1)}, u32[]{:S(2)}, u32[]{:S(2)}) collective-permute-start(f32[2,64,2,1024]{3,2,1,0:T(2,128)S(1)} %get-tuple-element.6), channel_id=1, source_target_pairs={{0,1},{1,2},{2,3},{3,4},{4,5},{5,6},{6,7},{7,8},{8,9},{9,10},{10,1... | collective-permute-start | bytes 3145736 | tf_op jit(solution)/shard_map/ppermute | solution.py:44
  6.5 16.7 %collective-permute-start.1 = (f32[2,64,2,1024]{3,2,1,0:T(2,128)S(1)}, f32[2,64,2,1024]{3,2,1,0:T(2,128)}, u32[]{:S(2)}, u32[]{:S(2)}) collective-permute-start(f32[2,64,2,1024]{3,2,1,0:T(2,128)S(1)} %get-tuple-element.5), channel_id=1, source_target_pairs={{1,0},{2,1},{3,2},{4,3},{5,4},{6,5},{7,6},{8,7},{9,8},{10,9},{11,1... | collective-permute-start | bytes 3145736 | tf_op jit(solution)/shard_map/ppermute | solution.py:45
  10.2 12.4 %collective-permute-start.2 = (f32[2,1024]{1,0:T(2,128)S(1)}, f32[2,1024]{1,0:T(2,128)S(1)}, u32[]{:S(2)}, u32[]{:S(2)}) collective-permute-start(f32[2,1024]{1,0:T(2,128)S(1)} %get-tuple-element.7), channel_id=1, source_target_pairs={{1,0},{2,1},{3,2},{4,3},{5,4},{6,5},{7,6},{8,7},{9,8},{10,9},{11,1... | collective-permute-start | bytes 24584 | tf_op jit(solution)/shard_map/ppermute | solution.py:45
  12.2 10.4 %collective-permute-start.3 = (f32[2,1024]{1,0:T(2,128)S(1)}, f32[2,1024]{1,0:T(2,128)S(1)}, u32[]{:S(2)}, u32[]{:S(2)}) collective-permute-start(f32[2,1024]{1,0:T(2,128)S(1)} %get-tuple-element.8), channel_id=1, source_target_pairs={{0,1},{1,2},{2,3},{3,4},{4,5},{5,6},{6,7},{7,8},{8,9},{9,10},{10,1... | collective-permute-start | bytes 24584 | tf_op jit(solution)/shard_map/ppermute | solution.py:44
  23.3 1.0 copy-start
  49.8 56.5 %all-to-all-start = ((f32[8,2,512,128]{3,2,1,0:T(8,128)}), f32[8,2,512,128]{3,2,1,0:T(8,128)}, u32[]{:S(2)}, u32[]{:S(2)}) async-start(f32[8,2,512,128]{3,2,1,0:T(8,128)} %bitcast.8), calls=%async_computation | async-start | bytes 8388608 | tf_op jit(solution)/shard_map/all_to_all | solution.py:238

commit v4 on v3

--- a/solution.py
+++ b/solution.py
@@ -86,8 +86,14 @@
         for order in (1, 2):
             n_re, b_re = around(c_re)
             n_im, b_im = around(c_im)
-            a_re = dr * c_re - lam_i * c_im - diff * b_re - flow_speed * n_re
-            a_im = dr * c_im + lam_i * c_re - diff * b_im - flow_speed * n_im
+            if order == 2:
+                n_re, b_re, n_im, b_im = n_re[0:8], b_re[0:8], n_im[0:8], b_im[0:8]
+                c_re, c_im, r_re, r_im = c_re[0:8], c_im[0:8], r_re[0:8], r_im[0:8]
+                dr, inv_mag, d = dr[0:8], inv_mag[0:8], diff[0:8]
+            else:
+                d = diff
+            a_re = dr * c_re - lam_i * c_im - d * b_re - flow_speed * n_re
+            a_im = dr * c_im + lam_i * c_re - d * b_im - flow_speed * n_im
             s_re = r_re - a_re
             s_im = r_im - a_im
             c_re = c_re + sweep_weights[order] * ((s_re * dr + s_im * lam_i) * inv_mag)

time: 183 us -> 183 us (level)
  no operation moved by 1% of the time
where the time goes in v4:
time: 183 us
  blocking collectives  67.9 us (37%)
  waiting for transfers between devices  56.4 us (31%)
  Pallas kernels  31.2 us (17%)
  starting transfers between devices  15.7 us (9%)
  local copies, waits for them, and re-layouts  8.29 us (5%)
  other arithmetic  2.87 us (2%)
    all_to_all x1, blocking collectives, on_device(): returned = lax.all_to_all(combined, 'tm', 0, 0, tiled=True)  67.9 us
    all_to_all x1, waiting for transfers between devices, on_device(): arrived = lax.all_to_all(outgoing, 'tm', 0, 0, tiled=True)  50 us
    pallas_call x1, Pallas kernels, sweep_call(): pl.pallas_call(sweep_kernel, out_shape=jax.ShapeDtypeStruct((blocks, out_...  25.5 us
    ppermute x2, waiting for transfers between devices, halo_pair(): lax.ppermute(lax.slice_in_dim(block, 0, width, axis=dim), axis, backward)  6.41 us
    all_to_all x1, starting transfers between devices, on_device(): arrived = lax.all_to_all(outgoing, 'tm', 0, 0, tiled=True)  5.82 us
    pallas_call x1, Pallas kernels, combine_call(): pl.pallas_call(functools.partial(combine_kernel, weights), out_shape=jax....  5.78 us
    ppermute x2, starting transfers between devices, halo_pair(): lax.ppermute(lax.slice_in_dim(block, 0, width, axis=dim), axis, backward)  5.56 us
    slice x2, local copies, waits for them, and re-layouts, halo_pair(): lax.slice_in_dim(block, 0, width, axis=dim)  4.61 us
  transfers between devices with their start and end apart: 5, of which 2 were waited for; matrix products, arithmetic and copies ran while one was open for 2% of the time, Pallas kernels for 0%

profile of v4, /device:TPU:4, one launch (start us, length us, event | category | flops | bytes accessed | tf_op | source)
XLA Modules:
  0.0 182.6 jit_solution(5788743585342655710)
XLA Ops:
  0.0 4.6 %fusion.9 = (f32[2,64,2,1024]{3,2,1,0:T(2,128)S(1)}, f32[2,64,2,1024]{3,2,1,0:T(2,128)S(1)}) fusion(f32[2,64,8,1024]{3,2,1,0:T(8,128)} %rhs_ref.1), kind=kLoop, calls=%fused_computation.23 | loop fusion | bytes 4194304 | tf_op jit(solution)/shard_map/slice | solution.py:45
  4.6 1.9 %collective-permute-start = (f32[2,64,2,1024]{3,2,1,0:T(2,128)S(1)}, f32[2,64,2,1024]{3,2,1,0:T(2,128)S(1)}, u32[]{:S(2)}, u32[]{:S(2)}) collective-permute-start(f32[2,64,2,1024]{3,2,1,0:T(2,128)S(1)} %get-tuple-element.6), channel_id=1, source_target_pairs={{0,1},{1,2},{2,3},{3,4},{4,5},{5,6},{6,7},{7,8},{8,9},{9,10},{10,1... | collective-permute-start | bytes 3145736 | tf_op jit(solution)/shard_map/ppermute | solution.py:44
  6.5 3.6 %collective-permute-start.1 = (f32[2,64,2,1024]{3,2,1,0:T(2,128)S(1)}, f32[2,64,2,1024]{3,2,1,0:T(2,128)}, u32[]{:S(2)}, u32[]{:S(2)}) collective-permute-start(f32[2,64,2,1024]{3,2,1,0:T(2,128)S(1)} %get-tuple-element.5), channel_id=1, source_target_pairs={{1,0},{2,1},{3,2},{4,3},{5,4},{6,5},{7,6},{8,7},{9,8},{10,9},{11,1... | collective-permute-start | bytes 3145736 | tf_op jit(solution)/shard_map/ppermute | solution.py:45
  10.2 0.0 copy-done.1
  10.2 1.9 %collective-permute-start.2 = (f32[2,1024]{1,0:T(2,128)S(1)}, f32[2,1024]{1,0:T(2,128)S(1)}, u32[]{:S(2)}, u32[]{:S(2)}) collective-permute-start(f32[2,1024]{1,0:T(2,128)S(1)} %get-tuple-element.7), channel_id=1, source_target_pairs={{1,0},{2,1},{3,2},{4,3},{5,4},{6,5},{7,6},{8,7},{9,8},{10,9},{11,1... | collective-permute-start | bytes 24584 | tf_op jit(solution)/shard_map/ppermute | solution.py:45
  12.2 2.4 %collective-permute-start.3 = (f32[2,1024]{1,0:T(2,128)S(1)}, f32[2,1024]{1,0:T(2,128)S(1)}, u32[]{:S(2)}, u32[]{:S(2)}) collective-permute-start(f32[2,1024]{1,0:T(2,128)S(1)} %get-tuple-element.8), channel_id=1, source_target_pairs={{0,1},{1,2},{2,3},{3,4},{4,5},{5,6},{6,7},{7,8},{8,9},{9,10},{10,1... | collective-permute-start | bytes 24584 | tf_op jit(solution)/shard_map/ppermute | solution.py:44
  14.6 0.6 pad_maximum_fusion.1.lam_ref
  15.2 0.1 fusion.8
  15.4 0.7 maximum_maximum_fusion.table_ref
  16.1 0.1 pad.6.clone
  16.2 6.4 %collective-permute-done.2 = f32[2,1024]{1,0:T(2,128)S(1)} collective-permute-done((f32[2,1024]{1,0:T(2,128)S(1)}, f32[2,1024]{1,0:T(2,128)S(1)}, u32[]{:S(2)}, u32[]{:S(2)}) %collective-permute-start.2) | collective-permute-done | bytes 8224 | tf_op jit(solution)/shard_map/ppermute | solution.py:45
  22.6 0.0 collective-permute-done.3
  22.6 0.7 pad_maximum_fusion.diff_ref
  23.3 0.0 collective-permute-done.top_ref
  23.3 0.0 collective-permute-done.1.bot_ref
  23.3 0.8 broadcast_in_dim.5.mask_ref
  24.1 0.2 copy-done
  24.3 25.5 %shard_map.28 = f32[8,1024,128]{2,1,0:T(8,128)} custom-call(f32[2,64]{1,0:T(2,128)} %pad_maximum_fusion.1.lam_ref, f32[2,64,8,1024]{3,2,1,0:T(8,128)} %rhs_ref.1, f32[2,64,2,1024]{3,2,1,0:T(2,128)} %copy-done, f32[2,64,2,1024]{3,2,1,0:T(2,128)} %collective-permute-done.1.bot_ref, f32[16,1024]{1,0:T(8,128)} %pad_maximum_fusion.diff_ref, ...), custom_call_target="tpu_custom_call" | custom-call | flops 209715200 | bytes 8388608 | tf_op jit(solution)/shard_map/pallas_call | solution.py:133
  49.8 5.8 %all-to-all-start = ((f32[8,2,512,128]{3,2,1,0:T(8,128)}), f32[8,2,512,128]{3,2,1,0:T(8,128)}, u32[]{:S(2)}, u32[]{:S(2)}) async-start(f32[8,2,512,128]{3,2,1,0:T(8,128)} %bitcast.8), calls=%async_computation | async-start | bytes 8388608 | tf_op jit(solution)/shard_map/all_to_all | solution.py:244
  55.6 0.7 exponential_multiply_fusion.fac_ref
  56.2 50.0 %all-to-all-done.a_ref = f32[8,2,512,128]{3,2,1,0:T(8,128)} async-done(((f32[8,2,512,128]{3,2,1,0:T(8,128)}), f32[8,2,512,128]{3,2,1,0:T(8,128)}, u32[]{:S(2)}, u32[]{:S(2)}) %all-to-all-start) | async-done | bytes 4194336 | tf_op jit(solution)/shard_map/all_to_all | solution.py:244
  106.3 5.8 %shard_map.29 = f32[8,2,512,128]{3,2,1,0:T(8,128)} custom-call(f32[8,64]{1,0:T(8,128)} %exponential_multiply_fusion.fac_ref, f32[8,2,512,128]{3,2,1,0:T(8,128)} %all-to-all-done.a_ref), custom_call_target="tpu_custom_call" | custom-call | flops 41943040 | bytes 8388608 | tf_op jit(solution)/shard_map/pallas_call | solution.py:176
  112.1 67.9 %all_to_all.10 = f32[8,2,512,128]{3,2,1,0:T(8,128)S(1)} all-to-all(f32[8,2,512,128]{3,2,1,0:T(8,128)} %shard_map.29), channel_id=1, replica_groups=mesh['tm'=8,'space'=16] {'tm'}, dimensions={0} | all-to-all | bytes 8388608 | tf_op jit(solution)/shard_map/all_to_all | solution.py:252
  180.0 2.6 %copy_bitcast_fusion = f32[2,64,8,1024]{3,2,1,0:T(8,128)} fusion(f32[8,2,512,128]{3,2,1,0:T(8,128)S(1)} %all_to_all.10), kind=kLoop, calls=%fused_computation | loop fusion | bytes 8388608 | tf_op jit(solution)/shard_map/reshape | solution.py:254
  (8 shorter events, 0.1 us)
Async XLA Ops:
  0.0 10.2 %copy-start.1 = (f32[8,1024]{1,0:T(8,128)S(1)}, f32[8,1024]{1,0:T(8,128)}, u32[]{:S(2)}) copy-start(f32[8,1024]{1,0:T(8,128)} %param.3) | copy-start | bytes 98308
  4.6 18.7 %collective-permute-start = (f32[2,64,2,1024]{3,2,1,0:T(2,128)S(1)}, f32[2,64,2,1024]{3,2,1,0:T(2,128)S(1)}, u32[]{:S(2)}, u32[]{:S(2)}) collective-permute-start(f32[2,64,2,1024]{3,2,1,0:T(2,128)S(1)} %get-tuple-element.6), channel_id=1, source_target_pairs={{0,1},{1,2},{2,3},{3,4},{4,5},{5,6},{6,7},{7,8},{8,9},{9,10},{10,1... | collective-permute-start | bytes 3145736 | tf_op jit(solution)/shard_map/ppermute | solution.py:44
  6.5 16.7 %collective-permute-start.1 = (f32[2,64,2,1024]{3,2,1,0:T(2,128)S(1)}, f32[2,64,2,1024]{3,2,1,0:T(2,128)}, u32[]{:S(2)}, u32[]{:S(2)}) collective-permute-start(f32[2,64,2,1024]{3,2,1,0:T(2,128)S(1)} %get-tuple-element.5), channel_id=1, source_target_pairs={{1,0},{2,1},{3,2},{4,3},{5,4},{6,5},{7,6},{8,7},{9,8},{10,9},{11,1... | collective-permute-start | bytes 3145736 | tf_op jit(solution)/shard_map/ppermute | solution.py:45
  10.2 12.4 %collective-permute-start.2 = (f32[2,1024]{1,0:T(2,128)S(1)}, f32[2,1024]{1,0:T(2,128)S(1)}, u32[]{:S(2)}, u32[]{:S(2)}) collective-permute-start(f32[2,1024]{1,0:T(2,128)S(1)} %get-tuple-element.7), channel_id=1, source_target_pairs={{1,0},{2,1},{3,2},{4,3},{5,4},{6,5},{7,6},{8,7},{9,8},{10,9},{11,1... | collective-permute-start | bytes 24584 | tf_op jit(solution)/shard_map/ppermute | solution.py:45
  12.2 10.4 %collective-permute-start.3 = (f32[2,1024]{1,0:T(2,128)S(1)}, f32[2,1024]{1,0:T(2,128)S(1)}, u32[]{:S(2)}, u32[]{:S(2)}) collective-permute-start(f32[2,1024]{1,0:T(2,128)S(1)} %get-tuple-element.8), channel_id=1, source_target_pairs={{0,1},{1,2},{2,3},{3,4},{4,5},{5,6},{6,7},{7,8},{8,9},{9,10},{10,1... | collective-permute-start | bytes 24584 | tf_op jit(solution)/shard_map/ppermute | solution.py:44
  23.3 1.0 copy-start
  49.8 56.5 %all-to-all-start = ((f32[8,2,512,128]{3,2,1,0:T(8,128)}), f32[8,2,512,128]{3,2,1,0:T(8,128)}, u32[]{:S(2)}, u32[]{:S(2)}) async-start(f32[8,2,512,128]{3,2,1,0:T(8,128)} %bitcast.8), calls=%async_computation | async-start | bytes 8388608 | tf_op jit(solution)/shard_map/all_to_all | solution.py:244

commit v5 on v4

--- a/solution.py
+++ b/solution.py
@@ -16,7 +16,7 @@
     1.0 / (1.0 + 0.7 * math.cos(math.pi * (2 * order + 1) / 6.0)) for order in range(3)
 ]
 Q_BLOCK = 16
-F_BLOCK = 4
+F_BLOCK = 16
 HALO = 2
 
 
@@ -200,9 +200,8 @@
     return tuple(rows)
 
 
-def frames(diffusivity, space_place, space_count):
+def frames(diffusivity, d_top, d_bot, space_place, space_count):
     rows, cols = diffusivity.shape
-    d_top, d_bot = halo_pair(diffusivity, "space", 0, HALO)
     gap = jnp.zeros((16 - rows - 2 * HALO, cols), jnp.float32)
     diff_frame = jnp.concatenate([diffusivity, d_bot, gap, d_top], axis=0)
     row = jnp.arange(16, dtype=jnp.int32)
@@ -228,8 +227,9 @@
     freq_ids = index_f * tm_count + residue
     lam = jnp.stack(shift_parts(freq_ids, total_steps))
 
-    top, bottom = halo_pair(spectrum, "space", 2, HALO)
-    diff_frame, mask_frame = frames(diffusivity, space_place, space_count)
+    diff_slot = jnp.broadcast_to(diffusivity[None, None], (2, 1, row_count, col_count))
+    top, bottom = halo_pair(jnp.concatenate([spectrum, diff_slot], axis=1), "space", 2, HALO)
+    diff_frame, mask_frame = frames(diffusivity, top[0, local_count], bottom[0, local_count], space_place, space_count)
     grid_angle = (index_f[:, None] * freq_ids[None, :] % total_steps).astype(jnp.float32) * (
         2.0 * math.pi / total_steps
     )

time: 183 us -> 184 us (level)
  other arithmetic: 2.87 us -> 8.6 us
  waiting for transfers between devices: 56.4 us -> 60.9 us
  starting transfers between devices: 15.7 us -> 11.4 us
  local copies, waits for them, and re-layouts: 8.29 us -> 4.14 us
    ppermute x2 -> x1, waiting for transfers between devices: 0.01 us -> 9.32 us  [halo_pair(): lax.ppermute(lax.slice_in_dim(block, size - width, size, axis=dim), axis,...]
    concatenate x0 -> x1, other arithmetic: none -> 5.6 us  [on_device(): jnp.concatenate([spectrum, diff_slot], axis=1)]
    ppermute x2 -> x1, waiting for transfers between devices: 6.41 us -> 1.54 us  [halo_pair(): lax.ppermute(lax.slice_in_dim(block, 0, width, axis=dim), axis, backward)]
    slice x2 -> x0, local copies, waits for them, and re-layouts: 4.61 us -> none  [halo_pair(): lax.slice_in_dim(block, 0, width, axis=dim)]
    ppermute x2 -> x1, starting transfers between devices: 4.33 us -> 1.91 us  [halo_pair(): lax.ppermute(lax.slice_in_dim(block, size - width, size, axis=dim), axis,...]
    ppermute x2 -> x1, starting transfers between devices: 5.56 us -> 3.64 us  [halo_pair(): lax.ppermute(lax.slice_in_dim(block, 0, width, axis=dim), axis, backward)]
  transfers between devices with their start and end apart: 5 -> 3, of which waited for: 2 -> 3; matrix products, arithmetic and copies ran while one was open for 2% -> 1% of each run, Pallas kernels for 0% -> 0%
where the time goes in v5:
time: 184 us
  blocking collectives  67.9 us (37%)
  waiting for transfers between devices  60.9 us (33%)
  Pallas kernels  30.7 us (17%)
  starting transfers between devices  11.4 us (6%)
  other arithmetic  8.6 us (5%)
  local copies, waits for them, and re-layouts  4.14 us (2%)
    all_to_all x1, blocking collectives, on_device(): returned = lax.all_to_all(combined, 'tm', 0, 0, tiled=True)  67.9 us
    all_to_all x1, waiting for transfers between devices, on_device(): arrived = lax.all_to_all(outgoing, 'tm', 0, 0, tiled=True)  50 us
    pallas_call x1, Pallas kernels, sweep_call(): pl.pallas_call(sweep_kernel, out_shape=jax.ShapeDtypeStruct((blocks, out_...  24.9 us
    ppermute x1, waiting for transfers between devices, halo_pair(): lax.ppermute(lax.slice_in_dim(block, size - width, size, axis=dim), axis,...  9.32 us
    all_to_all x1, starting transfers between devices, on_device(): arrived = lax.all_to_all(outgoing, 'tm', 0, 0, tiled=True)  5.82 us
    pallas_call x1, Pallas kernels, combine_call(): pl.pallas_call(functools.partial(combine_kernel, weights), out_shape=jax....  5.78 us
    concatenate x1, other arithmetic, on_device(): jnp.concatenate([spectrum, diff_slot], axis=1)  5.6 us
  transfers between devices with their start and end apart: 3, of which 3 were waited for; matrix products, arithmetic and copies ran while one was open for 1% of the time, Pallas kernels for 0%

profile of v5, /device:TPU:4, one launch (start us, length us, event | category | flops | bytes accessed | tf_op | source)
XLA Modules:
  0.0 183.7 jit_solution(16394093752156481757)
XLA Ops:
  0.0 0.8 broadcast_in_dim.6
  0.8 0.0 copy-start.2
  0.8 5.6 %pad_maximum_fusion = (f32[2,65,2,1024]{3,2,1,0:T(2,128)S(1)}, f32[2,65,2,1024]{3,2,1,0:T(2,128)}) fusion(f32[2,1,8,1024]{3,2,1,0:T(8,128)S(1)} %broadcast_in_dim.6, f32[2,64,8,1024]{3,2,1,0:T(8,128)} %rhs_ref.1), kind=kLoop, calls=%fused_computation.1 | loop fusion | flops 532480 | bytes 6389760 | tf_op jit(solution)/shard_map/concatenate | solution.py:231
  6.4 1.9 %collective-permute-start = (f32[2,65,2,1024]{3,2,1,0:T(2,128)}, f32[2,65,2,1024]{3,2,1,0:T(2,128)S(1)}, u32[]{:S(2)}, u32[]{:S(2)}) collective-permute-start(f32[2,65,2,1024]{3,2,1,0:T(2,128)} %get-tuple-element.6), channel_id=1, source_target_pairs={{0,1},{1,2},{2,3},{3,4},{4,5},{5,6},{6,7},{7,8},{8,9},{9,10},{10,1... | collective-permute-start | bytes 3194888 | tf_op jit(solution)/shard_map/ppermute | solution.py:44
  8.3 3.6 %collective-permute-start.1 = (f32[2,65,2,1024]{3,2,1,0:T(2,128)S(1)}, f32[2,65,2,1024]{3,2,1,0:T(2,128)S(1)}, u32[]{:S(2)}, u32[]{:S(2)}) collective-permute-start(f32[2,65,2,1024]{3,2,1,0:T(2,128)S(1)} %get-tuple-element.5), channel_id=1, source_target_pairs={{1,0},{2,1},{3,2},{4,3},{5,4},{6,5},{7,6},{8,7},{9,8},{10,9},{11,1... | collective-permute-start | bytes 3194888 | tf_op jit(solution)/shard_map/ppermute | solution.py:45
  12.0 0.1 pad.6.clone
  12.1 0.6 pad_maximum_fusion.3.lam_ref
  12.7 0.1 fusion.8
  12.8 0.7 maximum_maximum_fusion.table_ref
  13.5 9.3 %collective-permute-done.top_ref = f32[2,65,2,1024]{3,2,1,0:T(2,128)S(1)} collective-permute-done((f32[2,65,2,1024]{3,2,1,0:T(2,128)}, f32[2,65,2,1024]{3,2,1,0:T(2,128)S(1)}, u32[]{:S(2)}, u32[]{:S(2)}) %collective-permute-start) | collective-permute-done | bytes 1064992 | tf_op jit(solution)/shard_map/ppermute | solution.py:44
  22.9 0.0 copy-start
  22.9 1.5 collective-permute-done.1.bot_ref
  24.4 0.0 copy-done.2
  24.4 0.8 pad_maximum_fusion.2.diff_ref
  25.2 0.7 broadcast_in_dim.8.mask_ref
  25.9 0.0 copy-done
  25.9 0.0 copy-done.1
  25.9 24.9 %shard_map.28 = f32[8,1024,128]{2,1,0:T(8,128)} custom-call(f32[2,64]{1,0:T(2,128)} %pad_maximum_fusion.3.lam_ref, f32[2,64,8,1024]{3,2,1,0:T(8,128)} %rhs_ref.1, f32[2,65,2,1024]{3,2,1,0:T(2,128)} %copy-done, f32[2,65,2,1024]{3,2,1,0:T(2,128)} %copy-done.1, f32[16,1024]{1,0:T(8,128)} %pad_maximum_fusion.2.diff_ref, f32[16,1024]{1,0:T(8,128)} %broadcast_in_dim.8.mask_ref, ...), custom_call_target="tpu_custom_call" | custom-call | flops 209715200 | bytes 8388608 | tf_op jit(solution)/shard_map/pallas_call | solution.py:133
  50.8 5.8 %all-to-all-start = ((f32[8,2,512,128]{3,2,1,0:T(8,128)}), f32[8,2,512,128]{3,2,1,0:T(8,128)}, u32[]{:S(2)}, u32[]{:S(2)}) async-start(f32[8,2,512,128]{3,2,1,0:T(8,128)} %bitcast.12), calls=%async_computation | async-start | bytes 8388608 | tf_op jit(solution)/shard_map/all_to_all | solution.py:244
  56.7 0.7 exponential_multiply_fusion.fac_ref
  57.3 50.0 %all-to-all-done.a_ref = f32[8,2,512,128]{3,2,1,0:T(8,128)} async-done(((f32[8,2,512,128]{3,2,1,0:T(8,128)}), f32[8,2,512,128]{3,2,1,0:T(8,128)}, u32[]{:S(2)}, u32[]{:S(2)}) %all-to-all-start) | async-done | bytes 4194336 | tf_op jit(solution)/shard_map/all_to_all | solution.py:244
  107.4 5.8 %shard_map.29 = f32[8,2,512,128]{3,2,1,0:T(8,128)} custom-call(f32[8,64]{1,0:T(8,128)} %exponential_multiply_fusion.fac_ref, f32[8,2,512,128]{3,2,1,0:T(8,128)} %all-to-all-done.a_ref), custom_call_target="tpu_custom_call" | custom-call | flops 41943040 | bytes 8388608 | tf_op jit(solution)/shard_map/pallas_call | solution.py:176
  113.2 67.9 %all_to_all.10 = f32[8,2,512,128]{3,2,1,0:T(8,128)S(1)} all-to-all(f32[8,2,512,128]{3,2,1,0:T(8,128)} %shard_map.29), channel_id=1, replica_groups=mesh['tm'=8,'space'=16] {'tm'}, dimensions={0} | all-to-all | bytes 8388608 | tf_op jit(solution)/shard_map/all_to_all | solution.py:252
  181.1 2.6 %copy_bitcast_fusion = f32[2,64,8,1024]{3,2,1,0:T(8,128)} fusion(f32[8,2,512,128]{3,2,1,0:T(8,128)S(1)} %all_to_all.10), kind=kLoop, calls=%fused_computation | loop fusion | bytes 8388608 | tf_op jit(solution)/shard_map/reshape | solution.py:254
  (8 shorter events, 0.1 us)
Async XLA Ops:
  0.8 23.6 %copy-start.2 = (f32[8,1024]{1,0:T(8,128)S(1)}, f32[8,1024]{1,0:T(8,128)}, u32[]{:S(2)}) copy-start(f32[8,1024]{1,0:T(8,128)} %param.3) | copy-start | bytes 98308
  6.4 16.5 %collective-permute-start = (f32[2,65,2,1024]{3,2,1,0:T(2,128)}, f32[2,65,2,1024]{3,2,1,0:T(2,128)S(1)}, u32[]{:S(2)}, u32[]{:S(2)}) collective-permute-start(f32[2,65,2,1024]{3,2,1,0:T(2,128)} %get-tuple-element.6), channel_id=1, source_target_pairs={{0,1},{1,2},{2,3},{3,4},{4,5},{5,6},{6,7},{7,8},{8,9},{9,10},{10,1... | collective-permute-start | bytes 3194888 | tf_op jit(solution)/shard_map/ppermute | solution.py:44
  8.3 16.1 %collective-permute-start.1 = (f32[2,65,2,1024]{3,2,1,0:T(2,128)S(1)}, f32[2,65,2,1024]{3,2,1,0:T(2,128)S(1)}, u32[]{:S(2)}, u32[]{:S(2)}) collective-permute-start(f32[2,65,2,1024]{3,2,1,0:T(2,128)S(1)} %get-tuple-element.5), channel_id=1, source_target_pairs={{1,0},{2,1},{3,2},{4,3},{5,4},{6,5},{7,6},{8,7},{9,8},{10,9},{11,1... | collective-permute-start | bytes 3194888 | tf_op jit(solution)/shard_map/ppermute | solution.py:45
  22.9 3.1 %copy-start = (f32[2,65,2,1024]{3,2,1,0:T(2,128)}, f32[2,65,2,1024]{3,2,1,0:T(2,128)S(1)}, u32[]{:S(2)}) copy-start(f32[2,65,2,1024]{3,2,1,0:T(2,128)S(1)} %collective-permute-done.top_ref) | copy-start | bytes 3194884
  24.4 1.5 copy-start.1
  50.8 56.5 %all-to-all-start = ((f32[8,2,512,128]{3,2,1,0:T(8,128)}), f32[8,2,512,128]{3,2,1,0:T(8,128)}, u32[]{:S(2)}, u32[]{:S(2)}) async-start(f32[8,2,512,128]{3,2,1,0:T(8,128)} %bitcast.12), calls=%async_computation | async-start | bytes 8388608 | tf_op jit(solution)/shard_map/all_to_all | solution.py:244

commit v6 on v3

--- a/solution.py
+++ b/solution.py
@@ -46,7 +46,7 @@
     return top, bottom
 
 
-def sweep_kernel(lam_ref, rhs_ref, top_ref, bot_ref, diff_ref, mask_ref, table_ref, o_ref, field):
+def sweep_kernel(half, lam_ref, rhs_ref, edge_ref, diff_ref, mask_ref, table_ref, o_ref, field):
     block = rhs_ref.shape[1]
     count = lam_ref.shape[1]
     cols = rhs_ref.shape[3]
@@ -54,22 +54,21 @@
     diff = diff_ref[...]
     diag_base = 4.0 * diff + flow_speed
     keep = mask_ref[...]
-    row8 = lax.broadcasted_iota(jnp.int32, (8, cols), 0)
-    col = lax.broadcasted_iota(jnp.int32, (16, cols), 1)
+    row = lax.broadcasted_iota(jnp.int32, (8, cols), 0)
+    col = lax.broadcasted_iota(jnp.int32, (8, cols), 1)
+    first = 6 if half == 0 else 4
 
     def frame(x, f):
         local = rhs_ref[x, f]
-        bv = bot_ref[x, f]
-        tv = top_ref[x, f]
-        hi = jnp.where(row8 == 0, jnp.broadcast_to(bv[0:1], (8, cols)), 0.0)
-        hi = jnp.where(row8 == 1, jnp.broadcast_to(bv[1:2], (8, cols)), hi)
-        hi = jnp.where(row8 == 6, jnp.broadcast_to(tv[0:1], (8, cols)), hi)
-        hi = jnp.where(row8 == 7, jnp.broadcast_to(tv[1:2], (8, cols)), hi)
-        return jnp.concatenate([local, hi], axis=0)
+        if half == 1:
+            local = pltpu.roll(local, 4, 0)
+        ev = edge_ref[x, f]
+        out = jnp.where(row == first, jnp.broadcast_to(ev[0:1], (8, cols)), local)
+        return jnp.where(row == first + 1, jnp.broadcast_to(ev[1:2], (8, cols)), out)
 
     def around(v):
         north = pltpu.roll(v, 1, 0)
-        south = pltpu.roll(v, 15, 0)
+        south = pltpu.roll(v, 7, 0)
         west = jnp.where(col == 0, 0.0, pltpu.roll(v, 1, 1))
         east = jnp.where(col == cols - 1, 0.0, pltpu.roll(v, cols - 1, 1))
         return north, north + south + west + east
@@ -98,8 +97,8 @@
         width = field.shape[2]
         for blk in range(field.shape[0]):
             lanes = slice(blk * width, (blk + 1) * width)
-            field[blk, pl.ds(pl.multiple_of((base + f) * 8, 8), 8), :] = c_re[0:8, lanes]
-            field[blk, pl.ds(pl.multiple_of((count + base + f) * 8, 8), 8), :] = c_im[0:8, lanes]
+            field[blk, pl.ds(pl.multiple_of((base + f) * 4, 4), 4), :] = c_re[0:4, lanes]
+            field[blk, pl.ds(pl.multiple_of((count + base + f) * 4, 4), 4), :] = c_im[0:4, lanes]
         return carry
 
     lax.fori_loop(0, block, body, 0)
@@ -108,39 +107,40 @@
     def _():
         table = table_ref[...]
         for blk in range(o_ref.shape[0]):
-            for r in range(8):
-                plane = field[blk, pl.ds(r, 2 * count, stride=8), :]
-                o_ref[blk, pl.ds(r, 2 * count, stride=8), :] = jnp.dot(
+            for r in range(4):
+                plane = field[blk, pl.ds(r, 2 * count, stride=4), :]
+                o_ref[blk, pl.ds(r, 2 * count, stride=4), :] = jnp.dot(
                     table, plane, precision=lax.Precision.HIGHEST, preferred_element_type=jnp.float32
                 )
 
 
-def sweep_call(lam, spectrum, top, bottom, diff_frame, mask_frame, table, blocks):
+def sweep_call(half, lam, spectrum, edge, diff_frame, mask_frame, table, blocks):
     _, count, rows, cols = spectrum.shape
     block = F_BLOCK
     width = cols // blocks
     big = pl.BlockSpec((2, block, rows, cols), lambda g: (0, g, 0, 0))
-    edge = pl.BlockSpec((2, block, HALO, cols), lambda g: (0, g, 0, 0))
-    whole = pl.BlockSpec((16, cols), lambda g: (0, 0))
+    edges = pl.BlockSpec((2, block, HALO, cols), lambda g: (0, g, 0, 0))
+    whole = pl.BlockSpec((8, cols), lambda g: (0, 0))
     square = pl.BlockSpec((2 * count, 2 * count), lambda g: (0, 0))
-    out_rows = 2 * count * rows
+    out_rows = 2 * count * 4
     return pl.pallas_call(
-        sweep_kernel,
+        functools.partial(sweep_kernel, half),
         out_shape=jax.ShapeDtypeStruct((blocks, out_rows, width), jnp.float32),
         grid=(count // block,),
-        in_specs=[pl.BlockSpec(memory_space=pltpu.SMEM), big, edge, edge, whole, whole, square],
+        in_specs=[pl.BlockSpec(memory_space=pltpu.SMEM), big, edges, whole, whole, square],
         out_specs=pl.BlockSpec((blocks, out_rows, width), lambda g: (0, 0, 0)),
         scratch_shapes=[pltpu.VMEM((blocks, out_rows, width), jnp.float32)],
         compiler_params=pltpu.CompilerParams(dimension_semantics=("arbitrary",)),
         cost_estimate=pl.CostEstimate(
-            flops=200 * spectrum.size, transcendentals=0, bytes_accessed=8 * spectrum.size
+            flops=100 * spectrum.size, transcendentals=0, bytes_accessed=6 * spectrum.size
         ),
-    )(lam, spectrum, top, bottom, diff_frame, mask_frame, table)
+    )(lam, spectrum, edge, diff_frame, mask_frame, table)
 
 
 def combine_kernel(weights, fac_ref, a_ref, o_ref):
     block = a_ref.shape[2] // 8
     base = pl.program_id(0) * block
+    sub = lax.broadcasted_iota(jnp.int32, (8, a_ref.shape[3]), 0)
 
     def body(qi, carry):
         rows = pl.ds(pl.multiple_of(qi * 8, 8), 8)
@@ -156,7 +156,8 @@
                         acc.append(-val)
                     elif coef != 0.0:
                         acc.append(coef * val)
-            scale = fac_ref[m, base + qi]
+            q0 = (base + qi) * 2
+            scale = jnp.where(sub < 4, fac_ref[m, q0], fac_ref[m, q0 + 1])
             o_ref[m, 0, rows, :] = sum(acc_re[1:], acc_re[0]) * scale
             o_ref[m, 1, rows, :] = sum(acc_im[1:], acc_im[0]) * scale
         return carry
@@ -197,14 +198,17 @@
 def frames(diffusivity, space_place, space_count):
     rows, cols = diffusivity.shape
     d_top, d_bot = halo_pair(diffusivity, "space", 0, HALO)
-    gap = jnp.zeros((16 - rows - 2 * HALO, cols), jnp.float32)
-    diff_frame = jnp.concatenate([diffusivity, d_bot, gap, d_top], axis=0)
-    row = jnp.arange(16, dtype=jnp.int32)
-    keep = (row < rows) | ((row == rows) & (space_place < space_count - 1)) | (
-        (row == 15) & (space_place > 0)
-    )
-    mask_frame = jnp.broadcast_to(keep.astype(jnp.float32)[:, None], (16, cols))
-    return diff_frame, mask_frame
+    diff_frames = (
+        jnp.concatenate([diffusivity[0:6], d_top], axis=0),
+        jnp.concatenate([diffusivity[4:8], d_bot, diffusivity[2:4]], axis=0),
+    )
+    row = jnp.arange(8, dtype=jnp.int32)
+    keeps = (
+        (row != 7) | (space_place > 0),
+        (row != 4) | (space_place < space_count - 1),
+    )
+    mask_frames = tuple(jnp.broadcast_to(k.astype(jnp.float32)[:, None], (8, cols)) for k in keeps)
+    return diff_frames, mask_frames
 
 
 def on_device(spectrum, diffusivity):
@@ -223,7 +227,8 @@
     lam = jnp.stack(shift_parts(freq_ids, total_steps))
 
     top, bottom = halo_pair(spectrum, "space", 2, HALO)
-    diff_frame, mask_frame = frames(diffusivity, space_place, space_count)
+    diff_frames, mask_frames = frames(diffusivity, space_place, space_count)
+
     grid_angle = (index_f[:, None] * freq_ids[None, :] % total_steps).astype(jnp.float32) * (
         2.0 * math.pi / total_steps
     )
@@ -232,20 +237,25 @@
     table = jnp.concatenate(
         [jnp.concatenate([cosine, -sine], 1), jnp.concatenate([sine, cosine], 1)], 0
     )
-    outgoing = sweep_call(lam, spectrum, top, bottom, diff_frame, mask_frame, table, tm_count)
     col_block = col_count // tm_count
-    outgoing = outgoing.reshape(tm_count, 2, local_count * row_count, col_block)
-    arrived = lax.all_to_all(outgoing, "tm", 0, 0, tiled=True)
-
     step_ids = (
         jnp.arange(tm_count, dtype=jnp.int32)[:, None] * local_count
         + jnp.arange(local_count, dtype=jnp.int32)[None, :]
     ).astype(jnp.float32)
     factor = jnp.exp(step_ids * (-math.log(alpha_wrap) / total_steps)) / math.sqrt(total_steps)
-    combined = combine_call(class_weights(tm_count, bit_count), factor, arrived, Q_BLOCK)
-    returned = lax.all_to_all(combined, "tm", 0, 0, tiled=True)
-    returned = returned.reshape(tm_count, 2, local_count, row_count, col_block)
-    return jnp.moveaxis(returned, 0, 3).reshape(2, local_count, row_count, col_count)
+    weights = class_weights(tm_count, bit_count)
+
+    arrived = []
+    for half, edge in ((0, top), (1, bottom)):
+        outgoing = sweep_call(half, lam, spectrum, edge, diff_frames[half], mask_frames[half], table, tm_count)
+        outgoing = outgoing.reshape(tm_count, 2, local_count * 4, col_block)
+        arrived.append(lax.all_to_all(outgoing, "tm", 0, 0, tiled=True))
+    returned = []
+    for piece in arrived:
+        combined = combine_call(weights, factor, piece, Q_BLOCK)
+        returned.append(lax.all_to_all(combined, "tm", 0, 0, tiled=True).reshape(tm_count, 2, local_count, 4, col_block))
+    joined = jnp.concatenate(returned, axis=3)
+    return jnp.moveaxis(joined, 0, 3).reshape(2, local_count, row_count, col_count)
 
 
 def solution(mesh):

time: 183 us -> 196 us (1.071)
  blocking collectives: 67.9 us -> 34.2 us
  Pallas kernels: 31.2 us -> 49.5 us
  starting transfers between devices: 15.7 us -> 29.8 us
  waiting for transfers between devices: 56.4 us -> 67.4 us
  other arithmetic: 2.87 us -> 6.25 us
    all_to_all x1, blocking collectives: 67.9 us -> 34.2 us  [on_device(): lax.all_to_all(combined, 'tm', 0, 0, tiled=True)]
    pallas_call x1 -> x2, Pallas kernels: 25.5 us -> 42.7 us  [sweep_call(): pl.pallas_call(functools.partial(sweep_kernel, half), out_shape=jax.Shape...]
    all_to_all x1 -> x3, starting transfers between devices: 5.82 us -> 20.2 us  [the longest x2 11.5 us: on_device(): arrived.append(lax.all_to_all(outgoing, 'tm', 0, 0, tiled=True))]
    ppermute x2, waiting for transfers between devices: 0.01 us -> 9.55 us  [halo_pair(): lax.ppermute(lax.slice_in_dim(block, size - width, size, axis=dim), axis,...]
    ppermute x2, waiting for transfers between devices: 6.41 us -> 9.8 us  [halo_pair(): lax.ppermute(lax.slice_in_dim(block, 0, width, axis=dim), axis, backward)]
    reshape x0 -> x1, other arithmetic: none -> 2.86 us  [on_device(): jnp.moveaxis(joined, 0, 3).reshape(2, local_count, row_count, col_count)]
    reshape x1 -> x0, local copies, waits for them, and re-layouts: 2.6 us -> none  [on_device(): jnp.moveaxis(returned, 0, 3).reshape(2, local_count, row_count, col_count)]
    all_to_all x1 -> x3, waiting for transfers between devices: 50 us -> 48.1 us  [the longest x1 24.1 us: on_device(): lax.all_to_all(combined, 'tm', 0, 0, tiled=True)]
  transfers between devices with their start and end apart: 5 -> 7, of which waited for: 2 -> 4; matrix products, arithmetic and copies ran while one was open for 2% -> 2% of each run, Pallas kernels for 0% -> 14%
where the time goes in v6:
time: 196 us; the launch traced here: 195 us
  waiting for transfers between devices  67.4 us (34%)
  Pallas kernels  49.5 us (25%)
  blocking collectives  34.2 us (17%)
  starting transfers between devices  29.8 us (15%)
  local copies, waits for them, and re-layouts  7.61 us (4%)
  other arithmetic  6.25 us (3%)
    pallas_call x2, Pallas kernels, sweep_call(): pl.pallas_call(functools.partial(sweep_kernel, half), out_shape=jax.Shape...  42.7 us
    all_to_all x1, blocking collectives, on_device(): lax.all_to_all(combined, 'tm', 0, 0, tiled=True)  34.2 us
    all_to_all x1, waiting for transfers between devices, on_device(): lax.all_to_all(combined, 'tm', 0, 0, tiled=True)  24.1 us
    all_to_all x2, waiting for transfers between devices, on_device(): arrived.append(lax.all_to_all(outgoing, 'tm', 0, 0, tiled=True))  24 us
    all_to_all x2, starting transfers between devices, on_device(): arrived.append(lax.all_to_all(outgoing, 'tm', 0, 0, tiled=True))  11.5 us
    ppermute x2, waiting for transfers between devices, halo_pair(): lax.ppermute(lax.slice_in_dim(block, 0, width, axis=dim), axis, backward)  9.8 us
    ppermute x2, waiting for transfers between devices, halo_pair(): lax.ppermute(lax.slice_in_dim(block, size - width, size, axis=dim), axis,...  9.55 us
    all_to_all x1, starting transfers between devices, on_device(): lax.all_to_all(combined, 'tm', 0, 0, tiled=True)  8.69 us
  transfers between devices with their start and end apart: 7, of which 4 were waited for; matrix products, arithmetic and copies ran while one was open for 2% of the time, Pallas kernels for 14%

profile of v6, /device:TPU:4, one launch (start us, length us, event | category | flops | bytes accessed | tf_op | source)
XLA Modules:
  0.0 194.9 jit_solution(10266620660088971439)
XLA Ops:
  0.0 4.6 %fusion.9 = (f32[2,64,2,1024]{3,2,1,0:T(2,128)S(1)}, f32[2,64,2,1024]{3,2,1,0:T(2,128)S(1)}) fusion(f32[2,64,8,1024]{3,2,1,0:T(8,128)} %rhs_ref.3), kind=kLoop, calls=%fused_computation.26 | loop fusion | bytes 4194304 | tf_op jit(solution)/shard_map/slice | solution.py:44
  4.6 1.9 collective-permute-start
  6.6 3.2 %collective-permute-start.1 = (f32[2,1024]{1,0:T(2,128)S(1)}, f32[2,1024]{1,0:T(2,128)S(1)}, u32[]{:S(2)}, u32[]{:S(2)}) collective-permute-start(f32[2,1024]{1,0:T(2,128)S(1)} %get-tuple-element.7), channel_id=1, source_target_pairs={{0,1},{1,2},{2,3},{3,4},{4,5},{5,6},{6,7},{7,8},{8,9},{9,10},{10,1... | collective-permute-start | bytes 24584 | tf_op jit(solution)/shard_map/ppermute | solution.py:44
  10.5 0.7 maximum_maximum_fusion.table_ref
  11.3 9.5 %collective-permute-done.1 = f32[2,1024]{1,0:T(2,128)S(1)} collective-permute-done((f32[2,1024]{1,0:T(2,128)S(1)}, f32[2,1024]{1,0:T(2,128)S(1)}, u32[]{:S(2)}, u32[]{:S(2)}) %collective-permute-start.1) | collective-permute-done | bytes 8224 | tf_op jit(solution)/shard_map/ppermute | solution.py:44
  21.4 0.8 broadcast_in_dim.4.mask_ref
  22.4 21.4 %shard_map.28 = f32[8,512,128]{2,1,0:T(8,128)} custom-call(f32[2,64]{1,0:T(2,128)} %pad_maximum_fusion.2.lam_ref, f32[2,64,8,1024]{3,2,1,0:T(8,128)} %rhs_ref.3, f32[2,64,2,1024]{3,2,1,0:T(2,128)} %copy-done.1, f32[8,1024]{1,0:T(8,128)} %pad_maximum_fusion.diff_ref, f32[8,1024]{1,0:T(8,128)} %broadcast_in_dim.4.mask_ref, ...), custom_call_target="tpu_custom_call" | custom-call | flops 104857600 | bytes 6291456 | tf_op jit(solution)/shard_map/pallas_call | solution.py:126
  43.8 5.8 %all-to-all-start = ((f32[8,2,256,128]{3,2,1,0:T(8,128)}), f32[8,2,256,128]{3,2,1,0:T(8,128)S(1)}, u32[]{:S(2)}, u32[]{:S(2)}) async-start(f32[8,2,256,128]{3,2,1,0:T(8,128)} %bitcast.10), calls=%async_computation | async-start | bytes 4194304 | tf_op jit(solution)/shard_map/all_to_all | solution.py:252
  49.6 1.9 collective-permute-start.2
  51.5 2.5 %collective-permute-start.3 = (f32[2,1024]{1,0:T(2,128)S(1)}, f32[2,1024]{1,0:T(2,128)S(1)}, u32[]{:S(2)}, u32[]{:S(2)}) collective-permute-start(f32[2,1024]{1,0:T(2,128)S(1)} %get-tuple-element.9), channel_id=1, source_target_pairs={{1,0},{2,1},{3,2},{4,3},{5,4},{6,5},{7,6},{8,7},{9,8},{10,9},{11,1... | collective-permute-start | bytes 24584 | tf_op jit(solution)/shard_map/ppermute | solution.py:45
  54.1 9.8 %collective-permute-done.3 = f32[2,1024]{1,0:T(2,128)S(1)} collective-permute-done((f32[2,1024]{1,0:T(2,128)S(1)}, f32[2,1024]{1,0:T(2,128)S(1)}, u32[]{:S(2)}, u32[]{:S(2)}) %collective-permute-start.3) | collective-permute-done | bytes 8224 | tf_op jit(solution)/shard_map/ppermute | solution.py:45
  63.9 0.6 pad_maximum_fusion.1.diff_ref
  64.5 0.7 broadcast_in_dim.5.mask_ref
  65.2 21.4 %shard_map.30 = f32[8,512,128]{2,1,0:T(8,128)} custom-call(f32[2,64]{1,0:T(2,128)} %pad_maximum_fusion.2.lam_ref, f32[2,64,8,1024]{3,2,1,0:T(8,128)} %rhs_ref.3, f32[2,64,2,1024]{3,2,1,0:T(2,128)} %collective-permute-done.2.edge_ref, f32[8,1024]{1,0:T(8,128)} %pad_maximum_fusion.1.diff_ref, f32[8,1024]{1,0:T(8,128)} %broadcast_in_dim.5.mask_ref, ...), custom_call_target="tpu_custom_call" | custom-call | flops 104857600 | bytes 6291456 | tf_op jit(solution)/shard_map/pallas_call | solution.py:126
  86.6 1.3 copy-done
  87.9 5.7 %all-to-all-start.2 = ((f32[8,2,256,128]{3,2,1,0:T(8,128)}), f32[8,2,256,128]{3,2,1,0:T(8,128)}, u32[]{:S(2)}, u32[]{:S(2)}) async-start(f32[8,2,256,128]{3,2,1,0:T(8,128)} %bitcast.11), calls=%async_computation.2 | async-start | bytes 4194304 | tf_op jit(solution)/shard_map/all_to_all | solution.py:252
  93.6 0.7 exponential_multiply_fusion.fac_ref
  94.3 3.4 %shard_map.29 = f32[8,2,256,128]{3,2,1,0:T(8,128)} custom-call(f32[8,64]{1,0:T(8,128)} %exponential_multiply_fusion.fac_ref, f32[8,2,256,128]{3,2,1,0:T(8,128)} %copy-done), custom_call_target="tpu_custom_call" | custom-call | flops 20971520 | bytes 4194304 | tf_op jit(solution)/shard_map/pallas_call | solution.py:171
  97.7 24.0 %all-to-all-done.2.a_ref = f32[8,2,256,128]{3,2,1,0:T(8,128)} async-done(((f32[8,2,256,128]{3,2,1,0:T(8,128)}), f32[8,2,256,128]{3,2,1,0:T(8,128)}, u32[]{:S(2)}, u32[]{:S(2)}) %all-to-all-start.2) | async-done | bytes 2097184 | tf_op jit(solution)/shard_map/all_to_all | solution.py:252
  121.7 8.7 %all-to-all-start.1 = ((f32[8,2,256,128]{3,2,1,0:T(8,128)}), f32[8,2,256,128]{3,2,1,0:T(8,128)S(1)}, u32[]{:S(2)}, u32[]{:S(2)}) async-start(f32[8,2,256,128]{3,2,1,0:T(8,128)} %shard_map.29), calls=%async_computation.1 | async-start | bytes 4194304 | tf_op jit(solution)/shard_map/all_to_all | solution.py:256
  130.4 3.3 %shard_map.31 = f32[8,2,256,128]{3,2,1,0:T(8,128)} custom-call(f32[8,64]{1,0:T(8,128)} %exponential_multiply_fusion.fac_ref, f32[8,2,256,128]{3,2,1,0:T(8,128)} %all-to-all-done.2.a_ref), custom_call_target="tpu_custom_call" | custom-call | flops 20971520 | bytes 4194304 | tf_op jit(solution)/shard_map/pallas_call | solution.py:171
  133.7 24.1 %all-to-all-done.1 = f32[8,2,256,128]{3,2,1,0:T(8,128)S(1)} async-done(((f32[8,2,256,128]{3,2,1,0:T(8,128)}), f32[8,2,256,128]{3,2,1,0:T(8,128)S(1)}, u32[]{:S(2)}, u32[]{:S(2)}) %all-to-all-start.1) | async-done | bytes 2097184 | tf_op jit(solution)/shard_map/all_to_all | solution.py:256
  157.8 34.2 %all_to_all.20 = f32[8,2,256,128]{3,2,1,0:T(8,128)S(1)} all-to-all(f32[8,2,256,128]{3,2,1,0:T(8,128)} %shard_map.31), channel_id=1, replica_groups=mesh['tm'=8,'space'=16] {'tm'}, dimensions={0} | all-to-all | bytes 4194304 | tf_op jit(solution)/shard_map/all_to_all | solution.py:256
  192.1 2.9 %copy_bitcast_fusion = f32[2,64,8,1024]{3,2,1,0:T(8,128)} fusion(f32[8,2,64,4,128]{4,3,2,1,0:T(4,128)S(1)} %bitcast.13, f32[8,2,64,4,128]{4,3,2,1,0:T(4,128)S(1)} %bitcast.12), kind=kLoop, calls=%fused_computation.1 | loop fusion | flops 1048576 | bytes 8388608 | tf_op jit(solution)/shard_map/reshape | solution.py:258
  (18 shorter events, 1.6 us)
Async XLA Ops:
  0.0 6.5 %copy-start.2 = (f32[8,1024]{1,0:T(8,128)S(1)}, f32[8,1024]{1,0:T(8,128)}, u32[]{:S(2)}) copy-start(f32[8,1024]{1,0:T(8,128)} %param.3) | copy-start | bytes 98308
  4.6 16.8 %collective-permute-start = (f32[2,64,2,1024]{3,2,1,0:T(2,128)S(1)}, f32[2,64,2,1024]{3,2,1,0:T(2,128)S(1)}, u32[]{:S(2)}, u32[]{:S(2)}) collective-permute-start(f32[2,64,2,1024]{3,2,1,0:T(2,128)S(1)} %get-tuple-element.5), channel_id=1, source_target_pairs={{0,1},{1,2},{2,3},{3,4},{4,5},{5,6},{6,7},{7,8},{8,9},{9,10},{10,1... | collective-permute-start | bytes 3145736 | tf_op jit(solution)/shard_map/ppermute | solution.py:44
  6.6 14.2 %collective-permute-start.1 = (f32[2,1024]{1,0:T(2,128)S(1)}, f32[2,1024]{1,0:T(2,128)S(1)}, u32[]{:S(2)}, u32[]{:S(2)}) collective-permute-start(f32[2,1024]{1,0:T(2,128)S(1)} %get-tuple-element.7), channel_id=1, source_target_pairs={{0,1},{1,2},{2,3},{3,4},{4,5},{5,6},{6,7},{7,8},{8,9},{9,10},{10,1... | collective-permute-start | bytes 24584 | tf_op jit(solution)/shard_map/ppermute | solution.py:44
  21.4 1.0 copy-start.1
  43.8 42.8 %all-to-all-start = ((f32[8,2,256,128]{3,2,1,0:T(8,128)}), f32[8,2,256,128]{3,2,1,0:T(8,128)S(1)}, u32[]{:S(2)}, u32[]{:S(2)}) async-start(f32[8,2,256,128]{3,2,1,0:T(8,128)} %bitcast.10), calls=%async_computation | async-start | bytes 4194304 | tf_op jit(solution)/shard_map/all_to_all | solution.py:252
  49.6 14.9 %collective-permute-start.2 = (f32[2,64,2,1024]{3,2,1,0:T(2,128)S(1)}, f32[2,64,2,1024]{3,2,1,0:T(2,128)}, u32[]{:S(2)}, u32[]{:S(2)}) collective-permute-start(f32[2,64,2,1024]{3,2,1,0:T(2,128)S(1)} %get-tuple-element.6), channel_id=1, source_target_pairs={{1,0},{2,1},{3,2},{4,3},{5,4},{6,5},{7,6},{8,7},{9,8},{10,9},{11,1... | collective-permute-start | bytes 3145736 | tf_op jit(solution)/shard_map/ppermute | solution.py:45
  51.5 12.4 %collective-permute-start.3 = (f32[2,1024]{1,0:T(2,128)S(1)}, f32[2,1024]{1,0:T(2,128)S(1)}, u32[]{:S(2)}, u32[]{:S(2)}) collective-permute-start(f32[2,1024]{1,0:T(2,128)S(1)} %get-tuple-element.9), channel_id=1, source_target_pairs={{1,0},{2,1},{3,2},{4,3},{5,4},{6,5},{7,6},{8,7},{9,8},{10,9},{11,1... | collective-permute-start | bytes 24584 | tf_op jit(solution)/shard_map/ppermute | solution.py:45
  86.6 1.3 copy-start
  87.9 33.8 %all-to-all-start.2 = ((f32[8,2,256,128]{3,2,1,0:T(8,128)}), f32[8,2,256,128]{3,2,1,0:T(8,128)}, u32[]{:S(2)}, u32[]{:S(2)}) async-start(f32[8,2,256,128]{3,2,1,0:T(8,128)} %bitcast.11), calls=%async_computation.2 | async-start | bytes 4194304 | tf_op jit(solution)/shard_map/all_to_all | solution.py:252
  121.7 36.1 %all-to-all-start.1 = ((f32[8,2,256,128]{3,2,1,0:T(8,128)}), f32[8,2,256,128]{3,2,1,0:T(8,128)S(1)}, u32[]{:S(2)}, u32[]{:S(2)}) async-start(f32[8,2,256,128]{3,2,1,0:T(8,128)} %shard_map.29), calls=%async_computation.1 | async-start | bytes 4194304 | tf_op jit(solution)/shard_map/all_to_all | solution.py:256

commit v7 on v5

--- a/solution.py
+++ b/solution.py
@@ -17,6 +17,7 @@
 ]
 Q_BLOCK = 16
 F_BLOCK = 16
+SWEEP_UNROLL = 2
 HALO = 2
 
 
@@ -108,7 +109,7 @@
             field[blk, pl.ds(pl.multiple_of((count + base + f) * 8, 8), 8), :] = c_im[0:8, lanes]
         return carry
 
-    lax.fori_loop(0, block, body, 0)
+    lax.fori_loop(0, block, body, 0, unroll=SWEEP_UNROLL)
 
     @pl.when(pl.program_id(0) == pl.num_programs(0) - 1)
     def _():
@@ -167,7 +168,7 @@
             o_ref[m, 1, rows, :] = sum(acc_im[1:], acc_im[0]) * scale
         return carry
 
-    lax.fori_loop(0, block, body, 0)
+    lax.fori_loop(0, block, body, 0, unroll=SWEEP_UNROLL)
 
 
 def combine_call(weights, factor, arrived, q_block):

time: 184 us -> 182 us (0.989)
  Pallas kernels: 30.7 us -> 28.8 us
where the time goes in v7:
time: 182 us
  blocking collectives  67.9 us (37%)
  waiting for transfers between devices  60.9 us (33%)
  Pallas kernels  28.8 us (16%)
  starting transfers between devices  11.4 us (6%)
  other arithmetic  8.6 us (5%)
  local copies, waits for them, and re-layouts  4.14 us (2%)
    all_to_all x1, blocking collectives, on_device(): returned = lax.all_to_all(combined, 'tm', 0, 0, tiled=True)  67.9 us
    all_to_all x1, waiting for transfers between devices, on_device(): arrived = lax.all_to_all(outgoing, 'tm', 0, 0, tiled=True)  50 us
    pallas_call x1, Pallas kernels, sweep_call(): pl.pallas_call(sweep_kernel, out_shape=jax.ShapeDtypeStruct((blocks, out_...  23.2 us
    ppermute x1, waiting for transfers between devices, halo_pair(): lax.ppermute(lax.slice_in_dim(block, size - width, size, axis=dim), axis,...  9.32 us
    all_to_all x1, starting transfers between devices, on_device(): arrived = lax.all_to_all(outgoing, 'tm', 0, 0, tiled=True)  5.84 us
    concatenate x1, other arithmetic, on_device(): jnp.concatenate([spectrum, diff_slot], axis=1)  5.6 us
    pallas_call x1, Pallas kernels, combine_call(): pl.pallas_call(functools.partial(combine_kernel, weights), out_shape=jax....  5.56 us
    ppermute x1, starting transfers between devices, halo_pair(): lax.ppermute(lax.slice_in_dim(block, 0, width, axis=dim), axis, backward)  3.64 us
  transfers between devices with their start and end apart: 3, of which 3 were waited for; matrix products, arithmetic and copies ran while one was open for 1% of the time, Pallas kernels for 0%

profile of v7, /device:TPU:4, one launch (start us, length us, event | category | flops | bytes accessed | tf_op | source)
XLA Modules:
  0.0 181.8 jit_solution(7519265158155913929)
XLA Ops:
  0.0 0.8 broadcast_in_dim.6
  0.8 0.0 copy-start.2
  0.8 5.6 %pad_maximum_fusion = (f32[2,65,2,1024]{3,2,1,0:T(2,128)S(1)}, f32[2,65,2,1024]{3,2,1,0:T(2,128)}) fusion(f32[2,1,8,1024]{3,2,1,0:T(8,128)S(1)} %broadcast_in_dim.6, f32[2,64,8,1024]{3,2,1,0:T(8,128)} %rhs_ref.1), kind=kLoop, calls=%fused_computation.1 | loop fusion | flops 532480 | bytes 6389760 | tf_op jit(solution)/shard_map/concatenate | solution.py:232
  6.4 1.9 %collective-permute-start = (f32[2,65,2,1024]{3,2,1,0:T(2,128)}, f32[2,65,2,1024]{3,2,1,0:T(2,128)S(1)}, u32[]{:S(2)}, u32[]{:S(2)}) collective-permute-start(f32[2,65,2,1024]{3,2,1,0:T(2,128)} %get-tuple-element.6), channel_id=1, source_target_pairs={{0,1},{1,2},{2,3},{3,4},{4,5},{5,6},{6,7},{7,8},{8,9},{9,10},{10,1... | collective-permute-start | bytes 3194888 | tf_op jit(solution)/shard_map/ppermute | solution.py:45
  8.3 3.6 %collective-permute-start.1 = (f32[2,65,2,1024]{3,2,1,0:T(2,128)S(1)}, f32[2,65,2,1024]{3,2,1,0:T(2,128)S(1)}, u32[]{:S(2)}, u32[]{:S(2)}) collective-permute-start(f32[2,65,2,1024]{3,2,1,0:T(2,128)S(1)} %get-tuple-element.5), channel_id=1, source_target_pairs={{1,0},{2,1},{3,2},{4,3},{5,4},{6,5},{7,6},{8,7},{9,8},{10,9},{11,1... | collective-permute-start | bytes 3194888 | tf_op jit(solution)/shard_map/ppermute | solution.py:46
  12.0 0.1 pad.6.clone
  12.1 0.6 pad_maximum_fusion.3.lam_ref
  12.7 0.1 fusion.8
  12.8 0.7 maximum_maximum_fusion.table_ref
  13.5 9.3 %collective-permute-done.top_ref = f32[2,65,2,1024]{3,2,1,0:T(2,128)S(1)} collective-permute-done((f32[2,65,2,1024]{3,2,1,0:T(2,128)}, f32[2,65,2,1024]{3,2,1,0:T(2,128)S(1)}, u32[]{:S(2)}, u32[]{:S(2)}) %collective-permute-start) | collective-permute-done | bytes 1064992 | tf_op jit(solution)/shard_map/ppermute | solution.py:45
  22.9 0.0 copy-start
  22.9 1.5 collective-permute-done.1.bot_ref
  24.4 0.0 copy-done.2
  24.4 0.8 pad_maximum_fusion.2.diff_ref
  25.2 0.7 broadcast_in_dim.8.mask_ref
  25.9 0.0 copy-done
  25.9 0.0 copy-done.1
  25.9 23.2 %shard_map.28 = f32[8,1024,128]{2,1,0:T(8,128)} custom-call(f32[2,64]{1,0:T(2,128)} %pad_maximum_fusion.3.lam_ref, f32[2,64,8,1024]{3,2,1,0:T(8,128)} %rhs_ref.1, f32[2,65,2,1024]{3,2,1,0:T(2,128)} %copy-done, f32[2,65,2,1024]{3,2,1,0:T(2,128)} %copy-done.1, f32[16,1024]{1,0:T(8,128)} %pad_maximum_fusion.2.diff_ref, f32[16,1024]{1,0:T(8,128)} %broadcast_in_dim.8.mask_ref, ...), custom_call_target="tpu_custom_call" | custom-call | flops 209715200 | bytes 8388608 | tf_op jit(solution)/shard_map/pallas_call | solution.py:134
  49.2 5.8 %all-to-all-start = ((f32[8,2,512,128]{3,2,1,0:T(8,128)}), f32[8,2,512,128]{3,2,1,0:T(8,128)}, u32[]{:S(2)}, u32[]{:S(2)}) async-start(f32[8,2,512,128]{3,2,1,0:T(8,128)} %bitcast.12), calls=%async_computation | async-start | bytes 8388608 | tf_op jit(solution)/shard_map/all_to_all | solution.py:245
  55.0 0.7 exponential_multiply_fusion.fac_ref
  55.7 50.0 %all-to-all-done.a_ref = f32[8,2,512,128]{3,2,1,0:T(8,128)} async-done(((f32[8,2,512,128]{3,2,1,0:T(8,128)}), f32[8,2,512,128]{3,2,1,0:T(8,128)}, u32[]{:S(2)}, u32[]{:S(2)}) %all-to-all-start) | async-done | bytes 4194336 | tf_op jit(solution)/shard_map/all_to_all | solution.py:245
  105.7 5.6 %shard_map.29 = f32[8,2,512,128]{3,2,1,0:T(8,128)} custom-call(f32[8,64]{1,0:T(8,128)} %exponential_multiply_fusion.fac_ref, f32[8,2,512,128]{3,2,1,0:T(8,128)} %all-to-all-done.a_ref), custom_call_target="tpu_custom_call" | custom-call | flops 41943040 | bytes 8388608 | tf_op jit(solution)/shard_map/pallas_call | solution.py:177
  111.3 67.9 %all_to_all.10 = f32[8,2,512,128]{3,2,1,0:T(8,128)S(1)} all-to-all(f32[8,2,512,128]{3,2,1,0:T(8,128)} %shard_map.29), channel_id=1, replica_groups=mesh['tm'=8,'space'=16] {'tm'}, dimensions={0} | all-to-all | bytes 8388608 | tf_op jit(solution)/shard_map/all_to_all | solution.py:253
  179.2 2.6 %copy_bitcast_fusion = f32[2,64,8,1024]{3,2,1,0:T(8,128)} fusion(f32[8,2,512,128]{3,2,1,0:T(8,128)S(1)} %all_to_all.10), kind=kLoop, calls=%fused_computation | loop fusion | bytes 8388608 | tf_op jit(solution)/shard_map/reshape | solution.py:255
  (8 shorter events, 0.1 us)
Async XLA Ops:
  0.8 23.6 %copy-start.2 = (f32[8,1024]{1,0:T(8,128)S(1)}, f32[8,1024]{1,0:T(8,128)}, u32[]{:S(2)}) copy-start(f32[8,1024]{1,0:T(8,128)} %param.3) | copy-start | bytes 98308
  6.4 16.5 %collective-permute-start = (f32[2,65,2,1024]{3,2,1,0:T(2,128)}, f32[2,65,2,1024]{3,2,1,0:T(2,128)S(1)}, u32[]{:S(2)}, u32[]{:S(2)}) collective-permute-start(f32[2,65,2,1024]{3,2,1,0:T(2,128)} %get-tuple-element.6), channel_id=1, source_target_pairs={{0,1},{1,2},{2,3},{3,4},{4,5},{5,6},{6,7},{7,8},{8,9},{9,10},{10,1... | collective-permute-start | bytes 3194888 | tf_op jit(solution)/shard_map/ppermute | solution.py:45
  8.3 16.1 %collective-permute-start.1 = (f32[2,65,2,1024]{3,2,1,0:T(2,128)S(1)}, f32[2,65,2,1024]{3,2,1,0:T(2,128)S(1)}, u32[]{:S(2)}, u32[]{:S(2)}) collective-permute-start(f32[2,65,2,1024]{3,2,1,0:T(2,128)S(1)} %get-tuple-element.5), channel_id=1, source_target_pairs={{1,0},{2,1},{3,2},{4,3},{5,4},{6,5},{7,6},{8,7},{9,8},{10,9},{11,1... | collective-permute-start | bytes 3194888 | tf_op jit(solution)/shard_map/ppermute | solution.py:46
  22.9 3.1 %copy-start = (f32[2,65,2,1024]{3,2,1,0:T(2,128)}, f32[2,65,2,1024]{3,2,1,0:T(2,128)S(1)}, u32[]{:S(2)}) copy-start(f32[2,65,2,1024]{3,2,1,0:T(2,128)S(1)} %collective-permute-done.top_ref) | copy-start | bytes 3194884
  24.4 1.5 copy-start.1
  49.2 56.5 %all-to-all-start = ((f32[8,2,512,128]{3,2,1,0:T(8,128)}), f32[8,2,512,128]{3,2,1,0:T(8,128)}, u32[]{:S(2)}, u32[]{:S(2)}) async-start(f32[8,2,512,128]{3,2,1,0:T(8,128)} %bitcast.12), calls=%async_computation | async-start | bytes 8388608 | tf_op jit(solution)/shard_map/all_to_all | solution.py:245

commit v8 on v7

--- a/solution.py
+++ b/solution.py
@@ -148,24 +148,36 @@
 def combine_kernel(weights, fac_ref, a_ref, o_ref):
     block = a_ref.shape[2] // 8
     base = pl.program_id(0) * block
+    half = float(np.float32(1.0 / math.sqrt(2.0)))
+
+    def turn(p, eighths):
+        re, im = p
+        if eighths == 0:
+            return p
+        if eighths == 2:
+            return -im, re
+        if eighths == 1:
+            return half * (re - im), half * (re + im)
+        return -half * (re + im), half * (re - im)
 
     def body(qi, carry):
         rows = pl.ds(pl.multiple_of(qi * 8, 8), 8)
-        parts = [(a_ref[s, 0, rows, :], a_ref[s, 1, rows, :]) for s in range(a_ref.shape[0])]
-        for m, row in enumerate(weights):
-            acc_re = []
-            acc_im = []
-            for (c, s), (x_re, x_im) in zip(row, parts):
-                for coef, val, acc in ((c, x_re, acc_re), (-s, x_im, acc_re), (s, x_re, acc_im), (c, x_im, acc_im)):
-                    if coef == 1.0:
-                        acc.append(val)
-                    elif coef == -1.0:
-                        acc.append(-val)
-                    elif coef != 0.0:
-                        acc.append(coef * val)
+        x = [(a_ref[s, 0, rows, :], a_ref[s, 1, rows, :]) for s in range(a_ref.shape[0])]
+        span = 1
+        while span < len(x):
+            y = list(x)
+            for start in range(0, len(x), 2 * span):
+                for j in range(span):
+                    u = x[start + j]
+                    v = turn(x[start + j + span], j * len(x) // (2 * span))
+                    y[start + j] = (u[0] + v[0], u[1] + v[1])
+                    y[start + j + span] = (u[0] - v[0], u[1] - v[1])
+            x = y
+            span *= 2
+        for m, (re, im) in enumerate(x):
             scale = fac_ref[m, base + qi]
-            o_ref[m, 0, rows, :] = sum(acc_re[1:], acc_re[0]) * scale
-            o_ref[m, 1, rows, :] = sum(acc_im[1:], acc_im[0]) * scale
+            o_ref[m, 0, rows, :] = re * scale
+            o_ref[m, 1, rows, :] = im * scale
         return carry
 
     lax.fori_loop(0, block, body, 0, unroll=SWEEP_UNROLL)

time: 182 us -> 182 us (level)
  no operation moved by 1% of the time
where the time goes in v8:
time: 182 us; the launch traced here: 181 us
  blocking collectives  67.9 us (37%)
  waiting for transfers between devices  60.9 us (33%)
  Pallas kernels  28.3 us (16%)
  starting transfers between devices  11.4 us (6%)
  other arithmetic  8.6 us (5%)
  local copies, waits for them, and re-layouts  4.14 us (2%)
    all_to_all x1, blocking collectives, on_device(): returned = lax.all_to_all(combined, 'tm', 0, 0, tiled=True)  67.9 us
    all_to_all x1, waiting for transfers between devices, on_device(): arrived = lax.all_to_all(outgoing, 'tm', 0, 0, tiled=True)  50 us
    pallas_call x1, Pallas kernels, sweep_call(): pl.pallas_call(sweep_kernel, out_shape=jax.ShapeDtypeStruct((blocks, out_...  23.2 us
    ppermute x1, waiting for transfers between devices, halo_pair(): lax.ppermute(lax.slice_in_dim(block, size - width, size, axis=dim), axis,...  9.32 us
    all_to_all x1, starting transfers between devices, on_device(): arrived = lax.all_to_all(outgoing, 'tm', 0, 0, tiled=True)  5.84 us
    concatenate x1, other arithmetic, on_device(): jnp.concatenate([spectrum, diff_slot], axis=1)  5.6 us
    pallas_call x1, Pallas kernels, combine_call(): pl.pallas_call(functools.partial(combine_kernel, weights), out_shape=jax....  5.08 us
    ppermute x1, starting transfers between devices, halo_pair(): lax.ppermute(lax.slice_in_dim(block, 0, width, axis=dim), axis, backward)  3.64 us
  transfers between devices with their start and end apart: 3, of which 3 were waited for; matrix products, arithmetic and copies ran while one was open for 1% of the time, Pallas kernels for 0%

profile of v8, /device:TPU:4, one launch (start us, length us, event | category | flops | bytes accessed | tf_op | source)
XLA Modules:
  0.0 181.3 jit_solution(9586502949555548001)
XLA Ops:
  0.0 0.8 broadcast_in_dim.6
  0.8 0.0 copy-start.2
  0.8 5.6 %pad_maximum_fusion = (f32[2,65,2,1024]{3,2,1,0:T(2,128)S(1)}, f32[2,65,2,1024]{3,2,1,0:T(2,128)}) fusion(f32[2,1,8,1024]{3,2,1,0:T(8,128)S(1)} %broadcast_in_dim.6, f32[2,64,8,1024]{3,2,1,0:T(8,128)} %rhs_ref.1), kind=kLoop, calls=%fused_computation.1 | loop fusion | flops 532480 | bytes 6389760 | tf_op jit(solution)/shard_map/concatenate | solution.py:244
  6.4 1.9 %collective-permute-start = (f32[2,65,2,1024]{3,2,1,0:T(2,128)}, f32[2,65,2,1024]{3,2,1,0:T(2,128)S(1)}, u32[]{:S(2)}, u32[]{:S(2)}) collective-permute-start(f32[2,65,2,1024]{3,2,1,0:T(2,128)} %get-tuple-element.6), channel_id=1, source_target_pairs={{0,1},{1,2},{2,3},{3,4},{4,5},{5,6},{6,7},{7,8},{8,9},{9,10},{10,1... | collective-permute-start | bytes 3194888 | tf_op jit(solution)/shard_map/ppermute | solution.py:45
  8.3 3.6 %collective-permute-start.1 = (f32[2,65,2,1024]{3,2,1,0:T(2,128)S(1)}, f32[2,65,2,1024]{3,2,1,0:T(2,128)S(1)}, u32[]{:S(2)}, u32[]{:S(2)}) collective-permute-start(f32[2,65,2,1024]{3,2,1,0:T(2,128)S(1)} %get-tuple-element.5), channel_id=1, source_target_pairs={{1,0},{2,1},{3,2},{4,3},{5,4},{6,5},{7,6},{8,7},{9,8},{10,9},{11,1... | collective-permute-start | bytes 3194888 | tf_op jit(solution)/shard_map/ppermute | solution.py:46
  12.0 0.1 pad.6.clone
  12.1 0.6 pad_maximum_fusion.3.lam_ref
  12.7 0.1 fusion.8
  12.8 0.7 maximum_maximum_fusion.table_ref
  13.5 9.3 %collective-permute-done.top_ref = f32[2,65,2,1024]{3,2,1,0:T(2,128)S(1)} collective-permute-done((f32[2,65,2,1024]{3,2,1,0:T(2,128)}, f32[2,65,2,1024]{3,2,1,0:T(2,128)S(1)}, u32[]{:S(2)}, u32[]{:S(2)}) %collective-permute-start) | collective-permute-done | bytes 1064992 | tf_op jit(solution)/shard_map/ppermute | solution.py:45
  22.9 0.0 copy-start
  22.9 1.5 collective-permute-done.1.bot_ref
  24.4 0.0 copy-done.2
  24.4 0.8 pad_maximum_fusion.2.diff_ref
  25.2 0.7 broadcast_in_dim.8.mask_ref
  25.9 0.0 copy-done
  25.9 0.0 copy-done.1
  25.9 23.2 %shard_map.28 = f32[8,1024,128]{2,1,0:T(8,128)} custom-call(f32[2,64]{1,0:T(2,128)} %pad_maximum_fusion.3.lam_ref, f32[2,64,8,1024]{3,2,1,0:T(8,128)} %rhs_ref.1, f32[2,65,2,1024]{3,2,1,0:T(2,128)} %copy-done, f32[2,65,2,1024]{3,2,1,0:T(2,128)} %copy-done.1, f32[16,1024]{1,0:T(8,128)} %pad_maximum_fusion.2.diff_ref, f32[16,1024]{1,0:T(8,128)} %broadcast_in_dim.8.mask_ref, ...), custom_call_target="tpu_custom_call" | custom-call | flops 209715200 | bytes 8388608 | tf_op jit(solution)/shard_map/pallas_call | solution.py:134
  49.2 5.8 %all-to-all-start = ((f32[8,2,512,128]{3,2,1,0:T(8,128)}), f32[8,2,512,128]{3,2,1,0:T(8,128)}, u32[]{:S(2)}, u32[]{:S(2)}) async-start(f32[8,2,512,128]{3,2,1,0:T(8,128)} %bitcast.12), calls=%async_computation | async-start | bytes 8388608 | tf_op jit(solution)/shard_map/all_to_all | solution.py:257
  55.0 0.7 exponential_multiply_fusion.fac_ref
  55.7 50.0 %all-to-all-done.a_ref = f32[8,2,512,128]{3,2,1,0:T(8,128)} async-done(((f32[8,2,512,128]{3,2,1,0:T(8,128)}), f32[8,2,512,128]{3,2,1,0:T(8,128)}, u32[]{:S(2)}, u32[]{:S(2)}) %all-to-all-start) | async-done | bytes 4194336 | tf_op jit(solution)/shard_map/all_to_all | solution.py:257
  105.7 5.1 %shard_map.29 = f32[8,2,512,128]{3,2,1,0:T(8,128)} custom-call(f32[8,64]{1,0:T(8,128)} %exponential_multiply_fusion.fac_ref, f32[8,2,512,128]{3,2,1,0:T(8,128)} %all-to-all-done.a_ref), custom_call_target="tpu_custom_call" | custom-call | flops 41943040 | bytes 8388608 | tf_op jit(solution)/shard_map/pallas_call | solution.py:189
  110.8 67.9 %all_to_all.10 = f32[8,2,512,128]{3,2,1,0:T(8,128)S(1)} all-to-all(f32[8,2,512,128]{3,2,1,0:T(8,128)} %shard_map.29), channel_id=1, replica_groups=mesh['tm'=8,'space'=16] {'tm'}, dimensions={0} | all-to-all | bytes 8388608 | tf_op jit(solution)/shard_map/all_to_all | solution.py:265
  178.7 2.6 %copy_bitcast_fusion = f32[2,64,8,1024]{3,2,1,0:T(8,128)} fusion(f32[8,2,512,128]{3,2,1,0:T(8,128)S(1)} %all_to_all.10), kind=kLoop, calls=%fused_computation | loop fusion | bytes 8388608 | tf_op jit(solution)/shard_map/reshape | solution.py:267
  (8 shorter events, 0.1 us)
Async XLA Ops:
  0.8 23.6 %copy-start.2 = (f32[8,1024]{1,0:T(8,128)S(1)}, f32[8,1024]{1,0:T(8,128)}, u32[]{:S(2)}) copy-start(f32[8,1024]{1,0:T(8,128)} %param.3) | copy-start | bytes 98308
  6.4 16.5 %collective-permute-start = (f32[2,65,2,1024]{3,2,1,0:T(2,128)}, f32[2,65,2,1024]{3,2,1,0:T(2,128)S(1)}, u32[]{:S(2)}, u32[]{:S(2)}) collective-permute-start(f32[2,65,2,1024]{3,2,1,0:T(2,128)} %get-tuple-element.6), channel_id=1, source_target_pairs={{0,1},{1,2},{2,3},{3,4},{4,5},{5,6},{6,7},{7,8},{8,9},{9,10},{10,1... | collective-permute-start | bytes 3194888 | tf_op jit(solution)/shard_map/ppermute | solution.py:45
  8.3 16.1 %collective-permute-start.1 = (f32[2,65,2,1024]{3,2,1,0:T(2,128)S(1)}, f32[2,65,2,1024]{3,2,1,0:T(2,128)S(1)}, u32[]{:S(2)}, u32[]{:S(2)}) collective-permute-start(f32[2,65,2,1024]{3,2,1,0:T(2,128)S(1)} %get-tuple-element.5), channel_id=1, source_target_pairs={{1,0},{2,1},{3,2},{4,3},{5,4},{6,5},{7,6},{8,7},{9,8},{10,9},{11,1... | collective-permute-start | bytes 3194888 | tf_op jit(solution)/shard_map/ppermute | solution.py:46
  22.9 3.1 %copy-start = (f32[2,65,2,1024]{3,2,1,0:T(2,128)}, f32[2,65,2,1024]{3,2,1,0:T(2,128)S(1)}, u32[]{:S(2)}) copy-start(f32[2,65,2,1024]{3,2,1,0:T(2,128)S(1)} %collective-permute-done.top_ref) | copy-start | bytes 3194884
  24.4 1.5 copy-start.1
  49.2 56.5 %all-to-all-start = ((f32[8,2,512,128]{3,2,1,0:T(8,128)}), f32[8,2,512,128]{3,2,1,0:T(8,128)}, u32[]{:S(2)}, u32[]{:S(2)}) async-start(f32[8,2,512,128]{3,2,1,0:T(8,128)} %bitcast.12), calls=%async_computation | async-start | bytes 8388608 | tf_op jit(solution)/shard_map/all_to_all | solution.py:257

commit v9 on v8

--- a/solution.py
+++ b/solution.py
@@ -118,7 +118,7 @@
             for r in range(8):
                 plane = field[blk, pl.ds(r, 2 * count, stride=8), :]
                 o_ref[blk, pl.ds(r, 2 * count, stride=8), :] = jnp.dot(
-                    table, plane, precision=lax.Precision.HIGHEST, preferred_element_type=jnp.float32
+                    table, plane, precision=lax.Precision.HIGH, preferred_element_type=jnp.float32
                 )
 
 

time: 182 us -> 180 us (0.989)
  Pallas kernels: 28.3 us -> 26.3 us
    pallas_call x1, Pallas kernels: 23.2 us -> 21.3 us  [sweep_call(): pl.pallas_call(sweep_kernel, out_shape=jax.ShapeDtypeStruct((blocks, out_...]
where the time goes in v9:
time: 180 us; the launch traced here: 179 us
  blocking collectives  67.9 us (38%)
  waiting for transfers between devices  60.9 us (34%)
  Pallas kernels  26.3 us (15%)
  starting transfers between devices  11.4 us (6%)
  other arithmetic  8.6 us (5%)
  local copies, waits for them, and re-layouts  4.14 us (2%)
    all_to_all x1, blocking collectives, on_device(): returned = lax.all_to_all(combined, 'tm', 0, 0, tiled=True)  67.9 us
    all_to_all x1, waiting for transfers between devices, on_device(): arrived = lax.all_to_all(outgoing, 'tm', 0, 0, tiled=True)  50 us
    pallas_call x1, Pallas kernels, sweep_call(): pl.pallas_call(sweep_kernel, out_shape=jax.ShapeDtypeStruct((blocks, out_...  21.3 us
    ppermute x1, waiting for transfers between devices, halo_pair(): lax.ppermute(lax.slice_in_dim(block, size - width, size, axis=dim), axis,...  9.32 us
    all_to_all x1, starting transfers between devices, on_device(): arrived = lax.all_to_all(outgoing, 'tm', 0, 0, tiled=True)  5.82 us
    concatenate x1, other arithmetic, on_device(): jnp.concatenate([spectrum, diff_slot], axis=1)  5.6 us
    pallas_call x1, Pallas kernels, combine_call(): pl.pallas_call(functools.partial(combine_kernel, weights), out_shape=jax....  5.08 us
    ppermute x1, starting transfers between devices, halo_pair(): lax.ppermute(lax.slice_in_dim(block, 0, width, axis=dim), axis, backward)  3.64 us
  transfers between devices with their start and end apart: 3, of which 3 were waited for; matrix products, arithmetic and copies ran while one was open for 1% of the time, Pallas kernels for 0%

profile of v9, /device:TPU:4, one launch (start us, length us, event | category | flops | bytes accessed | tf_op | source)
XLA Modules:
  0.0 179.3 jit_solution(18210593539989736443)
XLA Ops:
  0.0 0.8 broadcast_in_dim.6
  0.8 0.0 copy-start.2
  0.8 5.6 %pad_maximum_fusion = (f32[2,65,2,1024]{3,2,1,0:T(2,128)S(1)}, f32[2,65,2,1024]{3,2,1,0:T(2,128)}) fusion(f32[2,1,8,1024]{3,2,1,0:T(8,128)S(1)} %broadcast_in_dim.6, f32[2,64,8,1024]{3,2,1,0:T(8,128)} %rhs_ref.1), kind=kLoop, calls=%fused_computation.1 | loop fusion | flops 532480 | bytes 6389760 | tf_op jit(solution)/shard_map/concatenate | solution.py:244
  6.4 1.9 %collective-permute-start = (f32[2,65,2,1024]{3,2,1,0:T(2,128)}, f32[2,65,2,1024]{3,2,1,0:T(2,128)S(1)}, u32[]{:S(2)}, u32[]{:S(2)}) collective-permute-start(f32[2,65,2,1024]{3,2,1,0:T(2,128)} %get-tuple-element.6), channel_id=1, source_target_pairs={{0,1},{1,2},{2,3},{3,4},{4,5},{5,6},{6,7},{7,8},{8,9},{9,10},{10,1... | collective-permute-start | bytes 3194888 | tf_op jit(solution)/shard_map/ppermute | solution.py:45
  8.3 3.6 %collective-permute-start.1 = (f32[2,65,2,1024]{3,2,1,0:T(2,128)S(1)}, f32[2,65,2,1024]{3,2,1,0:T(2,128)S(1)}, u32[]{:S(2)}, u32[]{:S(2)}) collective-permute-start(f32[2,65,2,1024]{3,2,1,0:T(2,128)S(1)} %get-tuple-element.5), channel_id=1, source_target_pairs={{1,0},{2,1},{3,2},{4,3},{5,4},{6,5},{7,6},{8,7},{9,8},{10,9},{11,1... | collective-permute-start | bytes 3194888 | tf_op jit(solution)/shard_map/ppermute | solution.py:46
  12.0 0.1 pad.6.clone
  12.1 0.6 pad_maximum_fusion.3.lam_ref
  12.7 0.1 fusion.8
  12.8 0.7 maximum_maximum_fusion.table_ref
  13.5 9.3 %collective-permute-done.top_ref = f32[2,65,2,1024]{3,2,1,0:T(2,128)S(1)} collective-permute-done((f32[2,65,2,1024]{3,2,1,0:T(2,128)}, f32[2,65,2,1024]{3,2,1,0:T(2,128)S(1)}, u32[]{:S(2)}, u32[]{:S(2)}) %collective-permute-start) | collective-permute-done | bytes 1064992 | tf_op jit(solution)/shard_map/ppermute | solution.py:45
  22.9 0.0 copy-start
  22.9 1.5 collective-permute-done.1.bot_ref
  24.4 0.0 copy-done.2
  24.4 0.8 pad_maximum_fusion.2.diff_ref
  25.2 0.7 broadcast_in_dim.8.mask_ref
  25.9 0.0 copy-done
  25.9 0.0 copy-done.1
  25.9 21.3 %shard_map.28 = f32[8,1024,128]{2,1,0:T(8,128)} custom-call(f32[2,64]{1,0:T(2,128)} %pad_maximum_fusion.3.lam_ref, f32[2,64,8,1024]{3,2,1,0:T(8,128)} %rhs_ref.1, f32[2,65,2,1024]{3,2,1,0:T(2,128)} %copy-done, f32[2,65,2,1024]{3,2,1,0:T(2,128)} %copy-done.1, f32[16,1024]{1,0:T(8,128)} %pad_maximum_fusion.2.diff_ref, f32[16,1024]{1,0:T(8,128)} %broadcast_in_dim.8.mask_ref, ...), custom_call_target="tpu_custom_call" | custom-call | flops 209715200 | bytes 8388608 | tf_op jit(solution)/shard_map/pallas_call | solution.py:134
  47.2 5.8 %all-to-all-start = ((f32[8,2,512,128]{3,2,1,0:T(8,128)}), f32[8,2,512,128]{3,2,1,0:T(8,128)}, u32[]{:S(2)}, u32[]{:S(2)}) async-start(f32[8,2,512,128]{3,2,1,0:T(8,128)} %bitcast.12), calls=%async_computation | async-start | bytes 8388608 | tf_op jit(solution)/shard_map/all_to_all | solution.py:257
  53.0 0.7 exponential_multiply_fusion.fac_ref
  53.7 50.0 %all-to-all-done.a_ref = f32[8,2,512,128]{3,2,1,0:T(8,128)} async-done(((f32[8,2,512,128]{3,2,1,0:T(8,128)}), f32[8,2,512,128]{3,2,1,0:T(8,128)}, u32[]{:S(2)}, u32[]{:S(2)}) %all-to-all-start) | async-done | bytes 4194336 | tf_op jit(solution)/shard_map/all_to_all | solution.py:257
  103.7 5.1 %shard_map.29 = f32[8,2,512,128]{3,2,1,0:T(8,128)} custom-call(f32[8,64]{1,0:T(8,128)} %exponential_multiply_fusion.fac_ref, f32[8,2,512,128]{3,2,1,0:T(8,128)} %all-to-all-done.a_ref), custom_call_target="tpu_custom_call" | custom-call | flops 41943040 | bytes 8388608 | tf_op jit(solution)/shard_map/pallas_call | solution.py:189
  108.8 67.9 %all_to_all.10 = f32[8,2,512,128]{3,2,1,0:T(8,128)S(1)} all-to-all(f32[8,2,512,128]{3,2,1,0:T(8,128)} %shard_map.29), channel_id=1, replica_groups=mesh['tm'=8,'space'=16] {'tm'}, dimensions={0} | all-to-all | bytes 8388608 | tf_op jit(solution)/shard_map/all_to_all | solution.py:265
  176.7 2.6 %copy_bitcast_fusion = f32[2,64,8,1024]{3,2,1,0:T(8,128)} fusion(f32[8,2,512,128]{3,2,1,0:T(8,128)S(1)} %all_to_all.10), kind=kLoop, calls=%fused_computation | loop fusion | bytes 8388608 | tf_op jit(solution)/shard_map/reshape | solution.py:267
  (8 shorter events, 0.1 us)
Async XLA Ops:
  0.8 23.6 %copy-start.2 = (f32[8,1024]{1,0:T(8,128)S(1)}, f32[8,1024]{1,0:T(8,128)}, u32[]{:S(2)}) copy-start(f32[8,1024]{1,0:T(8,128)} %param.3) | copy-start | bytes 98308
  6.4 16.5 %collective-permute-start = (f32[2,65,2,1024]{3,2,1,0:T(2,128)}, f32[2,65,2,1024]{3,2,1,0:T(2,128)S(1)}, u32[]{:S(2)}, u32[]{:S(2)}) collective-permute-start(f32[2,65,2,1024]{3,2,1,0:T(2,128)} %get-tuple-element.6), channel_id=1, source_target_pairs={{0,1},{1,2},{2,3},{3,4},{4,5},{5,6},{6,7},{7,8},{8,9},{9,10},{10,1... | collective-permute-start | bytes 3194888 | tf_op jit(solution)/shard_map/ppermute | solution.py:45
  8.3 16.1 %collective-permute-start.1 = (f32[2,65,2,1024]{3,2,1,0:T(2,128)S(1)}, f32[2,65,2,1024]{3,2,1,0:T(2,128)S(1)}, u32[]{:S(2)}, u32[]{:S(2)}) collective-permute-start(f32[2,65,2,1024]{3,2,1,0:T(2,128)S(1)} %get-tuple-element.5), channel_id=1, source_target_pairs={{1,0},{2,1},{3,2},{4,3},{5,4},{6,5},{7,6},{8,7},{9,8},{10,9},{11,1... | collective-permute-start | bytes 3194888 | tf_op jit(solution)/shard_map/ppermute | solution.py:46
  22.9 3.1 %copy-start = (f32[2,65,2,1024]{3,2,1,0:T(2,128)}, f32[2,65,2,1024]{3,2,1,0:T(2,128)S(1)}, u32[]{:S(2)}) copy-start(f32[2,65,2,1024]{3,2,1,0:T(2,128)S(1)} %collective-permute-done.top_ref) | copy-start | bytes 3194884
  24.4 1.5 copy-start.1
  47.2 56.5 %all-to-all-start = ((f32[8,2,512,128]{3,2,1,0:T(8,128)}), f32[8,2,512,128]{3,2,1,0:T(8,128)}, u32[]{:S(2)}, u32[]{:S(2)}) async-start(f32[8,2,512,128]{3,2,1,0:T(8,128)} %bitcast.12), calls=%async_computation | async-start | bytes 8388608 | tf_op jit(solution)/shard_map/all_to_all | solution.py:257

commit v10 on v9

--- a/solution.py
+++ b/solution.py
@@ -47,7 +47,12 @@
     return top, bottom
 
 
-def sweep_kernel(lam_ref, rhs_ref, top_ref, bot_ref, diff_ref, mask_ref, table_ref, o_ref, field):
+def sweep_kernel(final, lam_ref, rhs_ref, top_ref, bot_ref, diff_ref, mask_ref, *rest):
+    if final:
+        low_ref, high_ref, prev_ref, o_ref, field = rest
+    else:
+        (o_ref,) = rest
+        field = o_ref
     block = rhs_ref.shape[1]
     count = lam_ref.shape[1]
     cols = rhs_ref.shape[3]
@@ -111,38 +116,56 @@
 
     lax.fori_loop(0, block, body, 0, unroll=SWEEP_UNROLL)
 
+    if not final:
+        return
+
     @pl.when(pl.program_id(0) == pl.num_programs(0) - 1)
     def _():
-        table = table_ref[...]
+        low = low_ref[...]
+        high = high_ref[...]
+        rows_out = o_ref.shape[1] // 8
         for blk in range(o_ref.shape[0]):
             for r in range(8):
-                plane = field[blk, pl.ds(r, 2 * count, stride=8), :]
-                o_ref[blk, pl.ds(r, 2 * count, stride=8), :] = jnp.dot(
-                    table, plane, precision=lax.Precision.HIGH, preferred_element_type=jnp.float32
-                )
-
-
-def sweep_call(lam, spectrum, top, bottom, diff_frame, mask_frame, table, blocks):
-    _, count, rows, cols = spectrum.shape
+                first = prev_ref[blk, pl.ds(r, 2 * count, stride=8), :]
+                second = field[blk, pl.ds(r, 2 * count, stride=8), :]
+                o_ref[blk, pl.ds(r, rows_out, stride=8), :] = jnp.dot(
+                    low, first, precision=lax.Precision.HIGH, preferred_element_type=jnp.float32
+                ) + jnp.dot(high, second, precision=lax.Precision.HIGH, preferred_element_type=jnp.float32)
+
+
+def sweep_call(lam, spectrum, offset, top, bottom, diff_frame, mask_frame, blocks, final=None):
+    _, total, rows, cols = spectrum.shape
+    count = lam.shape[1]
     block = F_BLOCK
     width = cols // blocks
-    big = pl.BlockSpec((2, block, rows, cols), lambda g: (0, g, 0, 0))
+    skip = offset // block
+    big = pl.BlockSpec((2, block, rows, cols), lambda g: (0, g + skip, 0, 0))
     edge = pl.BlockSpec((2, block, HALO, cols), lambda g: (0, g, 0, 0))
     whole = pl.BlockSpec((16, cols), lambda g: (0, 0))
-    square = pl.BlockSpec((2 * count, 2 * count), lambda g: (0, 0))
-    out_rows = 2 * count * rows
+    field_rows = 2 * count * rows
+    in_specs = [pl.BlockSpec(memory_space=pltpu.SMEM), big, edge, edge, whole, whole]
+    operands = [lam, spectrum, top, bottom, diff_frame, mask_frame]
+    scratch = []
+    out_rows = field_rows
+    if final is not None:
+        low, high, prev = final
+        half = pl.BlockSpec(low.shape, lambda g: (0, 0))
+        in_specs += [half, half, pl.BlockSpec(prev.shape, lambda g: (0, 0, 0))]
+        operands += [low, high, prev]
+        scratch = [pltpu.VMEM((blocks, field_rows, width), jnp.float32)]
+        out_rows = 2 * total * rows
     return pl.pallas_call(
-        sweep_kernel,
+        functools.partial(sweep_kernel, final is not None),
         out_shape=jax.ShapeDtypeStruct((blocks, out_rows, width), jnp.float32),
         grid=(count // block,),
-        in_specs=[pl.BlockSpec(memory_space=pltpu.SMEM), big, edge, edge, whole, whole, square],
+        in_specs=in_specs,
         out_specs=pl.BlockSpec((blocks, out_rows, width), lambda g: (0, 0, 0)),
-        scratch_shapes=[pltpu.VMEM((blocks, out_rows, width), jnp.float32)],
+        scratch_shapes=scratch,
         compiler_params=pltpu.CompilerParams(dimension_semantics=("arbitrary",)),
         cost_estimate=pl.CostEstimate(
-            flops=200 * spectrum.size, transcendentals=0, bytes_accessed=8 * spectrum.size
+            flops=100 * spectrum.size, transcendentals=0, bytes_accessed=4 * spectrum.size
         ),
-    )(lam, spectrum, top, bottom, diff_frame, mask_frame, table)
+    )(*operands)
 
 
 def combine_kernel(weights, fac_ref, a_ref, o_ref):
@@ -240,9 +263,11 @@
     freq_ids = index_f * tm_count + residue
     lam = jnp.stack(shift_parts(freq_ids, total_steps))
 
+    half = local_count // 2
     diff_slot = jnp.broadcast_to(diffusivity[None, None], (2, 1, row_count, col_count))
-    top, bottom = halo_pair(jnp.concatenate([spectrum, diff_slot], axis=1), "space", 2, HALO)
-    diff_frame, mask_frame = frames(diffusivity, top[0, local_count], bottom[0, local_count], space_place, space_count)
+    top_a, bottom_a = halo_pair(jnp.concatenate([spectrum[:, :half], diff_slot], axis=1), "space", 2, HALO)
+    top_b, bottom_b = halo_pair(spectrum[:, half:], "space", 2, HALO)
+    diff_frame, mask_frame = frames(diffusivity, top_a[0, half], bottom_a[0, half], space_place, space_count)
     grid_angle = (index_f[:, None] * freq_ids[None, :] % total_steps).astype(jnp.float32) * (
         2.0 * math.pi / total_steps
     )
@@ -251,7 +276,13 @@
     table = jnp.concatenate(
         [jnp.concatenate([cosine, -sine], 1), jnp.concatenate([sine, cosine], 1)], 0
     )
-    outgoing = sweep_call(lam, spectrum, top, bottom, diff_frame, mask_frame, table, tm_count)
+    low = jnp.concatenate([table[:, :half], table[:, local_count:local_count + half]], 1)
+    high = jnp.concatenate([table[:, half:local_count], table[:, local_count + half:]], 1)
+    first = sweep_call(lam[:, :half], spectrum, 0, top_a, bottom_a, diff_frame, mask_frame, tm_count)
+    outgoing = sweep_call(
+        lam[:, half:], spectrum, half, top_b, bottom_b, diff_frame, mask_frame, tm_count,
+        final=(low, high, first),
+    )
     col_block = col_count // tm_count
     outgoing = outgoing.reshape(tm_count, 2, local_count * row_count, col_block)
     arrived = lax.all_to_all(outgoing, "tm", 0, 0, tiled=True)

time: 180 us -> 175 us (0.972)
  waiting for transfers between devices: 60.9 us -> 48.8 us
  other arithmetic: 8.6 us -> 2.96 us
  starting transfers between devices: 11.4 us -> 16.9 us
  Pallas kernels: 26.3 us -> 31.4 us
  local copies, waits for them, and re-layouts: 4.14 us -> 7.86 us
  blocking collectives: 67.9 us -> 65.3 us
    ppermute x1 -> x2, waiting for transfers between devices: 9.32 us -> 0.01 us  [halo_pair(): lax.ppermute(lax.slice_in_dim(block, size - width, size, axis=dim), axis,...]
    pallas_call x1 -> x2, Pallas kernels: 21.3 us -> 26.3 us  [sweep_call(): pl.pallas_call(functools.partial(sweep_kernel, final is not None), out_sh...]
    concatenate x1, other arithmetic: 5.6 us -> 0.76 us  [on_device(): jnp.concatenate([table[:, :half], table[:, local_count:local_count + half...]
    ppermute x1 -> x2, starting transfers between devices: 3.64 us -> 7.29 us  [halo_pair(): lax.ppermute(lax.slice_in_dim(block, 0, width, axis=dim), axis, backward)]
    slice x0 -> x5, local copies, waits for them, and re-layouts: none -> 2.77 us  [the longest x1 1.36 us: halo_pair(): lax.slice_in_dim(block, 0, width, axis=dim)]
    all_to_all x1, blocking collectives: 67.9 us -> 65.3 us  [on_device(): returned = lax.all_to_all(combined, 'tm', 0, 0, tiled=True)]
    ppermute x1 -> x2, starting transfers between devices: 1.91 us -> 3.83 us  [halo_pair(): lax.ppermute(lax.slice_in_dim(block, size - width, size, axis=dim), axis,...]
  transfers between devices with their start and end apart: 3 -> 5, of which waited for: 3 -> 1; matrix products, arithmetic and copies ran while one was open for 1% -> 3% of each run, Pallas kernels for 0% -> 6%
where the time goes in v10:
time: 175 us; the launch traced here: 173 us
  blocking collectives  65.3 us (37%)
  waiting for transfers between devices  48.8 us (28%)
  Pallas kernels  31.4 us (18%)
  starting transfers between devices  16.9 us (10%)
  local copies, waits for them, and re-layouts  7.86 us (4%)
  other arithmetic  2.96 us (2%)
    all_to_all x1, blocking collectives, on_device(): returned = lax.all_to_all(combined, 'tm', 0, 0, tiled=True)  65.3 us
    all_to_all x1, waiting for transfers between devices, on_device(): arrived = lax.all_to_all(outgoing, 'tm', 0, 0, tiled=True)  48.7 us
    pallas_call x2, Pallas kernels, sweep_call(): pl.pallas_call(functools.partial(sweep_kernel, final is not None), out_sh...  26.3 us
    ppermute x2, starting transfers between devices, halo_pair(): lax.ppermute(lax.slice_in_dim(block, 0, width, axis=dim), axis, backward)  7.29 us
    all_to_all x1, starting transfers between devices, on_device(): arrived = lax.all_to_all(outgoing, 'tm', 0, 0, tiled=True)  5.82 us
    pallas_call x1, Pallas kernels, combine_call(): pl.pallas_call(functools.partial(combine_kernel, weights), out_shape=jax....  5.08 us
    ppermute x2, starting transfers between devices, halo_pair(): lax.ppermute(lax.slice_in_dim(block, size - width, size, axis=dim), axis,...  3.83 us
  transfers between devices with their start and end apart: 5, of which 1 were waited for; matrix products, arithmetic and copies ran while one was open for 3% of the time, Pallas kernels for 6%

profile of v10, /device:TPU:4, one launch (start us, length us, event | category | flops | bytes accessed | tf_op | source)
XLA Modules:
  0.0 173.4 jit_solution(11357006147884673883)
XLA Ops:
  0.0 0.9 broadcast_in_dim.6
  0.9 0.7 slice-done
  1.6 0.4 pad_maximum_fusion.1
  2.0 1.9 %collective-permute-start.3 = (f32[2,33,2,1024]{3,2,1,0:T(2,128)S(1)}, f32[2,33,2,1024]{3,2,1,0:T(2,128)S(1)}, u32[]{:S(2)}, u32[]{:S(2)}) collective-permute-start(f32[2,33,2,1024]{3,2,1,0:T(2,128)S(1)} %get-tuple-element.8), channel_id=1, source_target_pairs={{0,1},{1,2},{2,3},{3,4},{4,5},{5,6},{6,7},{7,8},{8,9},{9,10},{10,1... | collective-permute-start | bytes 1622024 | tf_op jit(solution)/shard_map/ppermute | solution.py:45
  3.9 3.6 %collective-permute-start.2 = (f32[2,33,2,1024]{3,2,1,0:T(2,128)S(1)}, f32[2,33,2,1024]{3,2,1,0:T(2,128)S(1)}, u32[]{:S(2)}, u32[]{:S(2)}) collective-permute-start(f32[2,33,2,1024]{3,2,1,0:T(2,128)S(1)} %get-tuple-element.7), channel_id=1, source_target_pairs={{1,0},{2,1},{3,2},{4,3},{5,4},{6,5},{7,6},{8,7},{9,8},{10,9},{11,1... | collective-permute-start | bytes 1622024 | tf_op jit(solution)/shard_map/ppermute | solution.py:46
  7.6 1.4 fusion.9
  8.9 1.9 %collective-permute-start = (f32[2,32,2,1024]{3,2,1,0:T(2,128)}, f32[2,32,2,1024]{3,2,1,0:T(2,128)S(1)}, u32[]{:S(2)}, u32[]{:S(2)}) collective-permute-start(f32[2,32,2,1024]{3,2,1,0:T(2,128)} %get-tuple-element.6), channel_id=1, source_target_pairs={{0,1},{1,2},{2,3},{3,4},{4,5},{5,6},{6,7},{7,8},{8,9},{9,10},{10,1... | collective-permute-start | bytes 1572872 | tf_op jit(solution)/shard_map/ppermute | solution.py:45
  10.9 3.6 %collective-permute-start.1 = (f32[2,32,2,1024]{3,2,1,0:T(2,128)}, f32[2,32,2,1024]{3,2,1,0:T(2,128)}, u32[]{:S(2)}, u32[]{:S(2)}) collective-permute-start(f32[2,32,2,1024]{3,2,1,0:T(2,128)} %get-tuple-element.5), channel_id=1, source_target_pairs={{1,0},{2,1},{3,2},{4,3},{5,4},{6,5},{7,6},{8,7},{9,8},{10,9},{11,1... | collective-permute-start | bytes 1572872 | tf_op jit(solution)/shard_map/ppermute | solution.py:46
  14.6 0.1 fusion.8
  14.7 0.1 maximum_maximum_fusion
  14.8 0.1 fusion.10
  15.1 0.8 pad_maximum_fusion.3
  15.8 0.6 fusion.11
  16.5 0.8 pad_maximum_fusion.2.diff_ref
  17.3 0.7 broadcast_in_dim.8.mask_ref
  18.0 10.7 %shard_map.28.rest_2_ = f32[8,512,128]{2,1,0:T(8,128)} custom-call(f32[2,32]{1,0:T(2,128)} %get-tuple-element.13.lam_ref, f32[2,64,8,1024]{3,2,1,0:T(8,128)} %rhs_ref.3, f32[2,33,2,1024]{3,2,1,0:T(2,128)} %copy-done.1, f32[2,33,2,1024]{3,2,1,0:T(2,128)} %copy-done.2, f32[16,1024]{1,0:T(8,128)} %pad_maximum_fusion.2.diff_ref, f32[16,1024]{1,0:T(8,128)} %broadcast_in_dim.8.mask_ref), custom_call_target="tpu_custom_call" | custom-call | flops 104857600 | bytes 4194304 | tf_op jit(solution)/shard_map/pallas_call | solution.py:157
  28.7 0.8 copy-done.3
  29.5 15.6 %shard_map.29 = f32[8,1024,128]{2,1,0:T(8,128)} custom-call(f32[2,32]{1,0:T(2,128)} %get-tuple-element.14.lam_ref, f32[2,64,8,1024]{3,2,1,0:T(8,128)} %rhs_ref.3, f32[2,32,2,1024]{3,2,1,0:T(2,128)} %copy-done.3, f32[2,32,2,1024]{3,2,1,0:T(2,128)} %collective-permute-done.1.bot_ref, f32[16,1024]{1,0:T(8,128)} %pad_maximum_fusion.2.diff_ref, ...), custom_call_target="tpu_custom_call" | custom-call | flops 104857600 | bytes 4194304 | tf_op jit(solution)/shard_map/pallas_call | solution.py:157
  45.1 5.8 %all-to-all-start = ((f32[8,2,512,128]{3,2,1,0:T(8,128)}), f32[8,2,512,128]{3,2,1,0:T(8,128)}, u32[]{:S(2)}, u32[]{:S(2)}) async-start(f32[8,2,512,128]{3,2,1,0:T(8,128)} %bitcast.12), calls=%async_computation | async-start | bytes 8388608 | tf_op jit(solution)/shard_map/all_to_all | solution.py:288
  51.0 0.7 exponential_multiply_fusion.fac_ref
  51.6 48.7 %all-to-all-done.a_ref = f32[8,2,512,128]{3,2,1,0:T(8,128)} async-done(((f32[8,2,512,128]{3,2,1,0:T(8,128)}), f32[8,2,512,128]{3,2,1,0:T(8,128)}, u32[]{:S(2)}, u32[]{:S(2)}) %all-to-all-start) | async-done | bytes 4194336 | tf_op jit(solution)/shard_map/all_to_all | solution.py:288
  100.4 5.1 %shard_map.30 = f32[8,2,512,128]{3,2,1,0:T(8,128)} custom-call(f32[8,64]{1,0:T(8,128)} %exponential_multiply_fusion.fac_ref, f32[8,2,512,128]{3,2,1,0:T(8,128)} %all-to-all-done.a_ref), custom_call_target="tpu_custom_call" | custom-call | flops 41943040 | bytes 8388608 | tf_op jit(solution)/shard_map/pallas_call | solution.py:212
  105.5 65.3 %all_to_all.10 = f32[8,2,512,128]{3,2,1,0:T(8,128)S(1)} all-to-all(f32[8,2,512,128]{3,2,1,0:T(8,128)} %shard_map.30), channel_id=1, replica_groups=mesh['tm'=8,'space'=16] {'tm'}, dimensions={0} | all-to-all | bytes 8388608 | tf_op jit(solution)/shard_map/all_to_all | solution.py:296
  170.8 2.6 %copy_bitcast_fusion = f32[2,64,8,1024]{3,2,1,0:T(8,128)} fusion(f32[8,2,512,128]{3,2,1,0:T(8,128)S(1)} %all_to_all.10), kind=kLoop, calls=%fused_computation | loop fusion | bytes 8388608 | tf_op jit(solution)/shard_map/reshape | solution.py:298
  (23 shorter events, 0.2 us)
Async XLA Ops:
  0.0 1.6 slice-start
  0.0 7.6 %copy-start = (f32[2,64,8,1024]{3,2,1,0:T(8,128)S(1)}, f32[2,64,8,1024]{3,2,1,0:T(8,128)}, u32[]{:S(2)}) copy-start(f32[2,64,8,1024]{3,2,1,0:T(8,128)} %rhs_ref.3) | copy-start | bytes 12582916
  0.0 16.5 %copy-start.4 = (f32[8,1024]{1,0:T(8,128)S(1)}, f32[8,1024]{1,0:T(8,128)}, u32[]{:S(2)}) copy-start(f32[8,1024]{1,0:T(8,128)} %param.3) | copy-start | bytes 98308
  2.0 14.4 %collective-permute-start.3 = (f32[2,33,2,1024]{3,2,1,0:T(2,128)S(1)}, f32[2,33,2,1024]{3,2,1,0:T(2,128)S(1)}, u32[]{:S(2)}, u32[]{:S(2)}) collective-permute-start(f32[2,33,2,1024]{3,2,1,0:T(2,128)S(1)} %get-tuple-element.8), channel_id=1, source_target_pairs={{0,1},{1,2},{2,3},{3,4},{4,5},{5,6},{6,7},{7,8},{8,9},{9,10},{10,1... | collective-permute-start | bytes 1622024 | tf_op jit(solution)/shard_map/ppermute | solution.py:45
  3.9 12.5 %collective-permute-start.2 = (f32[2,33,2,1024]{3,2,1,0:T(2,128)S(1)}, f32[2,33,2,1024]{3,2,1,0:T(2,128)S(1)}, u32[]{:S(2)}, u32[]{:S(2)}) collective-permute-start(f32[2,33,2,1024]{3,2,1,0:T(2,128)S(1)} %get-tuple-element.7), channel_id=1, source_target_pairs={{1,0},{2,1},{3,2},{4,3},{5,4},{6,5},{7,6},{8,7},{9,8},{10,9},{11,1... | collective-permute-start | bytes 1622024 | tf_op jit(solution)/shard_map/ppermute | solution.py:46
  8.9 19.8 %collective-permute-start = (f32[2,32,2,1024]{3,2,1,0:T(2,128)}, f32[2,32,2,1024]{3,2,1,0:T(2,128)S(1)}, u32[]{:S(2)}, u32[]{:S(2)}) collective-permute-start(f32[2,32,2,1024]{3,2,1,0:T(2,128)} %get-tuple-element.6), channel_id=1, source_target_pairs={{0,1},{1,2},{2,3},{3,4},{4,5},{5,6},{6,7},{7,8},{8,9},{9,10},{10,1... | collective-permute-start | bytes 1572872 | tf_op jit(solution)/shard_map/ppermute | solution.py:45
  10.9 17.9 %collective-permute-start.1 = (f32[2,32,2,1024]{3,2,1,0:T(2,128)}, f32[2,32,2,1024]{3,2,1,0:T(2,128)}, u32[]{:S(2)}, u32[]{:S(2)}) collective-permute-start(f32[2,32,2,1024]{3,2,1,0:T(2,128)} %get-tuple-element.5), channel_id=1, source_target_pairs={{1,0},{2,1},{3,2},{4,3},{5,4},{6,5},{7,6},{8,7},{9,8},{10,9},{11,1... | collective-permute-start | bytes 1572872 | tf_op jit(solution)/shard_map/ppermute | solution.py:46
  16.4 1.6 copy-start.1
  16.5 1.6 copy-start.2
  28.7 0.8 copy-start.3
  45.1 55.2 %all-to-all-start = ((f32[8,2,512,128]{3,2,1,0:T(8,128)}), f32[8,2,512,128]{3,2,1,0:T(8,128)}, u32[]{:S(2)}, u32[]{:S(2)}) async-start(f32[8,2,512,128]{3,2,1,0:T(8,128)} %bitcast.12), calls=%async_computation | async-start | bytes 8388608 | tf_op jit(solution)/shard_map/all_to_all | solution.py:288

commit v11 on v10

--- a/solution.py
+++ b/solution.py
@@ -18,6 +18,7 @@
 Q_BLOCK = 16
 F_BLOCK = 16
 SWEEP_UNROLL = 2
+FIRST_SWEEP = 16
 HALO = 2
 
 
@@ -126,7 +127,7 @@
         rows_out = o_ref.shape[1] // 8
         for blk in range(o_ref.shape[0]):
             for r in range(8):
-                first = prev_ref[blk, pl.ds(r, 2 * count, stride=8), :]
+                first = prev_ref[blk, pl.ds(r, prev_ref.shape[1] // 8, stride=8), :]
                 second = field[blk, pl.ds(r, 2 * count, stride=8), :]
                 o_ref[blk, pl.ds(r, rows_out, stride=8), :] = jnp.dot(
                     low, first, precision=lax.Precision.HIGH, preferred_element_type=jnp.float32
@@ -149,8 +150,11 @@
     out_rows = field_rows
     if final is not None:
         low, high, prev = final
-        half = pl.BlockSpec(low.shape, lambda g: (0, 0))
-        in_specs += [half, half, pl.BlockSpec(prev.shape, lambda g: (0, 0, 0))]
+        in_specs += [
+            pl.BlockSpec(low.shape, lambda g: (0, 0)),
+            pl.BlockSpec(high.shape, lambda g: (0, 0)),
+            pl.BlockSpec(prev.shape, lambda g: (0, 0, 0)),
+        ]
         operands += [low, high, prev]
         scratch = [pltpu.VMEM((blocks, field_rows, width), jnp.float32)]
         out_rows = 2 * total * rows
@@ -263,7 +267,7 @@
     freq_ids = index_f * tm_count + residue
     lam = jnp.stack(shift_parts(freq_ids, total_steps))
 
-    half = local_count // 2
+    half = FIRST_SWEEP
     diff_slot = jnp.broadcast_to(diffusivity[None, None], (2, 1, row_count, col_count))
     top_a, bottom_a = halo_pair(jnp.concatenate([spectrum[:, :half], diff_slot], axis=1), "space", 2, HALO)
     top_b, bottom_b = halo_pair(spectrum[:, half:], "space", 2, HALO)

time: 175 us -> 183 us (1.046)
  local copies, waits for them, and re-layouts: 7.86 us -> 13.2 us
  other arithmetic: 2.96 us -> 5.41 us
    slice x1, local copies, waits for them, and re-layouts: 1.36 us -> 3.69 us  [halo_pair(): lax.slice_in_dim(block, 0, width, axis=dim)]
  transfers between devices with their start and end apart: 5 -> 5, of which waited for: 1 -> 1; matrix products, arithmetic and copies ran while one was open for 3% -> 6% of each run, Pallas kernels for 6% -> 4%
where the time goes in v11:
time: 183 us; the launch traced here: 180 us
  blocking collectives  64.9 us (35%)
  waiting for transfers between devices  48.6 us (27%)
  Pallas kernels  30.6 us (17%)
  starting transfers between devices  16.9 us (9%)
  local copies, waits for them, and re-layouts  13.2 us (7%)
  other arithmetic  5.41 us (3%)
    all_to_all x1, blocking collectives, on_device(): returned = lax.all_to_all(combined, 'tm', 0, 0, tiled=True)  64.9 us
    all_to_all x1, waiting for transfers between devices, on_device(): arrived = lax.all_to_all(outgoing, 'tm', 0, 0, tiled=True)  48.6 us
    pallas_call x2, Pallas kernels, sweep_call(): pl.pallas_call(functools.partial(sweep_kernel, final is not None), out_sh...  25.6 us
    ppermute x2, starting transfers between devices, halo_pair(): lax.ppermute(lax.slice_in_dim(block, 0, width, axis=dim), axis, backward)  7.29 us
    all_to_all x1, starting transfers between devices, on_device(): arrived = lax.all_to_all(outgoing, 'tm', 0, 0, tiled=True)  5.82 us
    pallas_call x1, Pallas kernels, combine_call(): pl.pallas_call(functools.partial(combine_kernel, weights), out_shape=jax....  5.08 us
    ppermute x2, starting transfers between devices, halo_pair(): lax.ppermute(lax.slice_in_dim(block, size - width, size, axis=dim), axis,...  3.83 us
    slice x1, local copies, waits for them, and re-layouts, halo_pair(): lax.slice_in_dim(block, 0, width, axis=dim)  3.69 us
  transfers between devices with their start and end apart: 5, of which 1 were waited for; matrix products, arithmetic and copies ran while one was open for 6% of the time, Pallas kernels for 4%

profile of v11, /device:TPU:4, one launch (start us, length us, event | category | flops | bytes accessed | tf_op | source)
XLA Modules:
  0.0 179.9 jit_solution(8598412201451856393)
XLA Ops:
  0.0 1.3 slice.45
  1.3 0.8 broadcast_in_dim.6
  2.1 1.0 pad_maximum_fusion.1
  3.1 1.9 %collective-permute-start.3 = (f32[2,17,2,1024]{3,2,1,0:T(2,128)}, f32[2,17,2,1024]{3,2,1,0:T(2,128)S(1)}, u32[]{:S(2)}, u32[]{:S(2)}) collective-permute-start(f32[2,17,2,1024]{3,2,1,0:T(2,128)} %get-tuple-element.8), channel_id=1, source_target_pairs={{0,1},{1,2},{2,3},{3,4},{4,5},{5,6},{6,7},{7,8},{8,9},{9,10},{10,1... | collective-permute-start | bytes 835592 | tf_op jit(solution)/shard_map/ppermute | solution.py:46
  5.0 3.6 %collective-permute-start.2 = (f32[2,17,2,1024]{3,2,1,0:T(2,128)}, f32[2,17,2,1024]{3,2,1,0:T(2,128)}, u32[]{:S(2)}, u32[]{:S(2)}) collective-permute-start(f32[2,17,2,1024]{3,2,1,0:T(2,128)} %get-tuple-element.7), channel_id=1, source_target_pairs={{1,0},{2,1},{3,2},{4,3},{5,4},{6,5},{7,6},{8,7},{9,8},{10,9},{11,1... | collective-permute-start | bytes 835592 | tf_op jit(solution)/shard_map/ppermute | solution.py:47
  8.6 3.7 %fusion.9 = (f32[2,48,2,1024]{3,2,1,0:T(2,128)S(1)}, f32[2,48,2,1024]{3,2,1,0:T(2,128)S(1)}) fusion(f32[2,64,8,1024]{3,2,1,0:T(8,128)} %rhs_ref.3), kind=kLoop, calls=%fused_computation.29 | loop fusion | bytes 3145728 | tf_op jit(solution)/shard_map/slice | solution.py:47
  12.3 1.9 %collective-permute-start = (f32[2,48,2,1024]{3,2,1,0:T(2,128)S(1)}, f32[2,48,2,1024]{3,2,1,0:T(2,128)S(1)}, u32[]{:S(2)}, u32[]{:S(2)}) collective-permute-start(f32[2,48,2,1024]{3,2,1,0:T(2,128)S(1)} %get-tuple-element.6), channel_id=1, source_target_pairs={{0,1},{1,2},{2,3},{3,4},{4,5},{5,6},{6,7},{7,8},{8,9},{9,10},{10,1... | collective-permute-start | bytes 2359304 | tf_op jit(solution)/shard_map/ppermute | solution.py:46
  14.3 3.6 %collective-permute-start.1 = (f32[2,48,2,1024]{3,2,1,0:T(2,128)S(1)}, f32[2,48,2,1024]{3,2,1,0:T(2,128)S(1)}, u32[]{:S(2)}, u32[]{:S(2)}) collective-permute-start(f32[2,48,2,1024]{3,2,1,0:T(2,128)S(1)} %get-tuple-element.5), channel_id=1, source_target_pairs={{1,0},{2,1},{3,2},{4,3},{5,4},{6,5},{7,6},{8,7},{9,8},{10,9},{11,1... | collective-permute-start | bytes 2359304 | tf_op jit(solution)/shard_map/ppermute | solution.py:47
  18.4 0.7 pad_maximum_fusion.3.rest_0_
  19.7 0.7 pad_maximum_fusion.4.rest_1_
  20.5 1.3 slice.42.lam_ref
  21.9 0.7 slice_bitcast_fusion.1
  22.6 1.5 pad_maximum_fusion.2.diff_ref
  24.1 0.7 broadcast_in_dim.8.mask_ref
  24.8 6.3 %shard_map.28.rest_2_ = f32[8,256,128]{2,1,0:T(8,128)} custom-call(f32[2,16]{1,0:T(2,128)} %bitcast.14, f32[2,64,8,1024]{3,2,1,0:T(8,128)} %rhs_ref.3, f32[2,17,2,1024]{3,2,1,0:T(2,128)} %copy-done.2, f32[2,17,2,1024]{3,2,1,0:T(2,128)} %collective-permute-done.2.bot_ref, f32[16,1024]{1,0:T(8,128)} %pad_maximum_fusion.2.diff_ref, ...), custom_call_target="tpu_custom_call" | custom-call | flops 104857600 | bytes 4194304 | tf_op jit(solution)/shard_map/pallas_call | solution.py:161
  31.1 0.9 copy-done
  32.0 0.9 copy-done.1
  32.9 19.3 %shard_map.29 = f32[8,1024,128]{2,1,0:T(8,128)} custom-call(f32[2,48]{1,0:T(2,128)} %slice.42.lam_ref, f32[2,64,8,1024]{3,2,1,0:T(8,128)} %rhs_ref.3, f32[2,48,2,1024]{3,2,1,0:T(2,128)} %copy-done, f32[2,48,2,1024]{3,2,1,0:T(2,128)} %copy-done.1, f32[16,1024]{1,0:T(8,128)} %pad_maximum_fusion.2.diff_ref, f32[16,1024]{1,0:T(8,128)} %broadcast_in_dim.8.mask_ref, ...), custom_call_target="tpu_custom_call" | custom-call | flops 104857600 | bytes 4194304 | tf_op jit(solution)/shard_map/pallas_call | solution.py:161
  52.2 5.8 %all-to-all-start = ((f32[8,2,512,128]{3,2,1,0:T(8,128)}), f32[8,2,512,128]{3,2,1,0:T(8,128)}, u32[]{:S(2)}, u32[]{:S(2)}) async-start(f32[8,2,512,128]{3,2,1,0:T(8,128)} %bitcast.13), calls=%async_computation | async-start | bytes 8388608 | tf_op jit(solution)/shard_map/all_to_all | solution.py:292
  58.0 0.7 exponential_multiply_fusion.fac_ref
  58.7 48.6 %all-to-all-done.a_ref = f32[8,2,512,128]{3,2,1,0:T(8,128)} async-done(((f32[8,2,512,128]{3,2,1,0:T(8,128)}), f32[8,2,512,128]{3,2,1,0:T(8,128)}, u32[]{:S(2)}, u32[]{:S(2)}) %all-to-all-start) | async-done | bytes 4194336 | tf_op jit(solution)/shard_map/all_to_all | solution.py:292
  107.2 5.1 %shard_map.30 = f32[8,2,512,128]{3,2,1,0:T(8,128)} custom-call(f32[8,64]{1,0:T(8,128)} %exponential_multiply_fusion.fac_ref, f32[8,2,512,128]{3,2,1,0:T(8,128)} %all-to-all-done.a_ref), custom_call_target="tpu_custom_call" | custom-call | flops 41943040 | bytes 8388608 | tf_op jit(solution)/shard_map/pallas_call | solution.py:216
  112.3 64.9 %all_to_all.10 = f32[8,2,512,128]{3,2,1,0:T(8,128)S(1)} all-to-all(f32[8,2,512,128]{3,2,1,0:T(8,128)} %shard_map.30), channel_id=1, replica_groups=mesh['tm'=8,'space'=16] {'tm'}, dimensions={0} | all-to-all | bytes 8388608 | tf_op jit(solution)/shard_map/all_to_all | solution.py:300
  177.3 2.6 %copy_bitcast_fusion = f32[2,64,8,1024]{3,2,1,0:T(8,128)} fusion(f32[8,2,512,128]{3,2,1,0:T(8,128)S(1)} %all_to_all.10), kind=kLoop, calls=%fused_computation | loop fusion | bytes 8388608 | tf_op jit(solution)/shard_map/reshape | solution.py:302
  (20 shorter events, 1.2 us)
Async XLA Ops:
  3.1 18.8 %collective-permute-start.3 = (f32[2,17,2,1024]{3,2,1,0:T(2,128)}, f32[2,17,2,1024]{3,2,1,0:T(2,128)S(1)}, u32[]{:S(2)}, u32[]{:S(2)}) collective-permute-start(f32[2,17,2,1024]{3,2,1,0:T(2,128)} %get-tuple-element.8), channel_id=1, source_target_pairs={{0,1},{1,2},{2,3},{3,4},{4,5},{5,6},{6,7},{7,8},{8,9},{9,10},{10,1... | collective-permute-start | bytes 835592 | tf_op jit(solution)/shard_map/ppermute | solution.py:46
  5.0 16.9 %collective-permute-start.2 = (f32[2,17,2,1024]{3,2,1,0:T(2,128)}, f32[2,17,2,1024]{3,2,1,0:T(2,128)}, u32[]{:S(2)}, u32[]{:S(2)}) collective-permute-start(f32[2,17,2,1024]{3,2,1,0:T(2,128)} %get-tuple-element.7), channel_id=1, source_target_pairs={{1,0},{2,1},{3,2},{4,3},{5,4},{6,5},{7,6},{8,7},{9,8},{10,9},{11,1... | collective-permute-start | bytes 835592 | tf_op jit(solution)/shard_map/ppermute | solution.py:47
  12.3 18.7 %collective-permute-start = (f32[2,48,2,1024]{3,2,1,0:T(2,128)S(1)}, f32[2,48,2,1024]{3,2,1,0:T(2,128)S(1)}, u32[]{:S(2)}, u32[]{:S(2)}) collective-permute-start(f32[2,48,2,1024]{3,2,1,0:T(2,128)S(1)} %get-tuple-element.6), channel_id=1, source_target_pairs={{0,1},{1,2},{2,3},{3,4},{4,5},{5,6},{6,7},{7,8},{8,9},{9,10},{10,1... | collective-permute-start | bytes 2359304 | tf_op jit(solution)/shard_map/ppermute | solution.py:46
  14.3 16.8 %collective-permute-start.1 = (f32[2,48,2,1024]{3,2,1,0:T(2,128)S(1)}, f32[2,48,2,1024]{3,2,1,0:T(2,128)S(1)}, u32[]{:S(2)}, u32[]{:S(2)}) collective-permute-start(f32[2,48,2,1024]{3,2,1,0:T(2,128)S(1)} %get-tuple-element.5), channel_id=1, source_target_pairs={{1,0},{2,1},{3,2},{4,3},{5,4},{6,5},{7,6},{8,7},{9,8},{10,9},{11,1... | collective-permute-start | bytes 2359304 | tf_op jit(solution)/shard_map/ppermute | solution.py:47
  21.9 2.9 %copy-start.2 = (f32[2,17,2,1024]{3,2,1,0:T(2,128)}, f32[2,17,2,1024]{3,2,1,0:T(2,128)S(1)}, u32[]{:S(2)}) copy-start(f32[2,17,2,1024]{3,2,1,0:T(2,128)S(1)} %collective-permute-done.3.top_ref) | copy-start | bytes 835588
  31.1 0.9 copy-start
  32.0 0.9 copy-start.1
  52.2 55.1 %all-to-all-start = ((f32[8,2,512,128]{3,2,1,0:T(8,128)}), f32[8,2,512,128]{3,2,1,0:T(8,128)}, u32[]{:S(2)}, u32[]{:S(2)}) async-start(f32[8,2,512,128]{3,2,1,0:T(8,128)} %bitcast.13), calls=%async_computation | async-start | bytes 8388608 | tf_op jit(solution)/shard_map/all_to_all | solution.py:292

commit v12 on v10

--- a/solution.py
+++ b/solution.py
@@ -17,7 +17,7 @@
 ]
 Q_BLOCK = 16
 F_BLOCK = 16
-SWEEP_UNROLL = 2
+SWEEP_UNROLL = 4
 HALO = 2
 
 

time: 175 us -> 174 us (level)
  no operation moved by 1% of the time
where the time goes in v12:
time: 174 us; the launch traced here: 172 us
  blocking collectives  65.3 us (38%)
  waiting for transfers between devices  48.8 us (28%)
  Pallas kernels  30.3 us (17%)
  starting transfers between devices  16.9 us (10%)
  local copies, waits for them, and re-layouts  7.86 us (5%)
  other arithmetic  2.96 us (2%)
    all_to_all x1, blocking collectives, on_device(): returned = lax.all_to_all(combined, 'tm', 0, 0, tiled=True)  65.3 us
    all_to_all x1, waiting for transfers between devices, on_device(): arrived = lax.all_to_all(outgoing, 'tm', 0, 0, tiled=True)  48.7 us
    pallas_call x2, Pallas kernels, sweep_call(): pl.pallas_call(functools.partial(sweep_kernel, final is not None), out_sh...  25.3 us
    ppermute x2, starting transfers between devices, halo_pair(): lax.ppermute(lax.slice_in_dim(block, 0, width, axis=dim), axis, backward)  7.29 us
    all_to_all x1, starting transfers between devices, on_device(): arrived = lax.all_to_all(outgoing, 'tm', 0, 0, tiled=True)  5.82 us
    pallas_call x1, Pallas kernels, combine_call(): pl.pallas_call(functools.partial(combine_kernel, weights), out_shape=jax....  5.03 us
    ppermute x2, starting transfers between devices, halo_pair(): lax.ppermute(lax.slice_in_dim(block, size - width, size, axis=dim), axis,...  3.83 us
  transfers between devices with their start and end apart: 5, of which 1 were waited for; matrix products, arithmetic and copies ran while one was open for 3% of the time, Pallas kernels for 6%

profile of v12, /device:TPU:4, one launch (start us, length us, event | category | flops | bytes accessed | tf_op | source)
XLA Modules:
  0.0 172.3 jit_solution(10376973139703166990)
XLA Ops:
  0.0 0.9 broadcast_in_dim.6
  0.9 0.7 slice-done
  1.6 0.4 pad_maximum_fusion.1
  2.0 1.9 %collective-permute-start.3 = (f32[2,33,2,1024]{3,2,1,0:T(2,128)S(1)}, f32[2,33,2,1024]{3,2,1,0:T(2,128)S(1)}, u32[]{:S(2)}, u32[]{:S(2)}) collective-permute-start(f32[2,33,2,1024]{3,2,1,0:T(2,128)S(1)} %get-tuple-element.8), channel_id=1, source_target_pairs={{0,1},{1,2},{2,3},{3,4},{4,5},{5,6},{6,7},{7,8},{8,9},{9,10},{10,1... | collective-permute-start | bytes 1622024 | tf_op jit(solution)/shard_map/ppermute | solution.py:45
  3.9 3.6 %collective-permute-start.2 = (f32[2,33,2,1024]{3,2,1,0:T(2,128)S(1)}, f32[2,33,2,1024]{3,2,1,0:T(2,128)S(1)}, u32[]{:S(2)}, u32[]{:S(2)}) collective-permute-start(f32[2,33,2,1024]{3,2,1,0:T(2,128)S(1)} %get-tuple-element.7), channel_id=1, source_target_pairs={{1,0},{2,1},{3,2},{4,3},{5,4},{6,5},{7,6},{8,7},{9,8},{10,9},{11,1... | collective-permute-start | bytes 1622024 | tf_op jit(solution)/shard_map/ppermute | solution.py:46
  7.6 1.4 fusion.9
  8.9 1.9 %collective-permute-start = (f32[2,32,2,1024]{3,2,1,0:T(2,128)}, f32[2,32,2,1024]{3,2,1,0:T(2,128)S(1)}, u32[]{:S(2)}, u32[]{:S(2)}) collective-permute-start(f32[2,32,2,1024]{3,2,1,0:T(2,128)} %get-tuple-element.6), channel_id=1, source_target_pairs={{0,1},{1,2},{2,3},{3,4},{4,5},{5,6},{6,7},{7,8},{8,9},{9,10},{10,1... | collective-permute-start | bytes 1572872 | tf_op jit(solution)/shard_map/ppermute | solution.py:45
  10.9 3.6 %collective-permute-start.1 = (f32[2,32,2,1024]{3,2,1,0:T(2,128)}, f32[2,32,2,1024]{3,2,1,0:T(2,128)}, u32[]{:S(2)}, u32[]{:S(2)}) collective-permute-start(f32[2,32,2,1024]{3,2,1,0:T(2,128)} %get-tuple-element.5), channel_id=1, source_target_pairs={{1,0},{2,1},{3,2},{4,3},{5,4},{6,5},{7,6},{8,7},{9,8},{10,9},{11,1... | collective-permute-start | bytes 1572872 | tf_op jit(solution)/shard_map/ppermute | solution.py:46
  14.6 0.1 fusion.8
  14.7 0.1 maximum_maximum_fusion
  14.8 0.1 fusion.10
  15.1 0.8 pad_maximum_fusion.3
  15.8 0.6 fusion.11
  16.5 0.8 pad_maximum_fusion.2.diff_ref
  17.3 0.7 broadcast_in_dim.8.mask_ref
  18.0 10.2 %shard_map.28.rest_2_ = f32[8,512,128]{2,1,0:T(8,128)} custom-call(f32[2,32]{1,0:T(2,128)} %get-tuple-element.13.lam_ref, f32[2,64,8,1024]{3,2,1,0:T(8,128)} %rhs_ref.3, f32[2,33,2,1024]{3,2,1,0:T(2,128)} %copy-done.1, f32[2,33,2,1024]{3,2,1,0:T(2,128)} %copy-done.2, f32[16,1024]{1,0:T(8,128)} %pad_maximum_fusion.2.diff_ref, f32[16,1024]{1,0:T(8,128)} %broadcast_in_dim.8.mask_ref), custom_call_target="tpu_custom_call" | custom-call | flops 104857600 | bytes 4194304 | tf_op jit(solution)/shard_map/pallas_call | solution.py:157
  28.2 0.8 copy-done.3
  29.0 15.1 %shard_map.29 = f32[8,1024,128]{2,1,0:T(8,128)} custom-call(f32[2,32]{1,0:T(2,128)} %get-tuple-element.14.lam_ref, f32[2,64,8,1024]{3,2,1,0:T(8,128)} %rhs_ref.3, f32[2,32,2,1024]{3,2,1,0:T(2,128)} %copy-done.3, f32[2,32,2,1024]{3,2,1,0:T(2,128)} %collective-permute-done.1.bot_ref, f32[16,1024]{1,0:T(8,128)} %pad_maximum_fusion.2.diff_ref, ...), custom_call_target="tpu_custom_call" | custom-call | flops 104857600 | bytes 4194304 | tf_op jit(solution)/shard_map/pallas_call | solution.py:157
  44.1 5.8 %all-to-all-start = ((f32[8,2,512,128]{3,2,1,0:T(8,128)}), f32[8,2,512,128]{3,2,1,0:T(8,128)}, u32[]{:S(2)}, u32[]{:S(2)}) async-start(f32[8,2,512,128]{3,2,1,0:T(8,128)} %bitcast.12), calls=%async_computation | async-start | bytes 8388608 | tf_op jit(solution)/shard_map/all_to_all | solution.py:288
  49.9 0.7 exponential_multiply_fusion.fac_ref
  50.6 48.7 %all-to-all-done.a_ref = f32[8,2,512,128]{3,2,1,0:T(8,128)} async-done(((f32[8,2,512,128]{3,2,1,0:T(8,128)}), f32[8,2,512,128]{3,2,1,0:T(8,128)}, u32[]{:S(2)}, u32[]{:S(2)}) %all-to-all-start) | async-done | bytes 4194336 | tf_op jit(solution)/shard_map/all_to_all | solution.py:288
  99.4 5.0 %shard_map.30 = f32[8,2,512,128]{3,2,1,0:T(8,128)} custom-call(f32[8,64]{1,0:T(8,128)} %exponential_multiply_fusion.fac_ref, f32[8,2,512,128]{3,2,1,0:T(8,128)} %all-to-all-done.a_ref), custom_call_target="tpu_custom_call" | custom-call | flops 41943040 | bytes 8388608 | tf_op jit(solution)/shard_map/pallas_call | solution.py:212
  104.4 65.3 %all_to_all.10 = f32[8,2,512,128]{3,2,1,0:T(8,128)S(1)} all-to-all(f32[8,2,512,128]{3,2,1,0:T(8,128)} %shard_map.30), channel_id=1, replica_groups=mesh['tm'=8,'space'=16] {'tm'}, dimensions={0} | all-to-all | bytes 8388608 | tf_op jit(solution)/shard_map/all_to_all | solution.py:296
  169.7 2.6 %copy_bitcast_fusion = f32[2,64,8,1024]{3,2,1,0:T(8,128)} fusion(f32[8,2,512,128]{3,2,1,0:T(8,128)S(1)} %all_to_all.10), kind=kLoop, calls=%fused_computation | loop fusion | bytes 8388608 | tf_op jit(solution)/shard_map/reshape | solution.py:298
  (23 shorter events, 0.2 us)
Async XLA Ops:
  0.0 1.6 slice-start
  0.0 7.6 %copy-start = (f32[2,64,8,1024]{3,2,1,0:T(8,128)S(1)}, f32[2,64,8,1024]{3,2,1,0:T(8,128)}, u32[]{:S(2)}) copy-start(f32[2,64,8,1024]{3,2,1,0:T(8,128)} %rhs_ref.3) | copy-start | bytes 12582916
  0.0 16.5 %copy-start.4 = (f32[8,1024]{1,0:T(8,128)S(1)}, f32[8,1024]{1,0:T(8,128)}, u32[]{:S(2)}) copy-start(f32[8,1024]{1,0:T(8,128)} %param.3) | copy-start | bytes 98308
  2.0 14.4 %collective-permute-start.3 = (f32[2,33,2,1024]{3,2,1,0:T(2,128)S(1)}, f32[2,33,2,1024]{3,2,1,0:T(2,128)S(1)}, u32[]{:S(2)}, u32[]{:S(2)}) collective-permute-start(f32[2,33,2,1024]{3,2,1,0:T(2,128)S(1)} %get-tuple-element.8), channel_id=1, source_target_pairs={{0,1},{1,2},{2,3},{3,4},{4,5},{5,6},{6,7},{7,8},{8,9},{9,10},{10,1... | collective-permute-start | bytes 1622024 | tf_op jit(solution)/shard_map/ppermute | solution.py:45
  3.9 12.5 %collective-permute-start.2 = (f32[2,33,2,1024]{3,2,1,0:T(2,128)S(1)}, f32[2,33,2,1024]{3,2,1,0:T(2,128)S(1)}, u32[]{:S(2)}, u32[]{:S(2)}) collective-permute-start(f32[2,33,2,1024]{3,2,1,0:T(2,128)S(1)} %get-tuple-element.7), channel_id=1, source_target_pairs={{1,0},{2,1},{3,2},{4,3},{5,4},{6,5},{7,6},{8,7},{9,8},{10,9},{11,1... | collective-permute-start | bytes 1622024 | tf_op jit(solution)/shard_map/ppermute | solution.py:46
  8.9 19.3 %collective-permute-start = (f32[2,32,2,1024]{3,2,1,0:T(2,128)}, f32[2,32,2,1024]{3,2,1,0:T(2,128)S(1)}, u32[]{:S(2)}, u32[]{:S(2)}) collective-permute-start(f32[2,32,2,1024]{3,2,1,0:T(2,128)} %get-tuple-element.6), channel_id=1, source_target_pairs={{0,1},{1,2},{2,3},{3,4},{4,5},{5,6},{6,7},{7,8},{8,9},{9,10},{10,1... | collective-permute-start | bytes 1572872 | tf_op jit(solution)/shard_map/ppermute | solution.py:45
  10.9 17.4 %collective-permute-start.1 = (f32[2,32,2,1024]{3,2,1,0:T(2,128)}, f32[2,32,2,1024]{3,2,1,0:T(2,128)}, u32[]{:S(2)}, u32[]{:S(2)}) collective-permute-start(f32[2,32,2,1024]{3,2,1,0:T(2,128)} %get-tuple-element.5), channel_id=1, source_target_pairs={{1,0},{2,1},{3,2},{4,3},{5,4},{6,5},{7,6},{8,7},{9,8},{10,9},{11,1... | collective-permute-start | bytes 1572872 | tf_op jit(solution)/shard_map/ppermute | solution.py:46
  16.4 1.6 copy-start.1
  16.5 1.6 copy-start.2
  28.2 0.8 copy-start.3
  44.1 55.2 %all-to-all-start = ((f32[8,2,512,128]{3,2,1,0:T(8,128)}), f32[8,2,512,128]{3,2,1,0:T(8,128)}, u32[]{:S(2)}, u32[]{:S(2)}) async-start(f32[8,2,512,128]{3,2,1,0:T(8,128)} %bitcast.12), calls=%async_computation | async-start | bytes 8388608 | tf_op jit(solution)/shard_map/all_to_all | solution.py:288

commit v13 on v12

--- a/solution.py
+++ b/solution.py
@@ -87,23 +87,25 @@
         inv_mag = 1.0 / (dr * dr + lam_i * lam_i)
         r_re = frame(0, f)
         r_im = frame(1, f)
-        c_re = sweep_weights[0] * ((r_re * dr + r_im * lam_i) * inv_mag)
-        c_im = sweep_weights[0] * ((r_im * dr - r_re * lam_i) * inv_mag)
+        g_re = (r_re * dr + r_im * lam_i) * inv_mag
+        g_im = (r_im * dr - r_re * lam_i) * inv_mag
+        c_re = sweep_weights[0] * g_re
+        c_im = sweep_weights[0] * g_im
         for order in (1, 2):
             n_re, b_re = around(c_re)
             n_im, b_im = around(c_im)
             if order == 2:
                 n_re, b_re, n_im, b_im = n_re[0:8], b_re[0:8], n_im[0:8], b_im[0:8]
-                c_re, c_im, r_re, r_im = c_re[0:8], c_im[0:8], r_re[0:8], r_im[0:8]
+                c_re, c_im, g_re, g_im = c_re[0:8], c_im[0:8], g_re[0:8], g_im[0:8]
                 dr, inv_mag, d = dr[0:8], inv_mag[0:8], diff[0:8]
             else:
                 d = diff
-            a_re = dr * c_re - lam_i * c_im - d * b_re - flow_speed * n_re
-            a_im = dr * c_im + lam_i * c_re - d * b_im - flow_speed * n_im
-            s_re = r_re - a_re
-            s_im = r_im - a_im
-            c_re = c_re + sweep_weights[order] * ((s_re * dr + s_im * lam_i) * inv_mag)
-            c_im = c_im + sweep_weights[order] * ((s_im * dr - s_re * lam_i) * inv_mag)
+            weight = sweep_weights[order]
+            t_re = d * b_re + flow_speed * n_re
+            t_im = d * b_im + flow_speed * n_im
+            scaled = weight * inv_mag
+            c_re = c_re + weight * (g_re - c_re) + (t_re * dr + t_im * lam_i) * scaled
+            c_im = c_im + weight * (g_im - c_im) + (t_im * dr - t_re * lam_i) * scaled
             if order == 1:
                 c_re = c_re * keep
                 c_im = c_im * keep

time: 174 us -> 174 us (level)
  no operation moved by 1% of the time
where the time goes in v13:
time: 174 us; the launch traced here: 172 us
  blocking collectives  65.3 us (38%)
  waiting for transfers between devices  48.8 us (28%)
  Pallas kernels  29.8 us (17%)
  starting transfers between devices  16.9 us (10%)
  local copies, waits for them, and re-layouts  7.86 us (5%)
  other arithmetic  2.96 us (2%)
    all_to_all x1, blocking collectives, on_device(): returned = lax.all_to_all(combined, 'tm', 0, 0, tiled=True)  65.3 us
    all_to_all x1, waiting for transfers between devices, on_device(): arrived = lax.all_to_all(outgoing, 'tm', 0, 0, tiled=True)  48.7 us
    pallas_call x2, Pallas kernels, sweep_call(): pl.pallas_call(functools.partial(sweep_kernel, final is not None), out_sh...  24.8 us
    ppermute x2, starting transfers between devices, halo_pair(): lax.ppermute(lax.slice_in_dim(block, 0, width, axis=dim), axis, backward)  7.29 us
    all_to_all x1, starting transfers between devices, on_device(): arrived = lax.all_to_all(outgoing, 'tm', 0, 0, tiled=True)  5.82 us
    pallas_call x1, Pallas kernels, combine_call(): pl.pallas_call(functools.partial(combine_kernel, weights), out_shape=jax....  5.03 us
    ppermute x2, starting transfers between devices, halo_pair(): lax.ppermute(lax.slice_in_dim(block, size - width, size, axis=dim), axis,...  3.83 us
  transfers between devices with their start and end apart: 5, of which 1 were waited for; matrix products, arithmetic and copies ran while one was open for 3% of the time, Pallas kernels for 6%

profile of v13, /device:TPU:4, one launch (start us, length us, event | category | flops | bytes accessed | tf_op | source)
XLA Modules:
  0.0 171.8 jit_solution(17233028477594452067)
XLA Ops:
  0.0 0.9 broadcast_in_dim.6
  0.9 0.7 slice-done
  1.6 0.4 pad_maximum_fusion.1
  2.0 1.9 %collective-permute-start.3 = (f32[2,33,2,1024]{3,2,1,0:T(2,128)S(1)}, f32[2,33,2,1024]{3,2,1,0:T(2,128)S(1)}, u32[]{:S(2)}, u32[]{:S(2)}) collective-permute-start(f32[2,33,2,1024]{3,2,1,0:T(2,128)S(1)} %get-tuple-element.8), channel_id=1, source_target_pairs={{0,1},{1,2},{2,3},{3,4},{4,5},{5,6},{6,7},{7,8},{8,9},{9,10},{10,1... | collective-permute-start | bytes 1622024 | tf_op jit(solution)/shard_map/ppermute | solution.py:45
  3.9 3.6 %collective-permute-start.2 = (f32[2,33,2,1024]{3,2,1,0:T(2,128)S(1)}, f32[2,33,2,1024]{3,2,1,0:T(2,128)S(1)}, u32[]{:S(2)}, u32[]{:S(2)}) collective-permute-start(f32[2,33,2,1024]{3,2,1,0:T(2,128)S(1)} %get-tuple-element.7), channel_id=1, source_target_pairs={{1,0},{2,1},{3,2},{4,3},{5,4},{6,5},{7,6},{8,7},{9,8},{10,9},{11,1... | collective-permute-start | bytes 1622024 | tf_op jit(solution)/shard_map/ppermute | solution.py:46
  7.6 1.4 fusion.9
  8.9 1.9 %collective-permute-start = (f32[2,32,2,1024]{3,2,1,0:T(2,128)}, f32[2,32,2,1024]{3,2,1,0:T(2,128)S(1)}, u32[]{:S(2)}, u32[]{:S(2)}) collective-permute-start(f32[2,32,2,1024]{3,2,1,0:T(2,128)} %get-tuple-element.6), channel_id=1, source_target_pairs={{0,1},{1,2},{2,3},{3,4},{4,5},{5,6},{6,7},{7,8},{8,9},{9,10},{10,1... | collective-permute-start | bytes 1572872 | tf_op jit(solution)/shard_map/ppermute | solution.py:45
  10.9 3.6 %collective-permute-start.1 = (f32[2,32,2,1024]{3,2,1,0:T(2,128)}, f32[2,32,2,1024]{3,2,1,0:T(2,128)}, u32[]{:S(2)}, u32[]{:S(2)}) collective-permute-start(f32[2,32,2,1024]{3,2,1,0:T(2,128)} %get-tuple-element.5), channel_id=1, source_target_pairs={{1,0},{2,1},{3,2},{4,3},{5,4},{6,5},{7,6},{8,7},{9,8},{10,9},{11,1... | collective-permute-start | bytes 1572872 | tf_op jit(solution)/shard_map/ppermute | solution.py:46
  14.6 0.1 fusion.8
  14.7 0.1 maximum_maximum_fusion
  14.8 0.1 fusion.10
  15.1 0.8 pad_maximum_fusion.3
  15.8 0.6 fusion.11
  16.5 0.8 pad_maximum_fusion.2.diff_ref
  17.3 0.7 broadcast_in_dim.8.mask_ref
  18.0 9.9 %shard_map.28.rest_2_ = f32[8,512,128]{2,1,0:T(8,128)} custom-call(f32[2,32]{1,0:T(2,128)} %get-tuple-element.13.lam_ref, f32[2,64,8,1024]{3,2,1,0:T(8,128)} %rhs_ref.3, f32[2,33,2,1024]{3,2,1,0:T(2,128)} %copy-done.1, f32[2,33,2,1024]{3,2,1,0:T(2,128)} %copy-done.2, f32[16,1024]{1,0:T(8,128)} %pad_maximum_fusion.2.diff_ref, f32[16,1024]{1,0:T(8,128)} %broadcast_in_dim.8.mask_ref), custom_call_target="tpu_custom_call" | custom-call | flops 104857600 | bytes 4194304 | tf_op jit(solution)/shard_map/pallas_call | solution.py:159
  28.0 0.8 copy-done.3
  28.8 14.9 %shard_map.29 = f32[8,1024,128]{2,1,0:T(8,128)} custom-call(f32[2,32]{1,0:T(2,128)} %get-tuple-element.14.lam_ref, f32[2,64,8,1024]{3,2,1,0:T(8,128)} %rhs_ref.3, f32[2,32,2,1024]{3,2,1,0:T(2,128)} %copy-done.3, f32[2,32,2,1024]{3,2,1,0:T(2,128)} %collective-permute-done.1.bot_ref, f32[16,1024]{1,0:T(8,128)} %pad_maximum_fusion.2.diff_ref, ...), custom_call_target="tpu_custom_call" | custom-call | flops 104857600 | bytes 4194304 | tf_op jit(solution)/shard_map/pallas_call | solution.py:159
  43.6 5.8 %all-to-all-start = ((f32[8,2,512,128]{3,2,1,0:T(8,128)}), f32[8,2,512,128]{3,2,1,0:T(8,128)}, u32[]{:S(2)}, u32[]{:S(2)}) async-start(f32[8,2,512,128]{3,2,1,0:T(8,128)} %bitcast.12), calls=%async_computation | async-start | bytes 8388608 | tf_op jit(solution)/shard_map/all_to_all | solution.py:290
  49.5 0.7 exponential_multiply_fusion.fac_ref
  50.1 48.7 %all-to-all-done.a_ref = f32[8,2,512,128]{3,2,1,0:T(8,128)} async-done(((f32[8,2,512,128]{3,2,1,0:T(8,128)}), f32[8,2,512,128]{3,2,1,0:T(8,128)}, u32[]{:S(2)}, u32[]{:S(2)}) %all-to-all-start) | async-done | bytes 4194336 | tf_op jit(solution)/shard_map/all_to_all | solution.py:290
  98.9 5.0 %shard_map.30 = f32[8,2,512,128]{3,2,1,0:T(8,128)} custom-call(f32[8,64]{1,0:T(8,128)} %exponential_multiply_fusion.fac_ref, f32[8,2,512,128]{3,2,1,0:T(8,128)} %all-to-all-done.a_ref), custom_call_target="tpu_custom_call" | custom-call | flops 41943040 | bytes 8388608 | tf_op jit(solution)/shard_map/pallas_call | solution.py:214
  103.9 65.3 %all_to_all.10 = f32[8,2,512,128]{3,2,1,0:T(8,128)S(1)} all-to-all(f32[8,2,512,128]{3,2,1,0:T(8,128)} %shard_map.30), channel_id=1, replica_groups=mesh['tm'=8,'space'=16] {'tm'}, dimensions={0} | all-to-all | bytes 8388608 | tf_op jit(solution)/shard_map/all_to_all | solution.py:298
  169.2 2.6 %copy_bitcast_fusion = f32[2,64,8,1024]{3,2,1,0:T(8,128)} fusion(f32[8,2,512,128]{3,2,1,0:T(8,128)S(1)} %all_to_all.10), kind=kLoop, calls=%fused_computation | loop fusion | bytes 8388608 | tf_op jit(solution)/shard_map/reshape | solution.py:300
  (23 shorter events, 0.2 us)
Async XLA Ops:
  0.0 1.6 slice-start
  0.0 7.6 %copy-start = (f32[2,64,8,1024]{3,2,1,0:T(8,128)S(1)}, f32[2,64,8,1024]{3,2,1,0:T(8,128)}, u32[]{:S(2)}) copy-start(f32[2,64,8,1024]{3,2,1,0:T(8,128)} %rhs_ref.3) | copy-start | bytes 12582916
  0.0 16.5 %copy-start.4 = (f32[8,1024]{1,0:T(8,128)S(1)}, f32[8,1024]{1,0:T(8,128)}, u32[]{:S(2)}) copy-start(f32[8,1024]{1,0:T(8,128)} %param.3) | copy-start | bytes 98308
  2.0 14.4 %collective-permute-start.3 = (f32[2,33,2,1024]{3,2,1,0:T(2,128)S(1)}, f32[2,33,2,1024]{3,2,1,0:T(2,128)S(1)}, u32[]{:S(2)}, u32[]{:S(2)}) collective-permute-start(f32[2,33,2,1024]{3,2,1,0:T(2,128)S(1)} %get-tuple-element.8), channel_id=1, source_target_pairs={{0,1},{1,2},{2,3},{3,4},{4,5},{5,6},{6,7},{7,8},{8,9},{9,10},{10,1... | collective-permute-start | bytes 1622024 | tf_op jit(solution)/shard_map/ppermute | solution.py:45
  3.9 12.5 %collective-permute-start.2 = (f32[2,33,2,1024]{3,2,1,0:T(2,128)S(1)}, f32[2,33,2,1024]{3,2,1,0:T(2,128)S(1)}, u32[]{:S(2)}, u32[]{:S(2)}) collective-permute-start(f32[2,33,2,1024]{3,2,1,0:T(2,128)S(1)} %get-tuple-element.7), channel_id=1, source_target_pairs={{1,0},{2,1},{3,2},{4,3},{5,4},{6,5},{7,6},{8,7},{9,8},{10,9},{11,1... | collective-permute-start | bytes 1622024 | tf_op jit(solution)/shard_map/ppermute | solution.py:46
  8.9 19.0 %collective-permute-start = (f32[2,32,2,1024]{3,2,1,0:T(2,128)}, f32[2,32,2,1024]{3,2,1,0:T(2,128)S(1)}, u32[]{:S(2)}, u32[]{:S(2)}) collective-permute-start(f32[2,32,2,1024]{3,2,1,0:T(2,128)} %get-tuple-element.6), channel_id=1, source_target_pairs={{0,1},{1,2},{2,3},{3,4},{4,5},{5,6},{6,7},{7,8},{8,9},{9,10},{10,1... | collective-permute-start | bytes 1572872 | tf_op jit(solution)/shard_map/ppermute | solution.py:45
  10.9 17.1 %collective-permute-start.1 = (f32[2,32,2,1024]{3,2,1,0:T(2,128)}, f32[2,32,2,1024]{3,2,1,0:T(2,128)}, u32[]{:S(2)}, u32[]{:S(2)}) collective-permute-start(f32[2,32,2,1024]{3,2,1,0:T(2,128)} %get-tuple-element.5), channel_id=1, source_target_pairs={{1,0},{2,1},{3,2},{4,3},{5,4},{6,5},{7,6},{8,7},{9,8},{10,9},{11,1... | collective-permute-start | bytes 1572872 | tf_op jit(solution)/shard_map/ppermute | solution.py:46
  16.4 1.6 copy-start.1
  16.5 1.6 copy-start.2
  28.0 0.8 copy-start.3
  43.6 55.2 %all-to-all-start = ((f32[8,2,512,128]{3,2,1,0:T(8,128)}), f32[8,2,512,128]{3,2,1,0:T(8,128)}, u32[]{:S(2)}, u32[]{:S(2)}) async-start(f32[8,2,512,128]{3,2,1,0:T(8,128)} %bitcast.12), calls=%async_computation | async-start | bytes 8388608 | tf_op jit(solution)/shard_map/all_to_all | solution.py:290

commit v14 on v13

--- a/solution.py
+++ b/solution.py
@@ -15,7 +15,7 @@
 sweep_weights = [
     1.0 / (1.0 + 0.7 * math.cos(math.pi * (2 * order + 1) / 6.0)) for order in range(3)
 ]
-Q_BLOCK = 16
+Q_BLOCK = 32
 F_BLOCK = 16
 SWEEP_UNROLL = 4
 HALO = 2

time: 174 us -> 173 us (level)
  no operation moved by 1% of the time
where the time goes in v14:
time: 173 us; the launch traced here: 171 us
  blocking collectives  65.3 us (38%)
  waiting for transfers between devices  48.8 us (28%)
  Pallas kernels  28.9 us (17%)
  starting transfers between devices  16.9 us (10%)
  local copies, waits for them, and re-layouts  7.86 us (5%)
  other arithmetic  2.96 us (2%)
    all_to_all x1, blocking collectives, on_device(): returned = lax.all_to_all(combined, 'tm', 0, 0, tiled=True)  65.3 us
    all_to_all x1, waiting for transfers between devices, on_device(): arrived = lax.all_to_all(outgoing, 'tm', 0, 0, tiled=True)  48.7 us
    pallas_call x2, Pallas kernels, sweep_call(): pl.pallas_call(functools.partial(sweep_kernel, final is not None), out_sh...  24.8 us
    ppermute x2, starting transfers between devices, halo_pair(): lax.ppermute(lax.slice_in_dim(block, 0, width, axis=dim), axis, backward)  7.29 us
    all_to_all x1, starting transfers between devices, on_device(): arrived = lax.all_to_all(outgoing, 'tm', 0, 0, tiled=True)  5.82 us
    pallas_call x1, Pallas kernels, combine_call(): pl.pallas_call(functools.partial(combine_kernel, weights), out_shape=jax....  4.07 us
    ppermute x2, starting transfers between devices, halo_pair(): lax.ppermute(lax.slice_in_dim(block, size - width, size, axis=dim), axis,...  3.83 us
  transfers between devices with their start and end apart: 5, of which 1 were waited for; matrix products, arithmetic and copies ran while one was open for 3% of the time, Pallas kernels for 6%

profile of v14, /device:TPU:4, one launch (start us, length us, event | category | flops | bytes accessed | tf_op | source)
XLA Modules:
  0.0 170.8 jit_solution(14818657301576320253)
XLA Ops:
  0.0 0.9 broadcast_in_dim.6
  0.9 0.7 slice-done
  1.6 0.4 pad_maximum_fusion.1
  2.0 1.9 %collective-permute-start.3 = (f32[2,33,2,1024]{3,2,1,0:T(2,128)S(1)}, f32[2,33,2,1024]{3,2,1,0:T(2,128)S(1)}, u32[]{:S(2)}, u32[]{:S(2)}) collective-permute-start(f32[2,33,2,1024]{3,2,1,0:T(2,128)S(1)} %get-tuple-element.8), channel_id=1, source_target_pairs={{0,1},{1,2},{2,3},{3,4},{4,5},{5,6},{6,7},{7,8},{8,9},{9,10},{10,1... | collective-permute-start | bytes 1622024 | tf_op jit(solution)/shard_map/ppermute | solution.py:45
  3.9 3.6 %collective-permute-start.2 = (f32[2,33,2,1024]{3,2,1,0:T(2,128)S(1)}, f32[2,33,2,1024]{3,2,1,0:T(2,128)S(1)}, u32[]{:S(2)}, u32[]{:S(2)}) collective-permute-start(f32[2,33,2,1024]{3,2,1,0:T(2,128)S(1)} %get-tuple-element.7), channel_id=1, source_target_pairs={{1,0},{2,1},{3,2},{4,3},{5,4},{6,5},{7,6},{8,7},{9,8},{10,9},{11,1... | collective-permute-start | bytes 1622024 | tf_op jit(solution)/shard_map/ppermute | solution.py:46
  7.6 1.4 fusion.9
  8.9 1.9 %collective-permute-start = (f32[2,32,2,1024]{3,2,1,0:T(2,128)}, f32[2,32,2,1024]{3,2,1,0:T(2,128)S(1)}, u32[]{:S(2)}, u32[]{:S(2)}) collective-permute-start(f32[2,32,2,1024]{3,2,1,0:T(2,128)} %get-tuple-element.6), channel_id=1, source_target_pairs={{0,1},{1,2},{2,3},{3,4},{4,5},{5,6},{6,7},{7,8},{8,9},{9,10},{10,1... | collective-permute-start | bytes 1572872 | tf_op jit(solution)/shard_map/ppermute | solution.py:45
  10.9 3.6 %collective-permute-start.1 = (f32[2,32,2,1024]{3,2,1,0:T(2,128)}, f32[2,32,2,1024]{3,2,1,0:T(2,128)}, u32[]{:S(2)}, u32[]{:S(2)}) collective-permute-start(f32[2,32,2,1024]{3,2,1,0:T(2,128)} %get-tuple-element.5), channel_id=1, source_target_pairs={{1,0},{2,1},{3,2},{4,3},{5,4},{6,5},{7,6},{8,7},{9,8},{10,9},{11,1... | collective-permute-start | bytes 1572872 | tf_op jit(solution)/shard_map/ppermute | solution.py:46
  14.6 0.1 fusion.8
  14.7 0.1 maximum_maximum_fusion
  14.8 0.1 fusion.10
  15.1 0.8 pad_maximum_fusion.3
  15.8 0.6 fusion.11
  16.5 0.8 pad_maximum_fusion.2.diff_ref
  17.3 0.7 broadcast_in_dim.8.mask_ref
  18.0 9.9 %shard_map.28.rest_2_ = f32[8,512,128]{2,1,0:T(8,128)} custom-call(f32[2,32]{1,0:T(2,128)} %get-tuple-element.13.lam_ref, f32[2,64,8,1024]{3,2,1,0:T(8,128)} %rhs_ref.3, f32[2,33,2,1024]{3,2,1,0:T(2,128)} %copy-done.1, f32[2,33,2,1024]{3,2,1,0:T(2,128)} %copy-done.2, f32[16,1024]{1,0:T(8,128)} %pad_maximum_fusion.2.diff_ref, f32[16,1024]{1,0:T(8,128)} %broadcast_in_dim.8.mask_ref), custom_call_target="tpu_custom_call" | custom-call | flops 104857600 | bytes 4194304 | tf_op jit(solution)/shard_map/pallas_call | solution.py:159
  28.0 0.8 copy-done.3
  28.8 14.9 %shard_map.29 = f32[8,1024,128]{2,1,0:T(8,128)} custom-call(f32[2,32]{1,0:T(2,128)} %get-tuple-element.14.lam_ref, f32[2,64,8,1024]{3,2,1,0:T(8,128)} %rhs_ref.3, f32[2,32,2,1024]{3,2,1,0:T(2,128)} %copy-done.3, f32[2,32,2,1024]{3,2,1,0:T(2,128)} %collective-permute-done.1.bot_ref, f32[16,1024]{1,0:T(8,128)} %pad_maximum_fusion.2.diff_ref, ...), custom_call_target="tpu_custom_call" | custom-call | flops 104857600 | bytes 4194304 | tf_op jit(solution)/shard_map/pallas_call | solution.py:159
  43.6 5.8 %all-to-all-start = ((f32[8,2,512,128]{3,2,1,0:T(8,128)}), f32[8,2,512,128]{3,2,1,0:T(8,128)}, u32[]{:S(2)}, u32[]{:S(2)}) async-start(f32[8,2,512,128]{3,2,1,0:T(8,128)} %bitcast.12), calls=%async_computation | async-start | bytes 8388608 | tf_op jit(solution)/shard_map/all_to_all | solution.py:290
  49.5 0.7 exponential_multiply_fusion.fac_ref
  50.1 48.7 %all-to-all-done.a_ref = f32[8,2,512,128]{3,2,1,0:T(8,128)} async-done(((f32[8,2,512,128]{3,2,1,0:T(8,128)}), f32[8,2,512,128]{3,2,1,0:T(8,128)}, u32[]{:S(2)}, u32[]{:S(2)}) %all-to-all-start) | async-done | bytes 4194336 | tf_op jit(solution)/shard_map/all_to_all | solution.py:290
  98.9 4.1 %shard_map.30 = f32[8,2,512,128]{3,2,1,0:T(8,128)} custom-call(f32[8,64]{1,0:T(8,128)} %exponential_multiply_fusion.fac_ref, f32[8,2,512,128]{3,2,1,0:T(8,128)} %all-to-all-done.a_ref), custom_call_target="tpu_custom_call" | custom-call | flops 41943040 | bytes 8388608 | tf_op jit(solution)/shard_map/pallas_call | solution.py:214
  102.9 65.3 %all_to_all.10 = f32[8,2,512,128]{3,2,1,0:T(8,128)S(1)} all-to-all(f32[8,2,512,128]{3,2,1,0:T(8,128)} %shard_map.30), channel_id=1, replica_groups=mesh['tm'=8,'space'=16] {'tm'}, dimensions={0} | all-to-all | bytes 8388608 | tf_op jit(solution)/shard_map/all_to_all | solution.py:298
  168.2 2.6 %copy_bitcast_fusion = f32[2,64,8,1024]{3,2,1,0:T(8,128)} fusion(f32[8,2,512,128]{3,2,1,0:T(8,128)S(1)} %all_to_all.10), kind=kLoop, calls=%fused_computation | loop fusion | bytes 8388608 | tf_op jit(solution)/shard_map/reshape | solution.py:300
  (23 shorter events, 0.2 us)
Async XLA Ops:
  0.0 1.6 slice-start
  0.0 7.6 %copy-start = (f32[2,64,8,1024]{3,2,1,0:T(8,128)S(1)}, f32[2,64,8,1024]{3,2,1,0:T(8,128)}, u32[]{:S(2)}) copy-start(f32[2,64,8,1024]{3,2,1,0:T(8,128)} %rhs_ref.3) | copy-start | bytes 12582916
  0.0 16.5 %copy-start.4 = (f32[8,1024]{1,0:T(8,128)S(1)}, f32[8,1024]{1,0:T(8,128)}, u32[]{:S(2)}) copy-start(f32[8,1024]{1,0:T(8,128)} %param.3) | copy-start | bytes 98308
  2.0 14.4 %collective-permute-start.3 = (f32[2,33,2,1024]{3,2,1,0:T(2,128)S(1)}, f32[2,33,2,1024]{3,2,1,0:T(2,128)S(1)}, u32[]{:S(2)}, u32[]{:S(2)}) collective-permute-start(f32[2,33,2,1024]{3,2,1,0:T(2,128)S(1)} %get-tuple-element.8), channel_id=1, source_target_pairs={{0,1},{1,2},{2,3},{3,4},{4,5},{5,6},{6,7},{7,8},{8,9},{9,10},{10,1... | collective-permute-start | bytes 1622024 | tf_op jit(solution)/shard_map/ppermute | solution.py:45
  3.9 12.5 %collective-permute-start.2 = (f32[2,33,2,1024]{3,2,1,0:T(2,128)S(1)}, f32[2,33,2,1024]{3,2,1,0:T(2,128)S(1)}, u32[]{:S(2)}, u32[]{:S(2)}) collective-permute-start(f32[2,33,2,1024]{3,2,1,0:T(2,128)S(1)} %get-tuple-element.7), channel_id=1, source_target_pairs={{1,0},{2,1},{3,2},{4,3},{5,4},{6,5},{7,6},{8,7},{9,8},{10,9},{11,1... | collective-permute-start | bytes 1622024 | tf_op jit(solution)/shard_map/ppermute | solution.py:46
  8.9 19.0 %collective-permute-start = (f32[2,32,2,1024]{3,2,1,0:T(2,128)}, f32[2,32,2,1024]{3,2,1,0:T(2,128)S(1)}, u32[]{:S(2)}, u32[]{:S(2)}) collective-permute-start(f32[2,32,2,1024]{3,2,1,0:T(2,128)} %get-tuple-element.6), channel_id=1, source_target_pairs={{0,1},{1,2},{2,3},{3,4},{4,5},{5,6},{6,7},{7,8},{8,9},{9,10},{10,1... | collective-permute-start | bytes 1572872 | tf_op jit(solution)/shard_map/ppermute | solution.py:45
  10.9 17.1 %collective-permute-start.1 = (f32[2,32,2,1024]{3,2,1,0:T(2,128)}, f32[2,32,2,1024]{3,2,1,0:T(2,128)}, u32[]{:S(2)}, u32[]{:S(2)}) collective-permute-start(f32[2,32,2,1024]{3,2,1,0:T(2,128)} %get-tuple-element.5), channel_id=1, source_target_pairs={{1,0},{2,1},{3,2},{4,3},{5,4},{6,5},{7,6},{8,7},{9,8},{10,9},{11,1... | collective-permute-start | bytes 1572872 | tf_op jit(solution)/shard_map/ppermute | solution.py:46
  16.4 1.6 copy-start.1
  16.5 1.6 copy-start.2
  28.0 0.8 copy-start.3
  43.6 55.2 %all-to-all-start = ((f32[8,2,512,128]{3,2,1,0:T(8,128)}), f32[8,2,512,128]{3,2,1,0:T(8,128)}, u32[]{:S(2)}, u32[]{:S(2)}) async-start(f32[8,2,512,128]{3,2,1,0:T(8,128)} %bitcast.12), calls=%async_computation | async-start | bytes 8388608 | tf_op jit(solution)/shard_map/all_to_all | solution.py:290

commit v15 on v14

--- a/solution.py
+++ b/solution.py
@@ -49,7 +49,7 @@
 
 def sweep_kernel(final, lam_ref, rhs_ref, top_ref, bot_ref, diff_ref, mask_ref, *rest):
     if final:
-        low_ref, high_ref, prev_ref, o_ref, field = rest
+        low_ref, prev_ref, o_ref, field = rest
     else:
         (o_ref,) = rest
         field = o_ref
@@ -123,16 +123,16 @@
 
     @pl.when(pl.program_id(0) == pl.num_programs(0) - 1)
     def _():
-        low = low_ref[...]
-        high = high_ref[...]
+        table = low_ref[...]
         rows_out = o_ref.shape[1] // 8
         for blk in range(o_ref.shape[0]):
             for r in range(8):
                 first = prev_ref[blk, pl.ds(r, 2 * count, stride=8), :]
                 second = field[blk, pl.ds(r, 2 * count, stride=8), :]
                 o_ref[blk, pl.ds(r, rows_out, stride=8), :] = jnp.dot(
-                    low, first, precision=lax.Precision.HIGH, preferred_element_type=jnp.float32
-                ) + jnp.dot(high, second, precision=lax.Precision.HIGH, preferred_element_type=jnp.float32)
+                    table, jnp.concatenate([first, second], axis=0),
+                    precision=lax.Precision.HIGH, preferred_element_type=jnp.float32,
+                )
 
 
 def sweep_call(lam, spectrum, offset, top, bottom, diff_frame, mask_frame, blocks, final=None):
@@ -150,10 +150,9 @@
     scratch = []
     out_rows = field_rows
     if final is not None:
-        low, high, prev = final
-        half = pl.BlockSpec(low.shape, lambda g: (0, 0))
-        in_specs += [half, half, pl.BlockSpec(prev.shape, lambda g: (0, 0, 0))]
-        operands += [low, high, prev]
+        table, prev = final
+        in_specs += [pl.BlockSpec(table.shape, lambda g: (0, 0)), pl.BlockSpec(prev.shape, lambda g: (0, 0, 0))]
+        operands += [table, prev]
         scratch = [pltpu.VMEM((blocks, field_rows, width), jnp.float32)]
         out_rows = 2 * total * rows
     return pl.pallas_call(
@@ -283,7 +282,7 @@
     first = sweep_call(lam[:, :half], spectrum, 0, top_a, bottom_a, diff_frame, mask_frame, tm_count)
     outgoing = sweep_call(
         lam[:, half:], spectrum, half, top_b, bottom_b, diff_frame, mask_frame, tm_count,
-        final=(low, high, first),
+        final=(jnp.concatenate([low, high], 1), first),
     )
     col_block = col_count // tm_count
     outgoing = outgoing.reshape(tm_count, 2, local_count * row_count, col_block)

time: 173 us -> 171 us (0.988)
  no operation moved by 1% of the time
where the time goes in v15:
time: 171 us; the launch traced here: 169 us
  blocking collectives  65.3 us (38%)
  waiting for transfers between devices  48.8 us (29%)
  Pallas kernels  27.2 us (16%)
  starting transfers between devices  16.9 us (10%)
  local copies, waits for them, and re-layouts  7.89 us (5%)
  other arithmetic  2.95 us (2%)
    all_to_all x1, blocking collectives, on_device(): returned = lax.all_to_all(combined, 'tm', 0, 0, tiled=True)  65.3 us
    all_to_all x1, waiting for transfers between devices, on_device(): arrived = lax.all_to_all(outgoing, 'tm', 0, 0, tiled=True)  48.7 us
    pallas_call x2, Pallas kernels, sweep_call(): pl.pallas_call(functools.partial(sweep_kernel, final is not None), out_sh...  23.2 us
    ppermute x2, starting transfers between devices, halo_pair(): lax.ppermute(lax.slice_in_dim(block, 0, width, axis=dim), axis, backward)  7.29 us
    all_to_all x1, starting transfers between devices, on_device(): arrived = lax.all_to_all(outgoing, 'tm', 0, 0, tiled=True)  5.82 us
    pallas_call x1, Pallas kernels, combine_call(): pl.pallas_call(functools.partial(combine_kernel, weights), out_shape=jax....  4.07 us
    ppermute x2, starting transfers between devices, halo_pair(): lax.ppermute(lax.slice_in_dim(block, size - width, size, axis=dim), axis,...  3.83 us
  transfers between devices with their start and end apart: 5, of which 1 were waited for; matrix products, arithmetic and copies ran while one was open for 3% of the time, Pallas kernels for 6%

profile of v15, /device:TPU:4, one launch (start us, length us, event | category | flops | bytes accessed | tf_op | source)
XLA Modules:
  0.0 169.2 jit_solution(7562972521565671660)
XLA Ops:
  0.0 0.9 broadcast_in_dim.6
  0.9 0.7 slice-done
  1.6 0.4 pad_maximum_fusion.1
  2.0 1.9 %collective-permute-start.3 = (f32[2,33,2,1024]{3,2,1,0:T(2,128)S(1)}, f32[2,33,2,1024]{3,2,1,0:T(2,128)S(1)}, u32[]{:S(2)}, u32[]{:S(2)}) collective-permute-start(f32[2,33,2,1024]{3,2,1,0:T(2,128)S(1)} %get-tuple-element.8), channel_id=1, source_target_pairs={{0,1},{1,2},{2,3},{3,4},{4,5},{5,6},{6,7},{7,8},{8,9},{9,10},{10,1... | collective-permute-start | bytes 1622024 | tf_op jit(solution)/shard_map/ppermute | solution.py:45
  3.9 3.6 %collective-permute-start.2 = (f32[2,33,2,1024]{3,2,1,0:T(2,128)S(1)}, f32[2,33,2,1024]{3,2,1,0:T(2,128)S(1)}, u32[]{:S(2)}, u32[]{:S(2)}) collective-permute-start(f32[2,33,2,1024]{3,2,1,0:T(2,128)S(1)} %get-tuple-element.7), channel_id=1, source_target_pairs={{1,0},{2,1},{3,2},{4,3},{5,4},{6,5},{7,6},{8,7},{9,8},{10,9},{11,1... | collective-permute-start | bytes 1622024 | tf_op jit(solution)/shard_map/ppermute | solution.py:46
  7.6 1.4 fusion.9
  9.0 1.9 %collective-permute-start = (f32[2,32,2,1024]{3,2,1,0:T(2,128)}, f32[2,32,2,1024]{3,2,1,0:T(2,128)S(1)}, u32[]{:S(2)}, u32[]{:S(2)}) collective-permute-start(f32[2,32,2,1024]{3,2,1,0:T(2,128)} %get-tuple-element.6), channel_id=1, source_target_pairs={{0,1},{1,2},{2,3},{3,4},{4,5},{5,6},{6,7},{7,8},{8,9},{9,10},{10,1... | collective-permute-start | bytes 1572872 | tf_op jit(solution)/shard_map/ppermute | solution.py:45
  10.9 3.6 %collective-permute-start.1 = (f32[2,32,2,1024]{3,2,1,0:T(2,128)}, f32[2,32,2,1024]{3,2,1,0:T(2,128)}, u32[]{:S(2)}, u32[]{:S(2)}) collective-permute-start(f32[2,32,2,1024]{3,2,1,0:T(2,128)} %get-tuple-element.5), channel_id=1, source_target_pairs={{1,0},{2,1},{3,2},{4,3},{5,4},{6,5},{7,6},{8,7},{9,8},{10,9},{11,1... | collective-permute-start | bytes 1572872 | tf_op jit(solution)/shard_map/ppermute | solution.py:46
  14.6 0.1 fusion.8
  14.8 0.1 maximum_maximum_fusion
  14.9 0.1 fusion.10
  15.1 0.7 pad_maximum_fusion.3.rest_0_
  15.8 0.6 fusion.11
  16.5 0.8 pad_maximum_fusion.2.diff_ref
  17.4 0.7 broadcast_in_dim.8.mask_ref
  18.0 9.9 %shard_map.28.rest_1_ = f32[8,512,128]{2,1,0:T(8,128)} custom-call(f32[2,32]{1,0:T(2,128)} %get-tuple-element.13.lam_ref, f32[2,64,8,1024]{3,2,1,0:T(8,128)} %rhs_ref.3, f32[2,33,2,1024]{3,2,1,0:T(2,128)} %copy-done.1, f32[2,33,2,1024]{3,2,1,0:T(2,128)} %copy-done.2, f32[16,1024]{1,0:T(8,128)} %pad_maximum_fusion.2.diff_ref, f32[16,1024]{1,0:T(8,128)} %broadcast_in_dim.8.mask_ref), custom_call_target="tpu_custom_call" | custom-call | flops 104857600 | bytes 4194304 | tf_op jit(solution)/shard_map/pallas_call | solution.py:158
  28.0 0.8 copy-done.3
  28.8 13.2 %shard_map.29 = f32[8,1024,128]{2,1,0:T(8,128)} custom-call(f32[2,32]{1,0:T(2,128)} %get-tuple-element.14.lam_ref, f32[2,64,8,1024]{3,2,1,0:T(8,128)} %rhs_ref.3, f32[2,32,2,1024]{3,2,1,0:T(2,128)} %copy-done.3, f32[2,32,2,1024]{3,2,1,0:T(2,128)} %collective-permute-done.1.bot_ref, f32[16,1024]{1,0:T(8,128)} %pad_maximum_fusion.2.diff_ref, ...), custom_call_target="tpu_custom_call" | custom-call | flops 104857600 | bytes 4194304 | tf_op jit(solution)/shard_map/pallas_call | solution.py:158
  42.0 5.8 %all-to-all-start = ((f32[8,2,512,128]{3,2,1,0:T(8,128)}), f32[8,2,512,128]{3,2,1,0:T(8,128)}, u32[]{:S(2)}, u32[]{:S(2)}) async-start(f32[8,2,512,128]{3,2,1,0:T(8,128)} %bitcast.12), calls=%async_computation | async-start | bytes 8388608 | tf_op jit(solution)/shard_map/all_to_all | solution.py:289
  47.8 0.7 exponential_multiply_fusion.fac_ref
  48.5 48.7 %all-to-all-done.a_ref = f32[8,2,512,128]{3,2,1,0:T(8,128)} async-done(((f32[8,2,512,128]{3,2,1,0:T(8,128)}), f32[8,2,512,128]{3,2,1,0:T(8,128)}, u32[]{:S(2)}, u32[]{:S(2)}) %all-to-all-start) | async-done | bytes 4194336 | tf_op jit(solution)/shard_map/all_to_all | solution.py:289
  97.3 4.1 %shard_map.30 = f32[8,2,512,128]{3,2,1,0:T(8,128)} custom-call(f32[8,64]{1,0:T(8,128)} %exponential_multiply_fusion.fac_ref, f32[8,2,512,128]{3,2,1,0:T(8,128)} %all-to-all-done.a_ref), custom_call_target="tpu_custom_call" | custom-call | flops 41943040 | bytes 8388608 | tf_op jit(solution)/shard_map/pallas_call | solution.py:213
  101.3 65.3 %all_to_all.10 = f32[8,2,512,128]{3,2,1,0:T(8,128)S(1)} all-to-all(f32[8,2,512,128]{3,2,1,0:T(8,128)} %shard_map.30), channel_id=1, replica_groups=mesh['tm'=8,'space'=16] {'tm'}, dimensions={0} | all-to-all | bytes 8388608 | tf_op jit(solution)/shard_map/all_to_all | solution.py:297
  166.6 2.6 %copy_bitcast_fusion = f32[2,64,8,1024]{3,2,1,0:T(8,128)} fusion(f32[8,2,512,128]{3,2,1,0:T(8,128)S(1)} %all_to_all.10), kind=kLoop, calls=%fused_computation | loop fusion | bytes 8388608 | tf_op jit(solution)/shard_map/reshape | solution.py:299
  (23 shorter events, 0.2 us)
Async XLA Ops:
  0.0 1.6 slice-start
  0.0 7.6 %copy-start = (f32[2,64,8,1024]{3,2,1,0:T(8,128)S(1)}, f32[2,64,8,1024]{3,2,1,0:T(8,128)}, u32[]{:S(2)}) copy-start(f32[2,64,8,1024]{3,2,1,0:T(8,128)} %rhs_ref.3) | copy-start | bytes 12582916
  0.0 16.5 %copy-start.4 = (f32[8,1024]{1,0:T(8,128)S(1)}, f32[8,1024]{1,0:T(8,128)}, u32[]{:S(2)}) copy-start(f32[8,1024]{1,0:T(8,128)} %param.3) | copy-start | bytes 98308
  2.0 14.5 %collective-permute-start.3 = (f32[2,33,2,1024]{3,2,1,0:T(2,128)S(1)}, f32[2,33,2,1024]{3,2,1,0:T(2,128)S(1)}, u32[]{:S(2)}, u32[]{:S(2)}) collective-permute-start(f32[2,33,2,1024]{3,2,1,0:T(2,128)S(1)} %get-tuple-element.8), channel_id=1, source_target_pairs={{0,1},{1,2},{2,3},{3,4},{4,5},{5,6},{6,7},{7,8},{8,9},{9,10},{10,1... | collective-permute-start | bytes 1622024 | tf_op jit(solution)/shard_map/ppermute | solution.py:45
  3.9 12.5 %collective-permute-start.2 = (f32[2,33,2,1024]{3,2,1,0:T(2,128)S(1)}, f32[2,33,2,1024]{3,2,1,0:T(2,128)S(1)}, u32[]{:S(2)}, u32[]{:S(2)}) collective-permute-start(f32[2,33,2,1024]{3,2,1,0:T(2,128)S(1)} %get-tuple-element.7), channel_id=1, source_target_pairs={{1,0},{2,1},{3,2},{4,3},{5,4},{6,5},{7,6},{8,7},{9,8},{10,9},{11,1... | collective-permute-start | bytes 1622024 | tf_op jit(solution)/shard_map/ppermute | solution.py:46
  9.0 19.0 %collective-permute-start = (f32[2,32,2,1024]{3,2,1,0:T(2,128)}, f32[2,32,2,1024]{3,2,1,0:T(2,128)S(1)}, u32[]{:S(2)}, u32[]{:S(2)}) collective-permute-start(f32[2,32,2,1024]{3,2,1,0:T(2,128)} %get-tuple-element.6), channel_id=1, source_target_pairs={{0,1},{1,2},{2,3},{3,4},{4,5},{5,6},{6,7},{7,8},{8,9},{9,10},{10,1... | collective-permute-start | bytes 1572872 | tf_op jit(solution)/shard_map/ppermute | solution.py:45
  10.9 17.1 %collective-permute-start.1 = (f32[2,32,2,1024]{3,2,1,0:T(2,128)}, f32[2,32,2,1024]{3,2,1,0:T(2,128)}, u32[]{:S(2)}, u32[]{:S(2)}) collective-permute-start(f32[2,32,2,1024]{3,2,1,0:T(2,128)} %get-tuple-element.5), channel_id=1, source_target_pairs={{1,0},{2,1},{3,2},{4,3},{5,4},{6,5},{7,6},{8,7},{9,8},{10,9},{11,1... | collective-permute-start | bytes 1572872 | tf_op jit(solution)/shard_map/ppermute | solution.py:46
  16.5 1.6 copy-start.1
  16.5 1.6 copy-start.2
  28.0 0.8 copy-start.3
  42.0 55.2 %all-to-all-start = ((f32[8,2,512,128]{3,2,1,0:T(8,128)}), f32[8,2,512,128]{3,2,1,0:T(8,128)}, u32[]{:S(2)}, u32[]{:S(2)}) async-start(f32[8,2,512,128]{3,2,1,0:T(8,128)} %bitcast.12), calls=%async_computation | async-start | bytes 8388608 | tf_op jit(solution)/shard_map/all_to_all | solution.py:289

commit v16 on v15

--- a/solution.py
+++ b/solution.py
@@ -15,7 +15,7 @@
 sweep_weights = [
     1.0 / (1.0 + 0.7 * math.cos(math.pi * (2 * order + 1) / 6.0)) for order in range(3)
 ]
-Q_BLOCK = 32
+Q_BLOCK = 64
 F_BLOCK = 16
 SWEEP_UNROLL = 4
 HALO = 2

time: 171 us -> 172 us (level)
  no operation moved by 1% of the time
where the time goes in v16:
time: 172 us; the launch traced here: 170 us
  blocking collectives  65.3 us (38%)
  waiting for transfers between devices  48.8 us (28%)
  Pallas kernels  28.3 us (16%)
  starting transfers between devices  16.9 us (10%)
  local copies, waits for them, and re-layouts  7.89 us (5%)
  other arithmetic  2.95 us (2%)
    all_to_all x1, blocking collectives, on_device(): returned = lax.all_to_all(combined, 'tm', 0, 0, tiled=True)  65.3 us
    all_to_all x1, waiting for transfers between devices, on_device(): arrived = lax.all_to_all(outgoing, 'tm', 0, 0, tiled=True)  48.7 us
    pallas_call x2, Pallas kernels, sweep_call(): pl.pallas_call(functools.partial(sweep_kernel, final is not None), out_sh...  23.2 us
    ppermute x2, starting transfers between devices, halo_pair(): lax.ppermute(lax.slice_in_dim(block, 0, width, axis=dim), axis, backward)  7.29 us
    all_to_all x1, starting transfers between devices, on_device(): arrived = lax.all_to_all(outgoing, 'tm', 0, 0, tiled=True)  5.82 us
    pallas_call x1, Pallas kernels, combine_call(): pl.pallas_call(functools.partial(combine_kernel, weights), out_shape=jax....  5.13 us
    ppermute x2, starting transfers between devices, halo_pair(): lax.ppermute(lax.slice_in_dim(block, size - width, size, axis=dim), axis,...  3.83 us
  transfers between devices with their start and end apart: 5, of which 1 were waited for; matrix products, arithmetic and copies ran while one was open for 3% of the time, Pallas kernels for 6%

profile of v16, /device:TPU:4, one launch (start us, length us, event | category | flops | bytes accessed | tf_op | source)
XLA Modules:
  0.0 170.3 jit_solution(14259873278205687676)
XLA Ops:
  0.0 0.9 broadcast_in_dim.6
  0.9 0.7 slice-done
  1.6 0.4 pad_maximum_fusion.1
  2.0 1.9 %collective-permute-start.3 = (f32[2,33,2,1024]{3,2,1,0:T(2,128)S(1)}, f32[2,33,2,1024]{3,2,1,0:T(2,128)S(1)}, u32[]{:S(2)}, u32[]{:S(2)}) collective-permute-start(f32[2,33,2,1024]{3,2,1,0:T(2,128)S(1)} %get-tuple-element.8), channel_id=1, source_target_pairs={{0,1},{1,2},{2,3},{3,4},{4,5},{5,6},{6,7},{7,8},{8,9},{9,10},{10,1... | collective-permute-start | bytes 1622024 | tf_op jit(solution)/shard_map/ppermute | solution.py:45
  3.9 3.6 %collective-permute-start.2 = (f32[2,33,2,1024]{3,2,1,0:T(2,128)S(1)}, f32[2,33,2,1024]{3,2,1,0:T(2,128)S(1)}, u32[]{:S(2)}, u32[]{:S(2)}) collective-permute-start(f32[2,33,2,1024]{3,2,1,0:T(2,128)S(1)} %get-tuple-element.7), channel_id=1, source_target_pairs={{1,0},{2,1},{3,2},{4,3},{5,4},{6,5},{7,6},{8,7},{9,8},{10,9},{11,1... | collective-permute-start | bytes 1622024 | tf_op jit(solution)/shard_map/ppermute | solution.py:46
  7.6 1.4 fusion.9
  9.0 1.9 %collective-permute-start = (f32[2,32,2,1024]{3,2,1,0:T(2,128)}, f32[2,32,2,1024]{3,2,1,0:T(2,128)S(1)}, u32[]{:S(2)}, u32[]{:S(2)}) collective-permute-start(f32[2,32,2,1024]{3,2,1,0:T(2,128)} %get-tuple-element.6), channel_id=1, source_target_pairs={{0,1},{1,2},{2,3},{3,4},{4,5},{5,6},{6,7},{7,8},{8,9},{9,10},{10,1... | collective-permute-start | bytes 1572872 | tf_op jit(solution)/shard_map/ppermute | solution.py:45
  10.9 3.6 %collective-permute-start.1 = (f32[2,32,2,1024]{3,2,1,0:T(2,128)}, f32[2,32,2,1024]{3,2,1,0:T(2,128)}, u32[]{:S(2)}, u32[]{:S(2)}) collective-permute-start(f32[2,32,2,1024]{3,2,1,0:T(2,128)} %get-tuple-element.5), channel_id=1, source_target_pairs={{1,0},{2,1},{3,2},{4,3},{5,4},{6,5},{7,6},{8,7},{9,8},{10,9},{11,1... | collective-permute-start | bytes 1572872 | tf_op jit(solution)/shard_map/ppermute | solution.py:46
  14.6 0.1 fusion.8
  14.8 0.1 maximum_maximum_fusion
  14.9 0.1 fusion.10
  15.1 0.7 pad_maximum_fusion.3.rest_0_
  15.8 0.6 fusion.11
  16.5 0.8 pad_maximum_fusion.2.diff_ref
  17.4 0.7 broadcast_in_dim.8.mask_ref
  18.0 9.9 %shard_map.28.rest_1_ = f32[8,512,128]{2,1,0:T(8,128)} custom-call(f32[2,32]{1,0:T(2,128)} %get-tuple-element.13.lam_ref, f32[2,64,8,1024]{3,2,1,0:T(8,128)} %rhs_ref.3, f32[2,33,2,1024]{3,2,1,0:T(2,128)} %copy-done.1, f32[2,33,2,1024]{3,2,1,0:T(2,128)} %copy-done.2, f32[16,1024]{1,0:T(8,128)} %pad_maximum_fusion.2.diff_ref, f32[16,1024]{1,0:T(8,128)} %broadcast_in_dim.8.mask_ref), custom_call_target="tpu_custom_call" | custom-call | flops 104857600 | bytes 4194304 | tf_op jit(solution)/shard_map/pallas_call | solution.py:158
  28.0 0.8 copy-done.3
  28.8 13.2 %shard_map.29 = f32[8,1024,128]{2,1,0:T(8,128)} custom-call(f32[2,32]{1,0:T(2,128)} %get-tuple-element.14.lam_ref, f32[2,64,8,1024]{3,2,1,0:T(8,128)} %rhs_ref.3, f32[2,32,2,1024]{3,2,1,0:T(2,128)} %copy-done.3, f32[2,32,2,1024]{3,2,1,0:T(2,128)} %collective-permute-done.1.bot_ref, f32[16,1024]{1,0:T(8,128)} %pad_maximum_fusion.2.diff_ref, ...), custom_call_target="tpu_custom_call" | custom-call | flops 104857600 | bytes 4194304 | tf_op jit(solution)/shard_map/pallas_call | solution.py:158
  42.0 5.8 %all-to-all-start = ((f32[8,2,512,128]{3,2,1,0:T(8,128)}), f32[8,2,512,128]{3,2,1,0:T(8,128)}, u32[]{:S(2)}, u32[]{:S(2)}) async-start(f32[8,2,512,128]{3,2,1,0:T(8,128)} %bitcast.12), calls=%async_computation | async-start | bytes 8388608 | tf_op jit(solution)/shard_map/all_to_all | solution.py:289
  47.8 0.7 exponential_multiply_fusion.fac_ref
  48.5 48.7 %all-to-all-done.a_ref = f32[8,2,512,128]{3,2,1,0:T(8,128)} async-done(((f32[8,2,512,128]{3,2,1,0:T(8,128)}), f32[8,2,512,128]{3,2,1,0:T(8,128)}, u32[]{:S(2)}, u32[]{:S(2)}) %all-to-all-start) | async-done | bytes 4194336 | tf_op jit(solution)/shard_map/all_to_all | solution.py:289
  97.3 5.1 %shard_map.30 = f32[8,2,512,128]{3,2,1,0:T(8,128)} custom-call(f32[8,64]{1,0:T(8,128)} %exponential_multiply_fusion.fac_ref, f32[8,2,512,128]{3,2,1,0:T(8,128)} %all-to-all-done.a_ref), custom_call_target="tpu_custom_call" | custom-call | flops 41943040 | bytes 8388608 | tf_op jit(solution)/shard_map/pallas_call | solution.py:213
  102.4 65.3 %all_to_all.10 = f32[8,2,512,128]{3,2,1,0:T(8,128)S(1)} all-to-all(f32[8,2,512,128]{3,2,1,0:T(8,128)} %shard_map.30), channel_id=1, replica_groups=mesh['tm'=8,'space'=16] {'tm'}, dimensions={0} | all-to-all | bytes 8388608 | tf_op jit(solution)/shard_map/all_to_all | solution.py:297
  167.7 2.6 %copy_bitcast_fusion = f32[2,64,8,1024]{3,2,1,0:T(8,128)} fusion(f32[8,2,512,128]{3,2,1,0:T(8,128)S(1)} %all_to_all.10), kind=kLoop, calls=%fused_computation | loop fusion | bytes 8388608 | tf_op jit(solution)/shard_map/reshape | solution.py:299
  (23 shorter events, 0.2 us)
Async XLA Ops:
  0.0 1.6 slice-start
  0.0 7.6 %copy-start = (f32[2,64,8,1024]{3,2,1,0:T(8,128)S(1)}, f32[2,64,8,1024]{3,2,1,0:T(8,128)}, u32[]{:S(2)}) copy-start(f32[2,64,8,1024]{3,2,1,0:T(8,128)} %rhs_ref.3) | copy-start | bytes 12582916
  0.0 16.5 %copy-start.4 = (f32[8,1024]{1,0:T(8,128)S(1)}, f32[8,1024]{1,0:T(8,128)}, u32[]{:S(2)}) copy-start(f32[8,1024]{1,0:T(8,128)} %param.3) | copy-start | bytes 98308
  2.0 14.5 %collective-permute-start.3 = (f32[2,33,2,1024]{3,2,1,0:T(2,128)S(1)}, f32[2,33,2,1024]{3,2,1,0:T(2,128)S(1)}, u32[]{:S(2)}, u32[]{:S(2)}) collective-permute-start(f32[2,33,2,1024]{3,2,1,0:T(2,128)S(1)} %get-tuple-element.8), channel_id=1, source_target_pairs={{0,1},{1,2},{2,3},{3,4},{4,5},{5,6},{6,7},{7,8},{8,9},{9,10},{10,1... | collective-permute-start | bytes 1622024 | tf_op jit(solution)/shard_map/ppermute | solution.py:45
  3.9 12.5 %collective-permute-start.2 = (f32[2,33,2,1024]{3,2,1,0:T(2,128)S(1)}, f32[2,33,2,1024]{3,2,1,0:T(2,128)S(1)}, u32[]{:S(2)}, u32[]{:S(2)}) collective-permute-start(f32[2,33,2,1024]{3,2,1,0:T(2,128)S(1)} %get-tuple-element.7), channel_id=1, source_target_pairs={{1,0},{2,1},{3,2},{4,3},{5,4},{6,5},{7,6},{8,7},{9,8},{10,9},{11,1... | collective-permute-start | bytes 1622024 | tf_op jit(solution)/shard_map/ppermute | solution.py:46
  9.0 19.0 %collective-permute-start = (f32[2,32,2,1024]{3,2,1,0:T(2,128)}, f32[2,32,2,1024]{3,2,1,0:T(2,128)S(1)}, u32[]{:S(2)}, u32[]{:S(2)}) collective-permute-start(f32[2,32,2,1024]{3,2,1,0:T(2,128)} %get-tuple-element.6), channel_id=1, source_target_pairs={{0,1},{1,2},{2,3},{3,4},{4,5},{5,6},{6,7},{7,8},{8,9},{9,10},{10,1... | collective-permute-start | bytes 1572872 | tf_op jit(solution)/shard_map/ppermute | solution.py:45
  10.9 17.1 %collective-permute-start.1 = (f32[2,32,2,1024]{3,2,1,0:T(2,128)}, f32[2,32,2,1024]{3,2,1,0:T(2,128)}, u32[]{:S(2)}, u32[]{:S(2)}) collective-permute-start(f32[2,32,2,1024]{3,2,1,0:T(2,128)} %get-tuple-element.5), channel_id=1, source_target_pairs={{1,0},{2,1},{3,2},{4,3},{5,4},{6,5},{7,6},{8,7},{9,8},{10,9},{11,1... | collective-permute-start | bytes 1572872 | tf_op jit(solution)/shard_map/ppermute | solution.py:46
  16.5 1.6 copy-start.1
  16.5 1.6 copy-start.2
  28.0 0.8 copy-start.3
  42.0 55.2 %all-to-all-start = ((f32[8,2,512,128]{3,2,1,0:T(8,128)}), f32[8,2,512,128]{3,2,1,0:T(8,128)}, u32[]{:S(2)}, u32[]{:S(2)}) async-start(f32[8,2,512,128]{3,2,1,0:T(8,128)} %bitcast.12), calls=%async_computation | async-start | bytes 8388608 | tf_op jit(solution)/shard_map/all_to_all | solution.py:289

commit v17 on v15

--- a/solution.py
+++ b/solution.py
@@ -16,7 +16,7 @@
     1.0 / (1.0 + 0.7 * math.cos(math.pi * (2 * order + 1) / 6.0)) for order in range(3)
 ]
 Q_BLOCK = 32
-F_BLOCK = 16
+F_BLOCK = 32
 SWEEP_UNROLL = 4
 HALO = 2
 

time: 171 us -> 172 us (level)
  no operation moved by 1% of the time
where the time goes in v17:
time: 172 us; the launch traced here: 170 us
  blocking collectives  65.3 us (38%)
  waiting for transfers between devices  48.8 us (28%)
  Pallas kernels  28 us (16%)
  starting transfers between devices  16.9 us (10%)
  local copies, waits for them, and re-layouts  7.9 us (5%)
  other arithmetic  2.95 us (2%)
    all_to_all x1, blocking collectives, on_device(): returned = lax.all_to_all(combined, 'tm', 0, 0, tiled=True)  65.3 us
    all_to_all x1, waiting for transfers between devices, on_device(): arrived = lax.all_to_all(outgoing, 'tm', 0, 0, tiled=True)  48.7 us
    pallas_call x2, Pallas kernels, sweep_call(): pl.pallas_call(functools.partial(sweep_kernel, final is not None), out_sh...  23.9 us
    ppermute x2, starting transfers between devices, halo_pair(): lax.ppermute(lax.slice_in_dim(block, 0, width, axis=dim), axis, backward)  7.29 us
    all_to_all x1, starting transfers between devices, on_device(): arrived = lax.all_to_all(outgoing, 'tm', 0, 0, tiled=True)  5.82 us
    pallas_call x1, Pallas kernels, combine_call(): pl.pallas_call(functools.partial(combine_kernel, weights), out_shape=jax....  4.07 us
    ppermute x2, starting transfers between devices, halo_pair(): lax.ppermute(lax.slice_in_dim(block, size - width, size, axis=dim), axis,...  3.83 us
  transfers between devices with their start and end apart: 5, of which 1 were waited for; matrix products, arithmetic and copies ran while one was open for 3% of the time, Pallas kernels for 6%

profile of v17, /device:TPU:4, one launch (start us, length us, event | category | flops | bytes accessed | tf_op | source)
XLA Modules:
  0.0 170.0 jit_solution(4393637426742404649)
XLA Ops:
  0.0 0.9 broadcast_in_dim.6
  0.9 0.7 slice-done
  1.6 0.4 pad_maximum_fusion.1
  2.0 1.9 %collective-permute-start.3 = (f32[2,33,2,1024]{3,2,1,0:T(2,128)S(1)}, f32[2,33,2,1024]{3,2,1,0:T(2,128)S(1)}, u32[]{:S(2)}, u32[]{:S(2)}) collective-permute-start(f32[2,33,2,1024]{3,2,1,0:T(2,128)S(1)} %get-tuple-element.8), channel_id=1, source_target_pairs={{0,1},{1,2},{2,3},{3,4},{4,5},{5,6},{6,7},{7,8},{8,9},{9,10},{10,1... | collective-permute-start | bytes 1622024 | tf_op jit(solution)/shard_map/ppermute | solution.py:45
  3.9 3.6 %collective-permute-start.2 = (f32[2,33,2,1024]{3,2,1,0:T(2,128)S(1)}, f32[2,33,2,1024]{3,2,1,0:T(2,128)S(1)}, u32[]{:S(2)}, u32[]{:S(2)}) collective-permute-start(f32[2,33,2,1024]{3,2,1,0:T(2,128)S(1)} %get-tuple-element.7), channel_id=1, source_target_pairs={{1,0},{2,1},{3,2},{4,3},{5,4},{6,5},{7,6},{8,7},{9,8},{10,9},{11,1... | collective-permute-start | bytes 1622024 | tf_op jit(solution)/shard_map/ppermute | solution.py:46
  7.6 1.4 fusion.9
  9.0 1.9 %collective-permute-start = (f32[2,32,2,1024]{3,2,1,0:T(2,128)}, f32[2,32,2,1024]{3,2,1,0:T(2,128)S(1)}, u32[]{:S(2)}, u32[]{:S(2)}) collective-permute-start(f32[2,32,2,1024]{3,2,1,0:T(2,128)} %get-tuple-element.6), channel_id=1, source_target_pairs={{0,1},{1,2},{2,3},{3,4},{4,5},{5,6},{6,7},{7,8},{8,9},{9,10},{10,1... | collective-permute-start | bytes 1572872 | tf_op jit(solution)/shard_map/ppermute | solution.py:45
  10.9 3.6 %collective-permute-start.1 = (f32[2,32,2,1024]{3,2,1,0:T(2,128)}, f32[2,32,2,1024]{3,2,1,0:T(2,128)}, u32[]{:S(2)}, u32[]{:S(2)}) collective-permute-start(f32[2,32,2,1024]{3,2,1,0:T(2,128)} %get-tuple-element.5), channel_id=1, source_target_pairs={{1,0},{2,1},{3,2},{4,3},{5,4},{6,5},{7,6},{8,7},{9,8},{10,9},{11,1... | collective-permute-start | bytes 1572872 | tf_op jit(solution)/shard_map/ppermute | solution.py:46
  14.6 0.1 fusion.8
  14.8 0.1 maximum_maximum_fusion
  14.9 0.1 fusion.10
  15.1 0.7 pad_maximum_fusion.3.rest_0_
  15.8 0.6 fusion.11
  16.5 0.8 pad_maximum_fusion.2.diff_ref
  17.4 0.7 broadcast_in_dim.8.mask_ref
  18.0 10.3 %shard_map.28.rest_1_ = f32[8,512,128]{2,1,0:T(8,128)} custom-call(f32[2,32]{1,0:T(2,128)} %get-tuple-element.13.lam_ref, f32[2,64,8,1024]{3,2,1,0:T(8,128)} %rhs_ref.3, f32[2,33,2,1024]{3,2,1,0:T(2,128)} %copy-done.1, f32[2,33,2,1024]{3,2,1,0:T(2,128)} %copy-done.2, f32[16,1024]{1,0:T(8,128)} %pad_maximum_fusion.2.diff_ref, f32[16,1024]{1,0:T(8,128)} %broadcast_in_dim.8.mask_ref), custom_call_target="tpu_custom_call" | custom-call | flops 104857600 | bytes 4194304 | tf_op jit(solution)/shard_map/pallas_call | solution.py:158
  28.4 0.8 copy-done.3
  29.2 13.6 %shard_map.29 = f32[8,1024,128]{2,1,0:T(8,128)} custom-call(f32[2,32]{1,0:T(2,128)} %get-tuple-element.14.lam_ref, f32[2,64,8,1024]{3,2,1,0:T(8,128)} %rhs_ref.3, f32[2,32,2,1024]{3,2,1,0:T(2,128)} %copy-done.3, f32[2,32,2,1024]{3,2,1,0:T(2,128)} %collective-permute-done.1.bot_ref, f32[16,1024]{1,0:T(8,128)} %pad_maximum_fusion.2.diff_ref, ...), custom_call_target="tpu_custom_call" | custom-call | flops 104857600 | bytes 4194304 | tf_op jit(solution)/shard_map/pallas_call | solution.py:158
  42.8 5.8 %all-to-all-start = ((f32[8,2,512,128]{3,2,1,0:T(8,128)}), f32[8,2,512,128]{3,2,1,0:T(8,128)}, u32[]{:S(2)}, u32[]{:S(2)}) async-start(f32[8,2,512,128]{3,2,1,0:T(8,128)} %bitcast.12), calls=%async_computation | async-start | bytes 8388608 | tf_op jit(solution)/shard_map/all_to_all | solution.py:289
  48.6 0.7 exponential_multiply_fusion.fac_ref
  49.3 48.7 %all-to-all-done.a_ref = f32[8,2,512,128]{3,2,1,0:T(8,128)} async-done(((f32[8,2,512,128]{3,2,1,0:T(8,128)}), f32[8,2,512,128]{3,2,1,0:T(8,128)}, u32[]{:S(2)}, u32[]{:S(2)}) %all-to-all-start) | async-done | bytes 4194336 | tf_op jit(solution)/shard_map/all_to_all | solution.py:289
  98.0 4.1 %shard_map.30 = f32[8,2,512,128]{3,2,1,0:T(8,128)} custom-call(f32[8,64]{1,0:T(8,128)} %exponential_multiply_fusion.fac_ref, f32[8,2,512,128]{3,2,1,0:T(8,128)} %all-to-all-done.a_ref), custom_call_target="tpu_custom_call" | custom-call | flops 41943040 | bytes 8388608 | tf_op jit(solution)/shard_map/pallas_call | solution.py:213
  102.1 65.3 %all_to_all.10 = f32[8,2,512,128]{3,2,1,0:T(8,128)S(1)} all-to-all(f32[8,2,512,128]{3,2,1,0:T(8,128)} %shard_map.30), channel_id=1, replica_groups=mesh['tm'=8,'space'=16] {'tm'}, dimensions={0} | all-to-all | bytes 8388608 | tf_op jit(solution)/shard_map/all_to_all | solution.py:297
  167.4 2.6 %copy_bitcast_fusion = f32[2,64,8,1024]{3,2,1,0:T(8,128)} fusion(f32[8,2,512,128]{3,2,1,0:T(8,128)S(1)} %all_to_all.10), kind=kLoop, calls=%fused_computation | loop fusion | bytes 8388608 | tf_op jit(solution)/shard_map/reshape | solution.py:299
  (23 shorter events, 0.2 us)
Async XLA Ops:
  0.0 1.6 slice-start
  0.0 7.6 %copy-start = (f32[2,64,8,1024]{3,2,1,0:T(8,128)S(1)}, f32[2,64,8,1024]{3,2,1,0:T(8,128)}, u32[]{:S(2)}) copy-start(f32[2,64,8,1024]{3,2,1,0:T(8,128)} %rhs_ref.3) | copy-start | bytes 12582916
  0.0 16.5 %copy-start.4 = (f32[8,1024]{1,0:T(8,128)S(1)}, f32[8,1024]{1,0:T(8,128)}, u32[]{:S(2)}) copy-start(f32[8,1024]{1,0:T(8,128)} %param.3) | copy-start | bytes 98308
  2.0 14.5 %collective-permute-start.3 = (f32[2,33,2,1024]{3,2,1,0:T(2,128)S(1)}, f32[2,33,2,1024]{3,2,1,0:T(2,128)S(1)}, u32[]{:S(2)}, u32[]{:S(2)}) collective-permute-start(f32[2,33,2,1024]{3,2,1,0:T(2,128)S(1)} %get-tuple-element.8), channel_id=1, source_target_pairs={{0,1},{1,2},{2,3},{3,4},{4,5},{5,6},{6,7},{7,8},{8,9},{9,10},{10,1... | collective-permute-start | bytes 1622024 | tf_op jit(solution)/shard_map/ppermute | solution.py:45
  3.9 12.5 %collective-permute-start.2 = (f32[2,33,2,1024]{3,2,1,0:T(2,128)S(1)}, f32[2,33,2,1024]{3,2,1,0:T(2,128)S(1)}, u32[]{:S(2)}, u32[]{:S(2)}) collective-permute-start(f32[2,33,2,1024]{3,2,1,0:T(2,128)S(1)} %get-tuple-element.7), channel_id=1, source_target_pairs={{1,0},{2,1},{3,2},{4,3},{5,4},{6,5},{7,6},{8,7},{9,8},{10,9},{11,1... | collective-permute-start | bytes 1622024 | tf_op jit(solution)/shard_map/ppermute | solution.py:46
  9.0 19.4 %collective-permute-start = (f32[2,32,2,1024]{3,2,1,0:T(2,128)}, f32[2,32,2,1024]{3,2,1,0:T(2,128)S(1)}, u32[]{:S(2)}, u32[]{:S(2)}) collective-permute-start(f32[2,32,2,1024]{3,2,1,0:T(2,128)} %get-tuple-element.6), channel_id=1, source_target_pairs={{0,1},{1,2},{2,3},{3,4},{4,5},{5,6},{6,7},{7,8},{8,9},{9,10},{10,1... | collective-permute-start | bytes 1572872 | tf_op jit(solution)/shard_map/ppermute | solution.py:45
  10.9 17.5 %collective-permute-start.1 = (f32[2,32,2,1024]{3,2,1,0:T(2,128)}, f32[2,32,2,1024]{3,2,1,0:T(2,128)}, u32[]{:S(2)}, u32[]{:S(2)}) collective-permute-start(f32[2,32,2,1024]{3,2,1,0:T(2,128)} %get-tuple-element.5), channel_id=1, source_target_pairs={{1,0},{2,1},{3,2},{4,3},{5,4},{6,5},{7,6},{8,7},{9,8},{10,9},{11,1... | collective-permute-start | bytes 1572872 | tf_op jit(solution)/shard_map/ppermute | solution.py:46
  16.5 1.6 copy-start.1
  16.5 1.6 copy-start.2
  28.4 0.8 copy-start.3
  42.8 55.2 %all-to-all-start = ((f32[8,2,512,128]{3,2,1,0:T(8,128)}), f32[8,2,512,128]{3,2,1,0:T(8,128)}, u32[]{:S(2)}, u32[]{:S(2)}) async-start(f32[8,2,512,128]{3,2,1,0:T(8,128)} %bitcast.12), calls=%async_computation | async-start | bytes 8388608 | tf_op jit(solution)/shard_map/all_to_all | solution.py:289

commit v18 on v15

--- a/solution.py
+++ b/solution.py
@@ -17,7 +17,7 @@
 ]
 Q_BLOCK = 32
 F_BLOCK = 16
-SWEEP_UNROLL = 4
+SWEEP_UNROLL = 8
 HALO = 2
 
 

time: 171 us -> 170 us (level)
  no operation moved by 1% of the time
where the time goes in v18:
time: 170 us; the launch traced here: 169 us
  blocking collectives  65.3 us (38%)
  waiting for transfers between devices  48.8 us (29%)
  Pallas kernels  26.6 us (16%)
  starting transfers between devices  16.9 us (10%)
  local copies, waits for them, and re-layouts  7.89 us (5%)
  other arithmetic  2.95 us (2%)
    all_to_all x1, blocking collectives, on_device(): returned = lax.all_to_all(combined, 'tm', 0, 0, tiled=True)  65.3 us
    all_to_all x1, waiting for transfers between devices, on_device(): arrived = lax.all_to_all(outgoing, 'tm', 0, 0, tiled=True)  48.7 us
    pallas_call x2, Pallas kernels, sweep_call(): pl.pallas_call(functools.partial(sweep_kernel, final is not None), out_sh...  22.6 us
    ppermute x2, starting transfers between devices, halo_pair(): lax.ppermute(lax.slice_in_dim(block, 0, width, axis=dim), axis, backward)  7.29 us
    all_to_all x1, starting transfers between devices, on_device(): arrived = lax.all_to_all(outgoing, 'tm', 0, 0, tiled=True)  5.82 us
    pallas_call x1, Pallas kernels, combine_call(): pl.pallas_call(functools.partial(combine_kernel, weights), out_shape=jax....  4.04 us
    ppermute x2, starting transfers between devices, halo_pair(): lax.ppermute(lax.slice_in_dim(block, size - width, size, axis=dim), axis,...  3.83 us
  transfers between devices with their start and end apart: 5, of which 1 were waited for; matrix products, arithmetic and copies ran while one was open for 3% of the time, Pallas kernels for 6%

profile of v18, /device:TPU:4, one launch (start us, length us, event | category | flops | bytes accessed | tf_op | source)
XLA Modules:
  0.0 168.6 jit_solution(3624264534912406993)
XLA Ops:
  0.0 0.9 broadcast_in_dim.6
  0.9 0.7 slice-done
  1.6 0.4 pad_maximum_fusion.1
  2.0 1.9 %collective-permute-start.3 = (f32[2,33,2,1024]{3,2,1,0:T(2,128)S(1)}, f32[2,33,2,1024]{3,2,1,0:T(2,128)S(1)}, u32[]{:S(2)}, u32[]{:S(2)}) collective-permute-start(f32[2,33,2,1024]{3,2,1,0:T(2,128)S(1)} %get-tuple-element.8), channel_id=1, source_target_pairs={{0,1},{1,2},{2,3},{3,4},{4,5},{5,6},{6,7},{7,8},{8,9},{9,10},{10,1... | collective-permute-start | bytes 1622024 | tf_op jit(solution)/shard_map/ppermute | solution.py:45
  3.9 3.6 %collective-permute-start.2 = (f32[2,33,2,1024]{3,2,1,0:T(2,128)S(1)}, f32[2,33,2,1024]{3,2,1,0:T(2,128)S(1)}, u32[]{:S(2)}, u32[]{:S(2)}) collective-permute-start(f32[2,33,2,1024]{3,2,1,0:T(2,128)S(1)} %get-tuple-element.7), channel_id=1, source_target_pairs={{1,0},{2,1},{3,2},{4,3},{5,4},{6,5},{7,6},{8,7},{9,8},{10,9},{11,1... | collective-permute-start | bytes 1622024 | tf_op jit(solution)/shard_map/ppermute | solution.py:46
  7.6 1.4 fusion.9
  9.0 1.9 %collective-permute-start = (f32[2,32,2,1024]{3,2,1,0:T(2,128)}, f32[2,32,2,1024]{3,2,1,0:T(2,128)S(1)}, u32[]{:S(2)}, u32[]{:S(2)}) collective-permute-start(f32[2,32,2,1024]{3,2,1,0:T(2,128)} %get-tuple-element.6), channel_id=1, source_target_pairs={{0,1},{1,2},{2,3},{3,4},{4,5},{5,6},{6,7},{7,8},{8,9},{9,10},{10,1... | collective-permute-start | bytes 1572872 | tf_op jit(solution)/shard_map/ppermute | solution.py:45
  10.9 3.6 %collective-permute-start.1 = (f32[2,32,2,1024]{3,2,1,0:T(2,128)}, f32[2,32,2,1024]{3,2,1,0:T(2,128)}, u32[]{:S(2)}, u32[]{:S(2)}) collective-permute-start(f32[2,32,2,1024]{3,2,1,0:T(2,128)} %get-tuple-element.5), channel_id=1, source_target_pairs={{1,0},{2,1},{3,2},{4,3},{5,4},{6,5},{7,6},{8,7},{9,8},{10,9},{11,1... | collective-permute-start | bytes 1572872 | tf_op jit(solution)/shard_map/ppermute | solution.py:46
  14.6 0.1 fusion.8
  14.8 0.1 maximum_maximum_fusion
  14.9 0.1 fusion.10
  15.1 0.7 pad_maximum_fusion.3.rest_0_
  15.8 0.6 fusion.11
  16.5 0.8 pad_maximum_fusion.2.diff_ref
  17.4 0.7 broadcast_in_dim.8.mask_ref
  18.0 9.6 %shard_map.28.rest_1_ = f32[8,512,128]{2,1,0:T(8,128)} custom-call(f32[2,32]{1,0:T(2,128)} %get-tuple-element.13.lam_ref, f32[2,64,8,1024]{3,2,1,0:T(8,128)} %rhs_ref.3, f32[2,33,2,1024]{3,2,1,0:T(2,128)} %copy-done.1, f32[2,33,2,1024]{3,2,1,0:T(2,128)} %copy-done.2, f32[16,1024]{1,0:T(8,128)} %pad_maximum_fusion.2.diff_ref, f32[16,1024]{1,0:T(8,128)} %broadcast_in_dim.8.mask_ref), custom_call_target="tpu_custom_call" | custom-call | flops 104857600 | bytes 4194304 | tf_op jit(solution)/shard_map/pallas_call | solution.py:158
  27.7 0.8 copy-done.3
  28.5 12.9 %shard_map.29 = f32[8,1024,128]{2,1,0:T(8,128)} custom-call(f32[2,32]{1,0:T(2,128)} %get-tuple-element.14.lam_ref, f32[2,64,8,1024]{3,2,1,0:T(8,128)} %rhs_ref.3, f32[2,32,2,1024]{3,2,1,0:T(2,128)} %copy-done.3, f32[2,32,2,1024]{3,2,1,0:T(2,128)} %collective-permute-done.1.bot_ref, f32[16,1024]{1,0:T(8,128)} %pad_maximum_fusion.2.diff_ref, ...), custom_call_target="tpu_custom_call" | custom-call | flops 104857600 | bytes 4194304 | tf_op jit(solution)/shard_map/pallas_call | solution.py:158
  41.5 5.8 %all-to-all-start = ((f32[8,2,512,128]{3,2,1,0:T(8,128)}), f32[8,2,512,128]{3,2,1,0:T(8,128)}, u32[]{:S(2)}, u32[]{:S(2)}) async-start(f32[8,2,512,128]{3,2,1,0:T(8,128)} %bitcast.12), calls=%async_computation | async-start | bytes 8388608 | tf_op jit(solution)/shard_map/all_to_all | solution.py:289
  47.3 0.7 exponential_multiply_fusion.fac_ref
  48.0 48.7 %all-to-all-done.a_ref = f32[8,2,512,128]{3,2,1,0:T(8,128)} async-done(((f32[8,2,512,128]{3,2,1,0:T(8,128)}), f32[8,2,512,128]{3,2,1,0:T(8,128)}, u32[]{:S(2)}, u32[]{:S(2)}) %all-to-all-start) | async-done | bytes 4194336 | tf_op jit(solution)/shard_map/all_to_all | solution.py:289
  96.7 4.0 %shard_map.30 = f32[8,2,512,128]{3,2,1,0:T(8,128)} custom-call(f32[8,64]{1,0:T(8,128)} %exponential_multiply_fusion.fac_ref, f32[8,2,512,128]{3,2,1,0:T(8,128)} %all-to-all-done.a_ref), custom_call_target="tpu_custom_call" | custom-call | flops 41943040 | bytes 8388608 | tf_op jit(solution)/shard_map/pallas_call | solution.py:213
  100.7 65.3 %all_to_all.10 = f32[8,2,512,128]{3,2,1,0:T(8,128)S(1)} all-to-all(f32[8,2,512,128]{3,2,1,0:T(8,128)} %shard_map.30), channel_id=1, replica_groups=mesh['tm'=8,'space'=16] {'tm'}, dimensions={0} | all-to-all | bytes 8388608 | tf_op jit(solution)/shard_map/all_to_all | solution.py:297
  166.0 2.6 %copy_bitcast_fusion = f32[2,64,8,1024]{3,2,1,0:T(8,128)} fusion(f32[8,2,512,128]{3,2,1,0:T(8,128)S(1)} %all_to_all.10), kind=kLoop, calls=%fused_computation | loop fusion | bytes 8388608 | tf_op jit(solution)/shard_map/reshape | solution.py:299
  (23 shorter events, 0.2 us)
Async XLA Ops:
  0.0 1.6 slice-start
  0.0 7.6 %copy-start = (f32[2,64,8,1024]{3,2,1,0:T(8,128)S(1)}, f32[2,64,8,1024]{3,2,1,0:T(8,128)}, u32[]{:S(2)}) copy-start(f32[2,64,8,1024]{3,2,1,0:T(8,128)} %rhs_ref.3) | copy-start | bytes 12582916
  0.0 16.5 %copy-start.4 = (f32[8,1024]{1,0:T(8,128)S(1)}, f32[8,1024]{1,0:T(8,128)}, u32[]{:S(2)}) copy-start(f32[8,1024]{1,0:T(8,128)} %param.3) | copy-start | bytes 98308
  2.0 14.5 %collective-permute-start.3 = (f32[2,33,2,1024]{3,2,1,0:T(2,128)S(1)}, f32[2,33,2,1024]{3,2,1,0:T(2,128)S(1)}, u32[]{:S(2)}, u32[]{:S(2)}) collective-permute-start(f32[2,33,2,1024]{3,2,1,0:T(2,128)S(1)} %get-tuple-element.8), channel_id=1, source_target_pairs={{0,1},{1,2},{2,3},{3,4},{4,5},{5,6},{6,7},{7,8},{8,9},{9,10},{10,1... | collective-permute-start | bytes 1622024 | tf_op jit(solution)/shard_map/ppermute | solution.py:45
  3.9 12.5 %collective-permute-start.2 = (f32[2,33,2,1024]{3,2,1,0:T(2,128)S(1)}, f32[2,33,2,1024]{3,2,1,0:T(2,128)S(1)}, u32[]{:S(2)}, u32[]{:S(2)}) collective-permute-start(f32[2,33,2,1024]{3,2,1,0:T(2,128)S(1)} %get-tuple-element.7), channel_id=1, source_target_pairs={{1,0},{2,1},{3,2},{4,3},{5,4},{6,5},{7,6},{8,7},{9,8},{10,9},{11,1... | collective-permute-start | bytes 1622024 | tf_op jit(solution)/shard_map/ppermute | solution.py:46
  9.0 18.7 %collective-permute-start = (f32[2,32,2,1024]{3,2,1,0:T(2,128)}, f32[2,32,2,1024]{3,2,1,0:T(2,128)S(1)}, u32[]{:S(2)}, u32[]{:S(2)}) collective-permute-start(f32[2,32,2,1024]{3,2,1,0:T(2,128)} %get-tuple-element.6), channel_id=1, source_target_pairs={{0,1},{1,2},{2,3},{3,4},{4,5},{5,6},{6,7},{7,8},{8,9},{9,10},{10,1... | collective-permute-start | bytes 1572872 | tf_op jit(solution)/shard_map/ppermute | solution.py:45
  10.9 16.8 %collective-permute-start.1 = (f32[2,32,2,1024]{3,2,1,0:T(2,128)}, f32[2,32,2,1024]{3,2,1,0:T(2,128)}, u32[]{:S(2)}, u32[]{:S(2)}) collective-permute-start(f32[2,32,2,1024]{3,2,1,0:T(2,128)} %get-tuple-element.5), channel_id=1, source_target_pairs={{1,0},{2,1},{3,2},{4,3},{5,4},{6,5},{7,6},{8,7},{9,8},{10,9},{11,1... | collective-permute-start | bytes 1572872 | tf_op jit(solution)/shard_map/ppermute | solution.py:46
  16.5 1.6 copy-start.1
  16.5 1.6 copy-start.2
  27.7 0.8 copy-start.3
  41.5 55.2 %all-to-all-start = ((f32[8,2,512,128]{3,2,1,0:T(8,128)}), f32[8,2,512,128]{3,2,1,0:T(8,128)}, u32[]{:S(2)}, u32[]{:S(2)}) async-start(f32[8,2,512,128]{3,2,1,0:T(8,128)} %bitcast.12), calls=%async_computation | async-start | bytes 8388608 | tf_op jit(solution)/shard_map/all_to_all | solution.py:289

commit v19 on v18

--- a/solution.py
+++ b/solution.py
@@ -17,7 +17,7 @@
 ]
 Q_BLOCK = 32
 F_BLOCK = 16
-SWEEP_UNROLL = 8
+SWEEP_UNROLL = 16
 HALO = 2
 
 

time: 170 us -> 170 us (level)
  no operation moved by 1% of the time
where the time goes in v19:
time: 170 us; the launch traced here: 168 us
  blocking collectives  65.3 us (38%)
  waiting for transfers between devices  48.7 us (29%)
  Pallas kernels  26.4 us (16%)
  starting transfers between devices  16.9 us (10%)
  local copies, waits for them, and re-layouts  7.89 us (5%)
  other arithmetic  2.95 us (2%)
    all_to_all x1, blocking collectives, on_device(): returned = lax.all_to_all(combined, 'tm', 0, 0, tiled=True)  65.3 us
    all_to_all x1, waiting for transfers between devices, on_device(): arrived = lax.all_to_all(outgoing, 'tm', 0, 0, tiled=True)  48.7 us
    pallas_call x2, Pallas kernels, sweep_call(): pl.pallas_call(functools.partial(sweep_kernel, final is not None), out_sh...  22.4 us
    ppermute x2, starting transfers between devices, halo_pair(): lax.ppermute(lax.slice_in_dim(block, 0, width, axis=dim), axis, backward)  7.29 us
    all_to_all x1, starting transfers between devices, on_device(): arrived = lax.all_to_all(outgoing, 'tm', 0, 0, tiled=True)  5.83 us
    pallas_call x1, Pallas kernels, combine_call(): pl.pallas_call(functools.partial(combine_kernel, weights), out_shape=jax....  4.03 us
    ppermute x2, starting transfers between devices, halo_pair(): lax.ppermute(lax.slice_in_dim(block, size - width, size, axis=dim), axis,...  3.83 us
  transfers between devices with their start and end apart: 5, of which 1 were waited for; matrix products, arithmetic and copies ran while one was open for 3% of the time, Pallas kernels for 6%

profile of v19, /device:TPU:4, one launch (start us, length us, event | category | flops | bytes accessed | tf_op | source)
XLA Modules:
  0.0 168.4 jit_solution(16856800026722396372)
XLA Ops:
  0.0 0.9 broadcast_in_dim.6
  0.9 0.7 slice-done
  1.6 0.4 pad_maximum_fusion.1
  2.0 1.9 %collective-permute-start.3 = (f32[2,33,2,1024]{3,2,1,0:T(2,128)S(1)}, f32[2,33,2,1024]{3,2,1,0:T(2,128)S(1)}, u32[]{:S(2)}, u32[]{:S(2)}) collective-permute-start(f32[2,33,2,1024]{3,2,1,0:T(2,128)S(1)} %get-tuple-element.8), channel_id=1, source_target_pairs={{0,1},{1,2},{2,3},{3,4},{4,5},{5,6},{6,7},{7,8},{8,9},{9,10},{10,1... | collective-permute-start | bytes 1622024 | tf_op jit(solution)/shard_map/ppermute | solution.py:45
  3.9 3.6 %collective-permute-start.2 = (f32[2,33,2,1024]{3,2,1,0:T(2,128)S(1)}, f32[2,33,2,1024]{3,2,1,0:T(2,128)S(1)}, u32[]{:S(2)}, u32[]{:S(2)}) collective-permute-start(f32[2,33,2,1024]{3,2,1,0:T(2,128)S(1)} %get-tuple-element.7), channel_id=1, source_target_pairs={{1,0},{2,1},{3,2},{4,3},{5,4},{6,5},{7,6},{8,7},{9,8},{10,9},{11,1... | collective-permute-start | bytes 1622024 | tf_op jit(solution)/shard_map/ppermute | solution.py:46
  7.6 1.4 fusion.9
  9.0 1.9 %collective-permute-start = (f32[2,32,2,1024]{3,2,1,0:T(2,128)}, f32[2,32,2,1024]{3,2,1,0:T(2,128)S(1)}, u32[]{:S(2)}, u32[]{:S(2)}) collective-permute-start(f32[2,32,2,1024]{3,2,1,0:T(2,128)} %get-tuple-element.6), channel_id=1, source_target_pairs={{0,1},{1,2},{2,3},{3,4},{4,5},{5,6},{6,7},{7,8},{8,9},{9,10},{10,1... | collective-permute-start | bytes 1572872 | tf_op jit(solution)/shard_map/ppermute | solution.py:45
  10.9 3.6 %collective-permute-start.1 = (f32[2,32,2,1024]{3,2,1,0:T(2,128)}, f32[2,32,2,1024]{3,2,1,0:T(2,128)}, u32[]{:S(2)}, u32[]{:S(2)}) collective-permute-start(f32[2,32,2,1024]{3,2,1,0:T(2,128)} %get-tuple-element.5), channel_id=1, source_target_pairs={{1,0},{2,1},{3,2},{4,3},{5,4},{6,5},{7,6},{8,7},{9,8},{10,9},{11,1... | collective-permute-start | bytes 1572872 | tf_op jit(solution)/shard_map/ppermute | solution.py:46
  14.6 0.1 fusion.8
  14.8 0.1 maximum_maximum_fusion
  14.9 0.1 fusion.10
  15.1 0.7 pad_maximum_fusion.3.rest_0_
  15.8 0.6 fusion.11
  16.5 0.8 pad_maximum_fusion.2.diff_ref
  17.4 0.7 broadcast_in_dim.8.mask_ref
  18.0 9.5 %shard_map.28.rest_1_ = f32[8,512,128]{2,1,0:T(8,128)} custom-call(f32[2,32]{1,0:T(2,128)} %get-tuple-element.13.lam_ref, f32[2,64,8,1024]{3,2,1,0:T(8,128)} %rhs_ref.3, f32[2,33,2,1024]{3,2,1,0:T(2,128)} %copy-done.1, f32[2,33,2,1024]{3,2,1,0:T(2,128)} %copy-done.2, f32[16,1024]{1,0:T(8,128)} %pad_maximum_fusion.2.diff_ref, f32[16,1024]{1,0:T(8,128)} %broadcast_in_dim.8.mask_ref), custom_call_target="tpu_custom_call" | custom-call | flops 104857600 | bytes 4194304 | tf_op jit(solution)/shard_map/pallas_call | solution.py:158
  27.6 0.8 copy-done.3
  28.4 12.8 %shard_map.29 = f32[8,1024,128]{2,1,0:T(8,128)} custom-call(f32[2,32]{1,0:T(2,128)} %get-tuple-element.14.lam_ref, f32[2,64,8,1024]{3,2,1,0:T(8,128)} %rhs_ref.3, f32[2,32,2,1024]{3,2,1,0:T(2,128)} %copy-done.3, f32[2,32,2,1024]{3,2,1,0:T(2,128)} %collective-permute-done.1.bot_ref, f32[16,1024]{1,0:T(8,128)} %pad_maximum_fusion.2.diff_ref, ...), custom_call_target="tpu_custom_call" | custom-call | flops 104857600 | bytes 4194304 | tf_op jit(solution)/shard_map/pallas_call | solution.py:158
  41.2 5.8 %all-to-all-start = ((f32[8,2,512,128]{3,2,1,0:T(8,128)}), f32[8,2,512,128]{3,2,1,0:T(8,128)}, u32[]{:S(2)}, u32[]{:S(2)}) async-start(f32[8,2,512,128]{3,2,1,0:T(8,128)} %bitcast.12), calls=%async_computation | async-start | bytes 8388608 | tf_op jit(solution)/shard_map/all_to_all | solution.py:289
  47.1 0.7 exponential_multiply_fusion.fac_ref
  47.7 48.7 %all-to-all-done.a_ref = f32[8,2,512,128]{3,2,1,0:T(8,128)} async-done(((f32[8,2,512,128]{3,2,1,0:T(8,128)}), f32[8,2,512,128]{3,2,1,0:T(8,128)}, u32[]{:S(2)}, u32[]{:S(2)}) %all-to-all-start) | async-done | bytes 4194336 | tf_op jit(solution)/shard_map/all_to_all | solution.py:289
  96.5 4.0 %shard_map.30 = f32[8,2,512,128]{3,2,1,0:T(8,128)} custom-call(f32[8,64]{1,0:T(8,128)} %exponential_multiply_fusion.fac_ref, f32[8,2,512,128]{3,2,1,0:T(8,128)} %all-to-all-done.a_ref), custom_call_target="tpu_custom_call" | custom-call | flops 41943040 | bytes 8388608 | tf_op jit(solution)/shard_map/pallas_call | solution.py:213
  100.5 65.3 %all_to_all.10 = f32[8,2,512,128]{3,2,1,0:T(8,128)S(1)} all-to-all(f32[8,2,512,128]{3,2,1,0:T(8,128)} %shard_map.30), channel_id=1, replica_groups=mesh['tm'=8,'space'=16] {'tm'}, dimensions={0} | all-to-all | bytes 8388608 | tf_op jit(solution)/shard_map/all_to_all | solution.py:297
  165.8 2.6 %copy_bitcast_fusion = f32[2,64,8,1024]{3,2,1,0:T(8,128)} fusion(f32[8,2,512,128]{3,2,1,0:T(8,128)S(1)} %all_to_all.10), kind=kLoop, calls=%fused_computation | loop fusion | bytes 8388608 | tf_op jit(solution)/shard_map/reshape | solution.py:299
  (23 shorter events, 0.2 us)
Async XLA Ops:
  0.0 1.6 slice-start
  0.0 7.6 %copy-start = (f32[2,64,8,1024]{3,2,1,0:T(8,128)S(1)}, f32[2,64,8,1024]{3,2,1,0:T(8,128)}, u32[]{:S(2)}) copy-start(f32[2,64,8,1024]{3,2,1,0:T(8,128)} %rhs_ref.3) | copy-start | bytes 12582916
  0.0 16.5 %copy-start.4 = (f32[8,1024]{1,0:T(8,128)S(1)}, f32[8,1024]{1,0:T(8,128)}, u32[]{:S(2)}) copy-start(f32[8,1024]{1,0:T(8,128)} %param.3) | copy-start | bytes 98308
  2.0 14.5 %collective-permute-start.3 = (f32[2,33,2,1024]{3,2,1,0:T(2,128)S(1)}, f32[2,33,2,1024]{3,2,1,0:T(2,128)S(1)}, u32[]{:S(2)}, u32[]{:S(2)}) collective-permute-start(f32[2,33,2,1024]{3,2,1,0:T(2,128)S(1)} %get-tuple-element.8), channel_id=1, source_target_pairs={{0,1},{1,2},{2,3},{3,4},{4,5},{5,6},{6,7},{7,8},{8,9},{9,10},{10,1... | collective-permute-start | bytes 1622024 | tf_op jit(solution)/shard_map/ppermute | solution.py:45
  3.9 12.5 %collective-permute-start.2 = (f32[2,33,2,1024]{3,2,1,0:T(2,128)S(1)}, f32[2,33,2,1024]{3,2,1,0:T(2,128)S(1)}, u32[]{:S(2)}, u32[]{:S(2)}) collective-permute-start(f32[2,33,2,1024]{3,2,1,0:T(2,128)S(1)} %get-tuple-element.7), channel_id=1, source_target_pairs={{1,0},{2,1},{3,2},{4,3},{5,4},{6,5},{7,6},{8,7},{9,8},{10,9},{11,1... | collective-permute-start | bytes 1622024 | tf_op jit(solution)/shard_map/ppermute | solution.py:46
  9.0 18.6 %collective-permute-start = (f32[2,32,2,1024]{3,2,1,0:T(2,128)}, f32[2,32,2,1024]{3,2,1,0:T(2,128)S(1)}, u32[]{:S(2)}, u32[]{:S(2)}) collective-permute-start(f32[2,32,2,1024]{3,2,1,0:T(2,128)} %get-tuple-element.6), channel_id=1, source_target_pairs={{0,1},{1,2},{2,3},{3,4},{4,5},{5,6},{6,7},{7,8},{8,9},{9,10},{10,1... | collective-permute-start | bytes 1572872 | tf_op jit(solution)/shard_map/ppermute | solution.py:45
  10.9 16.7 %collective-permute-start.1 = (f32[2,32,2,1024]{3,2,1,0:T(2,128)}, f32[2,32,2,1024]{3,2,1,0:T(2,128)}, u32[]{:S(2)}, u32[]{:S(2)}) collective-permute-start(f32[2,32,2,1024]{3,2,1,0:T(2,128)} %get-tuple-element.5), channel_id=1, source_target_pairs={{1,0},{2,1},{3,2},{4,3},{5,4},{6,5},{7,6},{8,7},{9,8},{10,9},{11,1... | collective-permute-start | bytes 1572872 | tf_op jit(solution)/shard_map/ppermute | solution.py:46
  16.5 1.6 copy-start.1
  16.5 1.6 copy-start.2
  27.6 0.8 copy-start.3
  41.2 55.2 %all-to-all-start = ((f32[8,2,512,128]{3,2,1,0:T(8,128)}), f32[8,2,512,128]{3,2,1,0:T(8,128)}, u32[]{:S(2)}, u32[]{:S(2)}) async-start(f32[8,2,512,128]{3,2,1,0:T(8,128)} %bitcast.12), calls=%async_computation | async-start | bytes 8388608 | tf_op jit(solution)/shard_map/all_to_all | solution.py:289
